TPU v7x, 256 devices: a whole 4x4x8 slice. The times are simulated.
256 devices in a mesh: gx: 16 (over z, core), gy: 16 (over y, x).
Axes of the slice: x: 4, y: 4, z: 8, core: 2. Of those that a mesh axis runs over, the one named last changes fastest.
Arguments:
- field: float32 [64, 4096, 128], P('gy', 'gx'), may hold values from -5 to 5
- courant: float32 [3, 64, 4096, 128], P(None, 'gy', 'gx'), may hold values from -2.5 to 2.5
- diffusion_number: float32 [64, 4096, 128], P('gy', 'gx'), may hold values from 65536 to 1310720
Outputs:
- solved: float32 [64, 4096, 128], P('gy', 'gx')
All inputs are finite; a program needn't handle non-finite values.
Results may differ from a plain program's by a relative error of at most 0.0013.
Values sent between devices are 32-bit elements; how exact they have to be, the bound alone decides.
No kernel may reach another device: no remote copies, remote signals or barrier semaphores. Data moves between devices by JAX's collectives and lax.ppermute only.
A program may use at most 64 MiB of HBM per device.

v0:
```python
import jax
import jax.numpy as jnp
from jax import lax
from jax.sharding import PartitionSpec as P


def padded_2(cells, sides, width, closed):
    for axis, dim in sides:
        count = lax.axis_size(axis)
        ends = count if closed else count - 1
        head = lax.slice_in_dim(cells, 0, width, axis=dim)
        tail = lax.slice_in_dim(cells, cells.shape[dim] - width, cells.shape[dim], axis=dim)
        cells = jnp.concatenate(
            [
                lax.ppermute(tail, axis, [(i, (i + 1) % count) for i in range(ends)]),
                cells,
                lax.ppermute(head, axis, [((i + 1) % count, i) for i in range(ends)]),
            ],
            axis=dim,
        )
    return cells


def difference_pair(padded, sweep_direction, length):
    shifted = [
        lax.slice_in_dim(padded, offset, offset + length, axis=sweep_direction)
        for offset in range(5)
    ]
    gradient = (8.0 * (shifted[3] - shifted[1]) - (shifted[4] - shifted[0])) / 12.0
    curvature = (
        16.0 * (shifted[3] + shifted[1]) - (shifted[4] + shifted[0]) - 30.0 * shifted[2]
    ) / 12.0
    return (gradient, curvature)


def build_rhs(field, courant, y_padded, x_padded):
    z_padded = jnp.concatenate([field[:, :, -2:], field, field[:, :, :2]], 2)
    grad_y, curve_y = difference_pair(y_padded, 0, field.shape[0])
    grad_x = difference_pair(x_padded, 1, field.shape[1])[0]
    grad_z, curve_z = difference_pair(z_padded, 2, field.shape[2])
    transport = courant[0] * grad_x + courant[1] * grad_y + courant[2] * grad_z
    return field - transport + 0.05 * (curve_y + curve_z) + 0.3 * field / (1.0 + field * field)


def rows_below(values, stride, fill, sweep_direction):
    length = values.shape[sweep_direction]
    filler = jnp.full_like(lax.slice_in_dim(values, 0, stride, axis=sweep_direction), fill)
    return jnp.concatenate(
        [filler, lax.slice_in_dim(values, 0, length - stride, axis=sweep_direction)],
        sweep_direction,
    )


def rows_above(values, stride, fill, sweep_direction):
    length = values.shape[sweep_direction]
    filler = jnp.full_like(
        lax.slice_in_dim(values, length - stride, length, axis=sweep_direction), fill
    )
    return jnp.concatenate(
        [lax.slice_in_dim(values, stride, length, axis=sweep_direction), filler], sweep_direction
    )


def combine_rows(own_rows, below_set, above_set):
    lower_band, main_diagonal, upper_band, right_hand_sides = own_rows
    low_sub, low_diag, low_super, low_rights = below_set
    high_sub, high_diag, high_super, high_rights = above_set
    factor_low = -lower_band / low_diag
    factor_high = -upper_band / high_diag
    new_sub = factor_low * low_sub
    new_super = factor_high * high_super
    new_diag = main_diagonal + factor_low * low_super + factor_high * high_sub
    new_rights = tuple(
        (
            value + factor_low * lower_value + factor_high * upper_value
            for value, lower_value, upper_value in zip(right_hand_sides, low_rights, high_rights)
        )
    )
    return (new_sub, new_diag, new_super, new_rights)


def parallel_cyclic_reduction(
    lower_band, main_diagonal, upper_band, right_hand_sides, sweep_direction
):
    length = main_diagonal.shape[sweep_direction]
    stride = 1
    while stride < length:
        below_set = (
            rows_below(lower_band, stride, 0.0, sweep_direction),
            rows_below(main_diagonal, stride, 1.0, sweep_direction),
            rows_below(upper_band, stride, 0.0, sweep_direction),
            tuple((rows_below(value, stride, 0.0, sweep_direction) for value in right_hand_sides)),
        )
        above_set = (
            rows_above(lower_band, stride, 0.0, sweep_direction),
            rows_above(main_diagonal, stride, 1.0, sweep_direction),
            rows_above(upper_band, stride, 0.0, sweep_direction),
            tuple((rows_above(value, stride, 0.0, sweep_direction) for value in right_hand_sides)),
        )
        lower_band, main_diagonal, upper_band, right_hand_sides = combine_rows(
            (lower_band, main_diagonal, upper_band, right_hand_sides), below_set, above_set
        )
        stride = stride * 2
    return tuple((value / main_diagonal for value in right_hand_sides))


def shards(field, courant, diffusion_number):
    y_padded = padded_2(field, (("gy", 0),), 2, True)
    x_padded = padded_2(field, (("gx", 1),), 2, False)
    rhs = build_rhs(field, courant, y_padded, x_padded)
    place = lax.axis_index("gx")
    device_count = lax.axis_size("gx")
    sub_full = -diffusion_number
    diag_full = 1.0 + 2.0 * diffusion_number
    super_full = -diffusion_number
    edge_zeros = jnp.zeros_like(rhs[:, 0:1])
    inner_zeros = jnp.zeros_like(rhs[:, 3:])
    sub_inner = jnp.concatenate([edge_zeros, sub_full[:, 2:-1]], 1)
    super_inner = jnp.concatenate([super_full[:, 1:-2], edge_zeros], 1)
    diag_inner = diag_full[:, 1:-1]
    first_unit = jnp.concatenate([-sub_full[:, 1:2], inner_zeros], 1)
    last_unit = jnp.concatenate([inner_zeros, -super_full[:, -2:-1]], 1)
    particular_solution, first_row_response, last_row_response = parallel_cyclic_reduction(
        sub_inner, diag_inner, super_inner, (rhs[:, 1:-1], first_unit, last_unit), 1
    )
    low_open = (place > 0).astype(jnp.float32)
    high_open = (place < device_count - 1).astype(jnp.float32)
    sub_first = sub_full[:, 0:1] * low_open
    diag_first = diag_full[:, 0:1] + super_full[:, 0:1] * first_row_response[:, 0:1]
    super_first = super_full[:, 0:1] * last_row_response[:, 0:1]
    right_first = rhs[:, 0:1] - super_full[:, 0:1] * particular_solution[:, 0:1]
    sub_last = sub_full[:, -1:] * first_row_response[:, -1:]
    diag_last = diag_full[:, -1:] + sub_full[:, -1:] * last_row_response[:, -1:]
    super_last = super_full[:, -1:] * high_open
    right_last = rhs[:, -1:] - sub_full[:, -1:] * particular_solution[:, -1:]
    reduced_sub = jnp.concatenate([sub_first, sub_last], 1)
    reduced_diag = jnp.concatenate([diag_first, diag_last], 1)
    reduced_super = jnp.concatenate([super_first, super_last], 1)
    reduced_right = jnp.concatenate([right_first, right_last], 1)
    gathered_lower_band, gathered_diagonal, gathered_upper_band, gathered_rhs = (
        lax.all_gather(reduced_sub, "gx", axis=1, tiled=True),
        lax.all_gather(reduced_diag, "gx", axis=1, tiled=True),
        lax.all_gather(reduced_super, "gx", axis=1, tiled=True),
        lax.all_gather(reduced_right, "gx", axis=1, tiled=True),
    )
    boundary_rows_gathered = parallel_cyclic_reduction(
        gathered_lower_band, gathered_diagonal, gathered_upper_band, (gathered_rhs,), 1
    )[0]
    ends = lax.dynamic_slice_in_dim(boundary_rows_gathered, 2 * place, 2, 1)
    interior = (
        particular_solution + first_row_response * ends[:, 0:1] + last_row_response * ends[:, 1:2]
    )
    return jnp.concatenate([ends[:, 0:1], interior, ends[:, 1:2]], 1)


def solution(mesh):
    in_specs = (P("gy", "gx", None), P(None, "gy", "gx", None), P("gy", "gx", None))
    out_specs = P("gy", "gx", None)
    return jax.shard_map(shards, mesh=mesh, in_specs=in_specs, out_specs=out_specs, check_vma=False)
```

profile of v0, /device:TPU:1, one launch (start us, length us, event | category | flops | bytes accessed | tf_op | source)
XLA Modules:
  0.0 117.3 jit_solution(6404665510396162908)
XLA Ops:
  0.0 1.4 %copy.19 = f32[4,256,128]{2,0,1:T(4,128)S(1)} copy(f32[4,256,128]{2,1,0:T(8,128)} %param.3) | data formatting | bytes 1048576 | tf_op args[0]
  1.4 4.9 %collective-permute-start.1 = (f32[4,2,128]{2,0,1:T(4,128)S(1)}, f32[4,2,128]{2,0,1:T(4,128)S(1)}, u32[]{:S(2)}, u32[]{:S(2)}) collective-permute-start(f32[4,2,128]{2,0,1:T(4,128)S(1)} %get-tuple-element.94), channel_id=1, source_target_pairs={{0,16},{16,32},{32,48},{48,64},{64,80},{80,96},{96,112},{112,128},... | collective-permute-start | bytes 12296 | tf_op jit(solution)/shard_map/ppermute | solution.py:15
  6.3 2.1 %collective-permute-start = (f32[4,2,128]{2,0,1:T(4,128)S(1)}, f32[4,2,128]{2,0,1:T(4,128)S(1)}, u32[]{:S(2)}, u32[]{:S(2)}) collective-permute-start(f32[4,2,128]{2,0,1:T(4,128)S(1)} %get-tuple-element.93), channel_id=1, source_target_pairs={{16,0},{32,16},{48,32},{64,48},{80,64},{96,80},{112,96},{128,112},... | collective-permute-start | bytes 12296 | tf_op jit(solution)/shard_map/ppermute | solution.py:17
  8.4 1.0 fusion.36
  9.4 4.9 %collective-permute-start.2 = (f32[2,256,128]{2,0,1:T(2,128)}, f32[2,256,128]{2,0,1:T(2,128)S(1)}, u32[]{:S(2)}, u32[]{:S(2)}) collective-permute-start(f32[2,256,128]{2,0,1:T(2,128)} %get-tuple-element.90), channel_id=1, source_target_pairs={{1,0},{2,1},{3,2},{4,3},{5,4},{6,5},{7,6},{8,7},{9,8},{10,9},{11,1... | collective-permute-start | bytes 786440 | tf_op jit(solution)/shard_map/ppermute | solution.py:17
  14.3 1.3 %fusion.37 = (f32[4,256,2]{2,0,1:T(4,128)}, f32[4,256,2]{2,0,1:T(4,128)}) fusion(f32[4,256,128]{2,0,1:T(4,128)S(1)} %copy.19), kind=kLoop, calls=%fused_computation.178 | loop fusion | bytes 32768 | tf_op jit(solution)/shard_map/slice | solution.py:37
  15.6 1.2 %fusion.32 = (f32[1,4,256,128]{3,2,1,0:T(8,128)}, f32[1,4,256,128]{3,2,1,0:T(8,128)}, f32[1,4,256,128]{3,2,1,0:T(8,128)}) fusion(f32[3,4,256,128]{3,2,1,0:T(8,128)S(1)} %copy-done.10), kind=kLoop, calls=%fused_computation.173 | loop fusion | bytes 3145728 | tf_op jit(solution)/shard_map/slice | solution.py:41
  16.9 0.5 copy_negate_fusion
  17.4 1.2 %fusion.33 = (f32[4,253,128]{2,0,1:T(4,128)S(1)}, f32[4,253,128]{2,0,1:T(4,128)S(1)}, f32[4,253,128]{2,0,1:T(4,128)}, f32[4,253,128]{2,0,1:T(4,128)}) fusion(f32[4,256,128]{2,0,1:T(4,128)S(1)} %get-tuple-element.85, f32[4,256,128]{2,0,1:T(4,128)S(1)} %get-tuple-element.86), kind=kLoop, calls=%fused_computation.174 | loop fusion | bytes 4145152 | tf_op jit(solution)/shard_map/slice | solution.py:119
  18.6 0.8 pad_slice_fusion.10
  19.5 1.1 pad_slice_fusion.8
  20.6 0.8 pad_slice_fusion.11
  21.5 0.4 constant_dynamic-update-slice_fusion.1
  22.0 2.4 %collective-permute-done.3 = f32[2,256,128]{2,0,1:T(2,128)} collective-permute-done((f32[2,256,128]{2,0,1:T(2,128)}, f32[2,256,128]{2,0,1:T(2,128)}, u32[]{:S(2)}, u32[]{:S(2)}) %collective-permute-start.3) | collective-permute-done | bytes 262176 | tf_op jit(solution)/shard_map/ppermute | solution.py:15
  24.4 4.7 %fusion.11 = f32[4,256,128]{2,0,1:T(4,128)S(1)} fusion(f32[4,256,128]{2,0,1:T(4,128)S(1)} %copy.19, f32[4,258,128]{2,0,1:T(4,128)S(1)} %get-tuple-element.96, f32[4,258,128]{2,0,1:T(4,128)S(1)} %constant_dynamic-update-slice_fusion, f32[1,4,256,128]{3,2,1,0:T(8,128)} %get-tuple-element.51, f32[1,4,256,128]{3,2,1,0:T(8,128)} %get-tuple-element.50, ...), kind=kLoop, calls=%fused_computation.28 | loop fusion | flops 6291456 | bytes 5259264 | tf_op jit(solution)/shard_map/add | solution.py:42
  29.3 0.9 copy-done.4
  30.3 0.6 fusion.18
  31.6 0.7 copy-done.6
  32.7 1.9 %multiply_add_fusion.26 = (f32[4,254,128]{2,0,1:T(4,128)S(1)}, f32[4,254,128]{2,0,1:T(4,128)S(1)}, f32[4,254,128]{2,0,1:T(4,128)S(1)}, f32[4,254,128]{2,0,1:T(4,...) fusion(f32[4,252,128]{2,0,1:T(4,128)S(1)} %get-tuple-element.178, ...), kind=kLoop, calls=%fused_computation.96 | loop fusion | flops 2340864 | bytes 9343992 | tf_op jit(solution)/shard_map/add | solution.py:75
  35.8 1.3 %multiply_add_fusion.24 = (f32[4,254,128]{2,0,1:T(4,128)S(1)}, f32[4,254,128]{2,0,1:T(4,128)S(1)}, f32[4,254,128]{2,0,1:T(4,128)S(1)}, f32[4,254,128]{2,0,1:T(4,...) fusion(f32[4,250,128]{2,0,1:T(4,128)S(1)} %get-tuple-element.174, ...), kind=kLoop, calls=%fused_computation.90 | loop fusion | flops 2340864 | bytes 11386880 | tf_op jit(solution)/shard_map/add | solution.py:75
  38.2 1.3 %multiply_add_fusion.22 = (f32[4,254,128]{2,0,1:T(4,128)S(1)}, f32[4,254,128]{2,0,1:T(4,128)S(1)}, f32[4,254,128]{2,0,1:T(4,128)S(1)}, f32[4,254,128]{2,0,1:T(4,...) fusion(f32[4,246,128]{2,0,1:T(4,128)S(1)} %get-tuple-element.166, ...), kind=kLoop, calls=%fused_computation.84 | loop fusion | flops 2340864 | bytes 11329536 | tf_op jit(solution)/shard_map/add | solution.py:75
  40.5 1.2 %multiply_add_fusion.20 = (f32[4,254,128]{2,0,1:T(4,128)S(1)}, f32[4,254,128]{2,0,1:T(4,128)S(1)}, f32[4,254,128]{2,0,1:T(4,128)S(1)}, f32[4,254,128]{2,0,1:T(4,...) fusion(f32[4,238,128]{2,0,1:T(4,128)S(1)} %get-tuple-element.158, ...), kind=kLoop, calls=%fused_computation.78 | loop fusion | flops 2340864 | bytes 11214848 | tf_op jit(solution)/shard_map/add | solution.py:75
  42.8 1.1 multiply_add_fusion.18
  44.8 1.1 multiply_add_fusion.16
  46.2 1.1 multiply_add_fusion.8
  47.5 0.5 add_divide_fusion.2
  48.0 20.7 %all_gather.12 = f32[4,32,128]{2,0,1:T(4,128)S(1)} all-gather(f32[4,2,128]{2,0,1:T(4,128)S(1)} %pad_maximum_fusion.5), channel_id=1, replica_groups=mesh['gx'=16,'gy'=16] {'gx'}, dimensions={1}, use_global_device_ids=true | all-gather | bytes 69632 | tf_op jit(solution)/shard_map/all_gather | solution.py:144
  68.8 0.7 add_divide_fusion.1
  69.5 15.0 %all_gather.15 = f32[4,32,128]{2,0,1:T(4,128)S(1)} all-gather(f32[4,2,128]{2,0,1:T(4,128)S(1)} %pad_maximum_fusion.8), channel_id=1, replica_groups=mesh['gx'=16,'gy'=16] {'gx'}, dimensions={1}, use_global_device_ids=true | all-gather | bytes 69632 | tf_op jit(solution)/shard_map/all_gather | solution.py:143
  84.5 15.7 %all_gather.14 = f32[4,32,128]{2,0,1:T(4,128)S(1)} all-gather(f32[4,2,128]{2,0,1:T(4,128)S(1)} %pad_maximum_fusion.7), channel_id=1, replica_groups=mesh['gx'=16,'gy'=16] {'gx'}, dimensions={1}, use_global_device_ids=true | all-gather | bytes 69632 | tf_op jit(solution)/shard_map/all_gather | solution.py:142
  100.3 14.9 %all_gather.13 = f32[4,32,128]{2,0,1:T(4,128)S(1)} all-gather(f32[4,2,128]{2,0,1:T(4,128)S(1)} %pad_maximum_fusion.6), channel_id=1, replica_groups=mesh['gx'=16,'gy'=16] {'gx'}, dimensions={1}, use_global_device_ids=true | all-gather | bytes 69632 | tf_op jit(solution)/shard_map/all_gather | solution.py:141
  116.5 0.8 copy.26
  (120 shorter events, 8.4 us)
Async XLA Ops:
  1.4 20.1 %collective-permute-start.1 = (f32[4,2,128]{2,0,1:T(4,128)S(1)}, f32[4,2,128]{2,0,1:T(4,128)S(1)}, u32[]{:S(2)}, u32[]{:S(2)}) collective-permute-start(f32[4,2,128]{2,0,1:T(4,128)S(1)} %get-tuple-element.94), channel_id=1, source_target_pairs={{0,16},{16,32},{32,48},{48,64},{64,80},{80,96},{96,112},{112,128},... | collective-permute-start | bytes 12296 | tf_op jit(solution)/shard_map/ppermute | solution.py:15
  6.3 9.3 %copy-start.10 = (f32[3,4,256,128]{3,2,1,0:T(8,128)S(1)}, f32[3,4,256,128]{3,2,1,0:T(8,128)}, u32[]{:S(2)}) copy-start(f32[3,4,256,128]{3,2,1,0:T(8,128)} %param.4) | copy-start | bytes 4718596
  6.3 15.6 %collective-permute-start = (f32[4,2,128]{2,0,1:T(4,128)S(1)}, f32[4,2,128]{2,0,1:T(4,128)S(1)}, u32[]{:S(2)}, u32[]{:S(2)}) collective-permute-start(f32[4,2,128]{2,0,1:T(4,128)S(1)} %get-tuple-element.93), channel_id=1, source_target_pairs={{16,0},{32,16},{48,32},{64,48},{80,64},{96,80},{112,96},{128,112},... | collective-permute-start | bytes 12296 | tf_op jit(solution)/shard_map/ppermute | solution.py:17
  9.4 12.6 %collective-permute-start.2 = (f32[2,256,128]{2,0,1:T(2,128)}, f32[2,256,128]{2,0,1:T(2,128)S(1)}, u32[]{:S(2)}, u32[]{:S(2)}) collective-permute-start(f32[2,256,128]{2,0,1:T(2,128)} %get-tuple-element.90), channel_id=1, source_target_pairs={{1,0},{2,1},{3,2},{4,3},{5,4},{6,5},{7,6},{8,7},{9,8},{10,9},{11,1... | collective-permute-start | bytes 786440 | tf_op jit(solution)/shard_map/ppermute | solution.py:17
  14.3 10.1 %collective-permute-start.3 = (f32[2,256,128]{2,0,1:T(2,128)}, f32[2,256,128]{2,0,1:T(2,128)}, u32[]{:S(2)}, u32[]{:S(2)}) collective-permute-start(f32[2,256,128]{2,0,1:T(2,128)} %get-tuple-element.89), channel_id=1, source_target_pairs={{0,1},{1,2},{2,3},{3,4},{4,5},{5,6},{6,7},{7,8},{8,9},{9,10},{10,1... | collective-permute-start | bytes 786440 | tf_op jit(solution)/shard_map/ppermute | solution.py:15
  15.6 1.3 %copy-start.11 = (f32[4,256,128]{2,1,0:T(8,128)S(1)}, f32[4,256,128]{2,1,0:T(8,128)}, u32[]{:S(2)}) copy-start(f32[4,256,128]{2,1,0:T(8,128)} %param.5) | copy-start | bytes 1572868
  18.6 2.9 %copy-start = (f32[4,256,128]{2,1,0:T(8,128)S(1)}, f32[4,256,128]{2,1,0:T(8,128)}, u32[]{:S(2)}) copy-start(f32[4,256,128]{2,1,0:T(8,128)} %param.3) | copy-start | bytes 1572868
  21.5 3.0 %copy-start.1 = (f32[4,256,2]{2,0,1:T(4,128)S(1)}, f32[4,256,2]{2,0,1:T(4,128)}, u32[]{:S(2)}) copy-start(f32[4,256,2]{2,0,1:T(4,128)} %get-tuple-element.91) | copy-start | bytes 24580
  21.5 3.0 %copy-start.2 = (f32[4,256,2]{2,0,1:T(4,128)S(1)}, f32[4,256,2]{2,0,1:T(4,128)}, u32[]{:S(2)}) copy-start(f32[4,256,2]{2,0,1:T(4,128)} %get-tuple-element.92) | copy-start | bytes 24580
  21.5 3.0 %copy-start.3 = (f32[1,4,256,128]{3,2,1,0:T(8,128)S(1)}, f32[1,4,256,128]{3,2,1,0:T(8,128)}, u32[]{:S(2)}) copy-start(f32[1,4,256,128]{3,2,1,0:T(8,128)} %get-tuple-element.49) | copy-start | bytes 1572868
  29.1 1.0 copy-start.4
  29.1 1.2 %copy-start.5 = (f32[4,253,128]{2,0,1:T(4,128)S(1)}, f32[4,253,128]{2,0,1:T(4,128)}, u32[]{:S(2)}) copy-start(f32[4,253,128]{2,0,1:T(4,128)} %get-tuple-element.225) | copy-start | bytes 1554436
  31.2 1.0 copy-start.6
  31.2 1.2 %copy-start.7 = (f32[4,253,128]{2,0,1:T(4,128)S(1)}, f32[4,253,128]{2,0,1:T(4,128)}, u32[]{:S(2)}) copy-start(f32[4,253,128]{2,0,1:T(4,128)} %get-tuple-element.226) | copy-start | bytes 1554436
  31.2 1.3 %copy-start.8 = (f32[4,253,128]{2,0,1:T(4,128)S(1)}, f32[4,253,128]{2,0,1:T(4,128)}, u32[]{:S(2)}) copy-start(f32[4,253,128]{2,0,1:T(4,128)} %get-tuple-element.227) | copy-start | bytes 1554436
  31.3 1.5 %copy-start.9 = (f32[4,253,128]{2,0,1:T(4,128)S(1)}, f32[4,253,128]{2,0,1:T(4,128)}, u32[]{:S(2)}) copy-start(f32[4,253,128]{2,0,1:T(4,128)} %pad_slice_fusion.11) | copy-start | bytes 1554436
where the time goes:
time: 118 us; the launch traced here: 117 us
  blocking collectives  66.3 us (56%)
  other arithmetic  18.4 us (16%)
  local copies, waits for them, and re-layouts  17.5 us (15%)
  starting transfers between devices  11.9 us (10%)
  waiting for transfers between devices  2.44 us (2%)
    all_gather x1, blocking collectives, shards(): lax.all_gather(reduced_right, 'gx', axis=1, tiled=True)  20.7 us
    all_gather x1, blocking collectives, shards(): lax.all_gather(reduced_diag, 'gx', axis=1, tiled=True)  15.7 us
    all_gather x1, blocking collectives, shards(): lax.all_gather(reduced_super, 'gx', axis=1, tiled=True)  15 us
    all_gather x1, blocking collectives, shards(): lax.all_gather(reduced_sub, 'gx', axis=1, tiled=True)  14.9 us
    add x11, other arithmetic, combine_rows(): value + factor_low * lower_value + factor_high * upper_value  9.81 us
    ppermute x2, starting transfers between devices, padded_2(): lax.ppermute(head, axis, [((i + 1) % count, i) for i in range(ends)])  6.98 us
    ppermute x2, starting transfers between devices, padded_2(): lax.ppermute(tail, axis, [(i, (i + 1) % count) for i in range(ends)])  4.93 us
    add x1, other arithmetic, build_rhs(): field - transport + 0.05 * (curve_y + curve_z)  4.7 us
  transfers between devices with their start and end apart: 4, of which 1 were waited for; matrix products, arithmetic and copies ran while one was open for 7% of the time, Pallas kernels for 0%

commit v1 on v0

--- a/solution.py
+++ b/solution.py
@@ -137,11 +137,12 @@
     reduced_diag = jnp.concatenate([diag_first, diag_last], 1)
     reduced_super = jnp.concatenate([super_first, super_last], 1)
     reduced_right = jnp.concatenate([right_first, right_last], 1)
+    stacked = jnp.concatenate([reduced_sub, reduced_diag, reduced_super, reduced_right], 1)
+    gathered = lax.all_gather(stacked, "gx", axis=1, tiled=True)
+    gathered = gathered.reshape(gathered.shape[0], device_count, 4, 2, gathered.shape[-1])
     gathered_lower_band, gathered_diagonal, gathered_upper_band, gathered_rhs = (
-        lax.all_gather(reduced_sub, "gx", axis=1, tiled=True),
-        lax.all_gather(reduced_diag, "gx", axis=1, tiled=True),
-        lax.all_gather(reduced_super, "gx", axis=1, tiled=True),
-        lax.all_gather(reduced_right, "gx", axis=1, tiled=True),
+        gathered[:, :, k].reshape(gathered.shape[0], 2 * device_count, gathered.shape[-1])
+        for k in range(4)
     )
     boundary_rows_gathered = parallel_cyclic_reduction(
         gathered_lower_band, gathered_diagonal, gathered_upper_band, (gathered_rhs,), 1

time: 118 us -> 55.1 us (0.47)
  blocking collectives: 66.3 us -> 19.3 us
  other arithmetic: 18.4 us -> 9.54 us
  local copies, waits for them, and re-layouts: 17.5 us -> 12.8 us
  waiting for transfers between devices: 2.44 us -> 0.01 us
    all_gather x4 -> x1, blocking collectives: 66.3 us -> 19.3 us  [shards(): gathered = lax.all_gather(stacked, 'gx', axis=1, tiled=True)]
    add x11, other arithmetic: 9.81 us -> 4.48 us  [combine_rows(): value + factor_low * lower_value + factor_high * upper_value]
    add x1, other arithmetic: 4.7 us -> 1.15 us  [build_rhs(): field - transport + 0.05 * (curve_y + curve_z)]
    slice x1 -> x2, local copies, waits for them, and re-layouts: 0.01 us -> 2.62 us  [padded_2(): head = lax.slice_in_dim(cells, 0, width, axis=dim)]
    ppermute x2, waiting for transfers between devices: 2.44 us -> 0.01 us  [padded_2(): lax.ppermute(tail, axis, [(i, (i + 1) % count) for i in range(ends)])]
    slice x2 -> x1, local copies, waits for them, and re-layouts: 2.18 us -> 0.12 us  [shards(): gathered[:, :, k]]
    slice x26, local copies, waits for them, and re-layouts: 3.68 us -> 2.09 us  [rows_above(): lax.slice_in_dim(values, stride, length, axis=sweep_direction)]
    ppermute x2, starting transfers between devices: 6.98 us -> 8.41 us  [padded_2(): lax.ppermute(head, axis, [((i + 1) % count, i) for i in range(ends)])]
  transfers between devices with their start and end apart: 4 -> 4, of which waited for: 1 -> 0; matrix products, arithmetic and copies ran while one was open for 7% -> 12% of each run, Pallas kernels for 0% -> 0%
where the time goes in v1:
time: 55.1 us; the launch traced here: 54.8 us
  blocking collectives  19.3 us (35%)
  local copies, waits for them, and re-layouts  12.8 us (23%)
  starting transfers between devices  12.4 us (23%)
  other arithmetic  9.54 us (17%)
  between operations  0.83 us (2%)
    all_gather x1, blocking collectives, shards(): gathered = lax.all_gather(stacked, 'gx', axis=1, tiled=True)  19.3 us
    ppermute x2, starting transfers between devices, padded_2(): lax.ppermute(head, axis, [((i + 1) % count, i) for i in range(ends)])  8.41 us
    add x11, other arithmetic, combine_rows(): value + factor_low * lower_value + factor_high * upper_value  4.48 us
    ppermute x2, starting transfers between devices, padded_2(): lax.ppermute(tail, axis, [(i, (i + 1) % count) for i in range(ends)])  3.95 us
    unnamed x16, local copies, waits for them, and re-layouts  3.76 us
    slice x40, local copies, waits for them, and re-layouts, rows_below(): lax.slice_in_dim(values, 0, length - stride, axis=sweep_direction)  2.66 us
    slice x2, local copies, waits for them, and re-layouts, padded_2(): head = lax.slice_in_dim(cells, 0, width, axis=dim)  2.62 us
    slice x26, local copies, waits for them, and re-layouts, rows_above(): lax.slice_in_dim(values, stride, length, axis=sweep_direction)  2.09 us
  transfers between devices with their start and end apart: 4, of which 0 were waited for; matrix products, arithmetic and copies ran while one was open for 12% of the time, Pallas kernels for 0%

profile of v1, /device:TPU:1, one launch (start us, length us, event | category | flops | bytes accessed | tf_op | source)
XLA Modules:
  0.0 54.8 jit_solution(11624598500980363579)
XLA Ops:
  0.0 1.9 %fusion.76 = (f32[2,256,128]{2,1,0:T(8,128)}, f32[2,256,128]{2,1,0:T(8,128)}) fusion(f32[4,256,128]{2,1,0:T(8,128)} %param.3), kind=kLoop, calls=%fused_computation.204 | loop fusion | bytes 1048576 | tf_op jit(solution)/shard_map/slice | solution.py:11
  1.9 2.0 %collective-permute-start.3 = (f32[2,256,128]{2,1,0:T(8,128)}, f32[2,256,128]{2,1,0:T(8,128)}, u32[]{:S(2)}, u32[]{:S(2)}) collective-permute-start(f32[2,256,128]{2,1,0:T(8,128)} %get-tuple-element.169), channel_id=1, source_target_pairs={{0,1},{1,2},{2,3},{3,4},{4,5},{5,6},{6,7},{7,8},{8,9},{9,10},{10,1... | collective-permute-start | bytes 786440 | tf_op jit(solution)/shard_map/ppermute | solution.py:15
  3.9 3.7 %collective-permute-start.2 = (f32[2,256,128]{2,1,0:T(8,128)}, f32[2,256,128]{2,1,0:T(8,128)S(1)}, u32[]{:S(2)}, u32[]{:S(2)}) collective-permute-start(f32[2,256,128]{2,1,0:T(8,128)} %get-tuple-element.168), channel_id=1, source_target_pairs={{1,0},{2,1},{3,2},{4,3},{5,4},{6,5},{7,6},{8,7},{9,8},{10,9},{11,1... | collective-permute-start | bytes 786440 | tf_op jit(solution)/shard_map/ppermute | solution.py:17
  7.6 0.7 %fusion.78 = (f32[4,2,128]{2,1,0:T(2,128)S(1)}, f32[4,2,128]{2,1,0:T(2,128)S(1)}) fusion(f32[4,256,128]{2,1,0:T(8,128)} %param.3), kind=kLoop, calls=%fused_computation.206 | loop fusion | bytes 16384 | tf_op jit(solution)/shard_map/slice | solution.py:11
  8.4 4.7 %collective-permute-start = (f32[4,2,128]{2,1,0:T(2,128)S(1)}, f32[4,2,128]{2,1,0:T(2,128)S(1)}, u32[]{:S(2)}, u32[]{:S(2)}) collective-permute-start(f32[4,2,128]{2,1,0:T(2,128)S(1)} %get-tuple-element.175), channel_id=1, source_target_pairs={{16,0},{32,16},{48,32},{64,48},{80,64},{96,80},{112,96},{128,112},... | collective-permute-start | bytes 12296 | tf_op jit(solution)/shard_map/ppermute | solution.py:17
  13.1 1.9 %collective-permute-start.1 = (f32[4,2,128]{2,1,0:T(2,128)S(1)}, f32[4,2,128]{2,1,0:T(2,128)S(1)}, u32[]{:S(2)}, u32[]{:S(2)}) collective-permute-start(f32[4,2,128]{2,1,0:T(2,128)S(1)} %get-tuple-element.176), channel_id=1, source_target_pairs={{0,16},{16,32},{32,48},{48,64},{64,80},{80,96},{96,112},{112,128},... | collective-permute-start | bytes 12296 | tf_op jit(solution)/shard_map/ppermute | solution.py:15
  15.0 1.1 %multiply_add_fusion.26 = (f32[4,256,128]{2,1,0:T(8,128)S(1)}, f32[4,256,128]{2,1,0:T(8,128)S(1)}) fusion(f32[4,256,128]{2,1,0:T(8,128)} %param.5), kind=kLoop, calls=%fused_computation.95 | loop fusion | flops 393216 | bytes 1572864 | tf_op jit(solution)/shard_map/add | solution.py:114
  16.1 1.2 %fusion.73 = (f32[4,253,128]{2,1,0:T(8,128)S(1)}, f32[4,253,128]{2,1,0:T(8,128)S(1)}, f32[4,253,128]{2,1,0:T(8,128)}, f32[4,253,128]{2,1,0:T(8,128)}) fusion(f32[4,256,128]{2,1,0:T(8,128)S(1)} %get-tuple-element.165, f32[4,256,128]{2,1,0:T(8,128)S(1)} %get-tuple-element.164), kind=kLoop, calls=%fused_computation.201 | loop fusion | bytes 4145152 | tf_op jit(solution)/shard_map/slice | solution.py:119
  17.4 0.8 %pad_slice_fusion.9 = f32[4,253,128]{2,1,0:T(8,128)} fusion(f32[4,253,128]{2,1,0:T(8,128)S(1)} %get-tuple-element.161), kind=kLoop, calls=%fused_computation.97 | loop fusion | bytes 1036288 | tf_op jit(solution)/shard_map/slice | solution.py:49
  18.3 1.1 %pad_slice_fusion.4 = (f32[4,253,128]{2,1,0:T(8,128)}, f32[4,253,128]{2,1,0:T(8,128)}) fusion(f32[4,1,128]{2,1,0:T(1,128)S(1)} %get-tuple-element.93, f32[4,1,128]{2,1,0:T(1,128)S(1)} %get-tuple-element.94), kind=kLoop, calls=%fused_computation.4 | loop fusion | bytes 1040384 | tf_op jit(solution)/shard_map/slice | solution.py:60
  19.3 0.2 fusion.77
  19.5 1.1 %constant_dynamic-update-slice_fusion.5 = f32[6,256,128]{2,1,0:T(8,128)S(1)} fusion(f32[2,256,128]{2,1,0:T(8,128)} %collective-permute-done.3), kind=kLoop, calls=%fused_computation.133 | loop fusion | bytes 524288
  20.8 0.2 copy-done.6
  21.0 1.2 %fusion.10 = f32[4,256,128]{2,1,0:T(8,128)S(1)} fusion(f32[4,256,128]{2,1,0:T(8,128)S(1)} %copy-done, f32[4,2,128]{2,1,0:T(2,128)S(1)} %collective-permute-done.1, f32[4,258,128]{2,1,0:T(8,128)S(1)} %constant_dynamic-update-slice_fusion, f32[4,256,2]{2,1,0:T(8,128)S(1)} %get-tuple-element.174, f32[4,256,2]{2,1,0:T(8,128)S(1)} %get-tuple-element.173, ...), kind=kLoop, calls=%fused_computation.20 | loop fusion | flops 6029312 | bytes 5787648 | tf_op jit(solution)/shard_map/add | solution.py:42
  22.3 0.9 %copy-done.4 = f32[4,253,128]{2,1,0:T(8,128)S(1)} copy-done((f32[4,253,128]{2,1,0:T(8,128)S(1)}, f32[4,253,128]{2,1,0:T(8,128)}, u32[]{:S(2)}) %copy-start.4) | copy-done | bytes 518168
  23.4 0.3 fusion.15
  23.7 0.2 fusion.17
  24.1 0.9 %copy-done.1 = f32[4,253,128]{2,1,0:T(8,128)S(1)} copy-done((f32[4,253,128]{2,1,0:T(8,128)S(1)}, f32[4,253,128]{2,1,0:T(8,128)}, u32[]{:S(2)}) %copy-start.1) | copy-done | bytes 518168
  25.2 0.2 copy-done.3
  25.3 0.6 %multiply_add_fusion.6 = (f32[4,254,128]{2,1,0:T(8,128)S(1)}, f32[4,254,128]{2,1,0:T(8,128)S(1)}, f32[4,254,128]{2,1,0:T(8,128)S(1)}, f32[4,254,128]{2,1,0:T(8,1...) fusion(f32[4,252,128]{2,1,0:T(8,128)S(1)} %get-tuple-element.159, ...), kind=kLoop, calls=%fused_computation.43 | loop fusion | flops 2340864 | bytes 9343992 | tf_op jit(solution)/shard_map/add | solution.py:75
  26.5 0.9 %multiply_add_fusion.5 = (f32[4,254,128]{2,1,0:T(8,128)S(1)}, f32[4,254,128]{2,1,0:T(8,128)S(1)}, f32[4,254,128]{2,1,0:T(8,128)S(1)}, f32[4,254,128]{2,1,0:T(8,1...) fusion(f32[4,250,128]{2,1,0:T(8,128)S(1)} %get-tuple-element.155, ...), kind=kLoop, calls=%fused_computation.42 | loop fusion | flops 2340864 | bytes 11386880 | tf_op jit(solution)/shard_map/add | solution.py:75
  27.6 0.2 multiply_add_fusion.22
  28.0 0.7 %multiply_add_fusion.4 = (f32[4,254,128]{2,1,0:T(8,128)S(1)}, f32[4,254,128]{2,1,0:T(8,128)S(1)}, f32[4,254,128]{2,1,0:T(8,128)S(1)}, f32[4,254,128]{2,1,0:T(8,1...) fusion(f32[4,246,128]{2,1,0:T(8,128)S(1)} %get-tuple-element.147, ...), kind=kLoop, calls=%fused_computation.41 | loop fusion | flops 2340864 | bytes 11329536 | tf_op jit(solution)/shard_map/add | solution.py:75
  29.3 0.4 multiply_add_fusion.3
  29.9 0.2 multiply_add_fusion.18
  30.3 0.5 multiply_add_fusion.2
  31.4 0.5 multiply_add_fusion.1
  32.2 0.4 multiply_add_fusion.7
  32.8 0.3 add_divide_fusion.2
  33.1 0.4 add_divide_fusion
  33.6 19.3 %all_gather.3 = f32[4,128,128]{2,1,0:T(8,128)S(1)} all-gather(f32[4,8,128]{2,1,0:T(8,128)S(1)} %concatenate.548), channel_id=1, replica_groups=mesh['gx'=16,'gy'=16] {'gx'}, dimensions={1}, use_global_device_ids=true | all-gather | bytes 278528 | tf_op jit(solution)/shard_map/all_gather | solution.py:141
  54.0 0.8 %pad_maximum_fusion.3 = f32[4,256,128]{2,1,0:T(8,128)} fusion(f32[4,1,128]{2,1,0:T(1,128)S(1)} %get-tuple-element.223, f32[4,254,128]{2,1,0:T(8,128)S(1)} %multiply_add_fusion, f32[4,1,128]{2,1,0:T(1,128)S(1)} %get-tuple-element.222), kind=kLoop, calls=%fused_computation.33 | loop fusion | flops 262144 | bytes 1048576 | tf_op jit(solution)/shard_map/concatenate | solution.py:154
  (100 shorter events, 4.5 us)
Async XLA Ops:
  1.9 17.7 %collective-permute-start.3 = (f32[2,256,128]{2,1,0:T(8,128)}, f32[2,256,128]{2,1,0:T(8,128)}, u32[]{:S(2)}, u32[]{:S(2)}) collective-permute-start(f32[2,256,128]{2,1,0:T(8,128)} %get-tuple-element.169), channel_id=1, source_target_pairs={{0,1},{1,2},{2,3},{3,4},{4,5},{5,6},{6,7},{7,8},{8,9},{9,10},{10,1... | collective-permute-start | bytes 786440 | tf_op jit(solution)/shard_map/ppermute | solution.py:15
  3.9 16.8 %collective-permute-start.2 = (f32[2,256,128]{2,1,0:T(8,128)}, f32[2,256,128]{2,1,0:T(8,128)S(1)}, u32[]{:S(2)}, u32[]{:S(2)}) collective-permute-start(f32[2,256,128]{2,1,0:T(8,128)} %get-tuple-element.168), channel_id=1, source_target_pairs={{1,0},{2,1},{3,2},{4,3},{5,4},{6,5},{7,6},{8,7},{9,8},{10,9},{11,1... | collective-permute-start | bytes 786440 | tf_op jit(solution)/shard_map/ppermute | solution.py:17
  8.4 12.4 %collective-permute-start = (f32[4,2,128]{2,1,0:T(2,128)S(1)}, f32[4,2,128]{2,1,0:T(2,128)S(1)}, u32[]{:S(2)}, u32[]{:S(2)}) collective-permute-start(f32[4,2,128]{2,1,0:T(2,128)S(1)} %get-tuple-element.175), channel_id=1, source_target_pairs={{16,0},{32,16},{48,32},{64,48},{80,64},{96,80},{112,96},{128,112},... | collective-permute-start | bytes 12296 | tf_op jit(solution)/shard_map/ppermute | solution.py:17
  13.1 7.7 %collective-permute-start.1 = (f32[4,2,128]{2,1,0:T(2,128)S(1)}, f32[4,2,128]{2,1,0:T(2,128)S(1)}, u32[]{:S(2)}, u32[]{:S(2)}) collective-permute-start(f32[4,2,128]{2,1,0:T(2,128)S(1)} %get-tuple-element.176), channel_id=1, source_target_pairs={{0,16},{16,32},{32,48},{48,64},{64,80},{80,96},{96,112},{112,128},... | collective-permute-start | bytes 12296 | tf_op jit(solution)/shard_map/ppermute | solution.py:15
  17.4 2.0 %copy-start = (f32[4,256,128]{2,1,0:T(8,128)S(1)}, f32[4,256,128]{2,1,0:T(8,128)}, u32[]{:S(2)}) copy-start(f32[4,256,128]{2,1,0:T(8,128)} %param.3) | copy-start | bytes 1572868
  19.5 1.5 %copy-start.6 = (f32[3,4,256,128]{3,2,1,0:T(8,128)S(1)}, f32[3,4,256,128]{3,2,1,0:T(8,128)}, u32[]{:S(2)}) copy-start(f32[3,4,256,128]{3,2,1,0:T(8,128)} %param.4) | copy-start | bytes 4718596
  22.2 1.0 %copy-start.4 = (f32[4,253,128]{2,1,0:T(8,128)S(1)}, f32[4,253,128]{2,1,0:T(8,128)}, u32[]{:S(2)}) copy-start(f32[4,253,128]{2,1,0:T(8,128)} %get-tuple-element.224) | copy-start | bytes 1554436
  22.2 1.2 %copy-start.5 = (f32[4,253,128]{2,1,0:T(8,128)S(1)}, f32[4,253,128]{2,1,0:T(8,128)}, u32[]{:S(2)}) copy-start(f32[4,253,128]{2,1,0:T(8,128)} %get-tuple-element.225) | copy-start | bytes 1554436
  24.0 1.0 %copy-start.1 = (f32[4,253,128]{2,1,0:T(8,128)S(1)}, f32[4,253,128]{2,1,0:T(8,128)}, u32[]{:S(2)}) copy-start(f32[4,253,128]{2,1,0:T(8,128)} %pad_slice_fusion.9) | copy-start | bytes 1554436
  24.0 1.2 %copy-start.2 = (f32[4,253,128]{2,1,0:T(8,128)S(1)}, f32[4,253,128]{2,1,0:T(8,128)}, u32[]{:S(2)}) copy-start(f32[4,253,128]{2,1,0:T(8,128)} %get-tuple-element.226) | copy-start | bytes 1554436
  24.0 1.3 %copy-start.3 = (f32[4,253,128]{2,1,0:T(8,128)S(1)}, f32[4,253,128]{2,1,0:T(8,128)}, u32[]{:S(2)}) copy-start(f32[4,253,128]{2,1,0:T(8,128)} %get-tuple-element.227) | copy-start | bytes 1554436

commit v2 on v1

--- a/solution.py
+++ b/solution.py
@@ -2,6 +2,8 @@
 import jax.numpy as jnp
 from jax import lax
 from jax.sharding import PartitionSpec as P
+from jax.experimental import pallas as pl
+from jax.experimental.pallas import tpu as pltpu
 
 
 def padded_2(cells, sides, width, closed):
@@ -104,54 +106,125 @@
     return tuple((value / main_diagonal for value in right_hand_sides))
 
 
+def to_chunks(values, chunks):
+    planes, length, lanes = values.shape
+    values = values.reshape(planes, chunks, length // chunks, lanes)
+    return values.transpose(2, 1, 0, 3).reshape(length // chunks, chunks * planes, lanes)
+
+
+def from_chunks(values, chunks):
+    rows, sublanes, lanes = values.shape
+    planes = sublanes // chunks
+    values = values.reshape(rows, chunks, planes, lanes).transpose(2, 1, 0, 3)
+    return values.reshape(planes, chunks * rows, lanes)
+
+
+def thomas_kernel(rate_ref, right_ref, part_ref, first_ref, last_ref, ratio_ref):
+    rows = rate_ref.shape[0]
+    zero = jnp.zeros(rate_ref.shape[1:], jnp.float32)
+    rate = rate_ref[1]
+    inverse = 1.0 / (1.0 + 2.0 * rate)
+    ratio = -rate * inverse
+    part = right_ref[1] * inverse
+    first = rate * inverse
+    ratio_ref[1] = ratio
+    part_ref[1] = part
+    first_ref[1] = first
+
+    def forward(i, carry):
+        ratio, part, first, _ = carry
+        rate = rate_ref[i]
+        inverse = 1.0 / ((1.0 + 2.0 * rate) + rate * ratio)
+        ratio = -rate * inverse
+        part = (right_ref[i] + rate * part) * inverse
+        first = rate * first * inverse
+        ratio_ref[i] = ratio
+        part_ref[i] = part
+        first_ref[i] = first
+        return ratio, part, first, inverse
+
+    _, part, first, inverse = lax.fori_loop(
+        2, rows - 1, forward, (ratio, part, first, zero), unroll=8
+    )
+    last = rate_ref[rows - 2] * inverse
+    last_ref[rows - 2] = last
+
+    def backward(j, carry):
+        part, first, last = carry
+        i = rows - 3 - j
+        ratio = ratio_ref[i]
+        part = part_ref[i] - ratio * part
+        first = first_ref[i] - ratio * first
+        last = -ratio * last
+        part_ref[i] = part
+        first_ref[i] = first
+        last_ref[i] = last
+        return part, first, last
+
+    lax.fori_loop(0, rows - 3, backward, (part, first, last), unroll=8)
+    for ref in (part_ref, first_ref, last_ref):
+        ref[0] = zero
+        ref[rows - 1] = zero
+
+
+def local_solve(rate, right):
+    shape = jax.ShapeDtypeStruct(rate.shape, jnp.float32)
+    return pl.pallas_call(
+        thomas_kernel,
+        out_shape=(shape, shape, shape),
+        scratch_shapes=[pltpu.VMEM(rate.shape, jnp.float32)],
+    )(rate, right)
+
+
 def shards(field, courant, diffusion_number):
+    chunks = 2
     y_padded = padded_2(field, (("gy", 0),), 2, True)
     x_padded = padded_2(field, (("gx", 1),), 2, False)
     rhs = build_rhs(field, courant, y_padded, x_padded)
     place = lax.axis_index("gx")
     device_count = lax.axis_size("gx")
-    sub_full = -diffusion_number
-    diag_full = 1.0 + 2.0 * diffusion_number
-    super_full = -diffusion_number
-    edge_zeros = jnp.zeros_like(rhs[:, 0:1])
-    inner_zeros = jnp.zeros_like(rhs[:, 3:])
-    sub_inner = jnp.concatenate([edge_zeros, sub_full[:, 2:-1]], 1)
-    super_inner = jnp.concatenate([super_full[:, 1:-2], edge_zeros], 1)
-    diag_inner = diag_full[:, 1:-1]
-    first_unit = jnp.concatenate([-sub_full[:, 1:2], inner_zeros], 1)
-    last_unit = jnp.concatenate([inner_zeros, -super_full[:, -2:-1]], 1)
-    particular_solution, first_row_response, last_row_response = parallel_cyclic_reduction(
-        sub_inner, diag_inner, super_inner, (rhs[:, 1:-1], first_unit, last_unit), 1
-    )
+    planes = field.shape[0]
+    rate = to_chunks(diffusion_number, chunks)
+    right = to_chunks(rhs, chunks)
+    part, first, last = local_solve(rate, right)
+    rows = rate.shape[0]
     low_open = (place > 0).astype(jnp.float32)
     high_open = (place < device_count - 1).astype(jnp.float32)
-    sub_first = sub_full[:, 0:1] * low_open
-    diag_first = diag_full[:, 0:1] + super_full[:, 0:1] * first_row_response[:, 0:1]
-    super_first = super_full[:, 0:1] * last_row_response[:, 0:1]
-    right_first = rhs[:, 0:1] - super_full[:, 0:1] * particular_solution[:, 0:1]
-    sub_last = sub_full[:, -1:] * first_row_response[:, -1:]
-    diag_last = diag_full[:, -1:] + sub_full[:, -1:] * last_row_response[:, -1:]
-    super_last = super_full[:, -1:] * high_open
-    right_last = rhs[:, -1:] - sub_full[:, -1:] * particular_solution[:, -1:]
-    reduced_sub = jnp.concatenate([sub_first, sub_last], 1)
-    reduced_diag = jnp.concatenate([diag_first, diag_last], 1)
-    reduced_super = jnp.concatenate([super_first, super_last], 1)
-    reduced_right = jnp.concatenate([right_first, right_last], 1)
-    stacked = jnp.concatenate([reduced_sub, reduced_diag, reduced_super, reduced_right], 1)
+    chunk_of = lax.broadcasted_iota(jnp.int32, (chunks, planes, 1), 0).reshape(chunks * planes, 1)
+    low_scale = jnp.where(chunk_of == 0, low_open, 1.0)
+    high_scale = jnp.where(chunk_of == chunks - 1, high_open, 1.0)
+    rate_first, rate_last = rate[0], rate[rows - 1]
+    sub_first = -rate_first * low_scale
+    diag_first = (1.0 + 2.0 * rate_first) - rate_first * first[1]
+    super_first = -rate_first * last[1]
+    right_first = right[0] + rate_first * part[1]
+    sub_last = -rate_last * first[rows - 2]
+    diag_last = (1.0 + 2.0 * rate_last) - rate_last * last[rows - 2]
+    super_last = -rate_last * high_scale
+    right_last = right[rows - 1] + rate_last * part[rows - 2]
+    stacked = jnp.stack(
+        [sub_first, sub_last, diag_first, diag_last, super_first, super_last, right_first, right_last]
+    )
+    lanes = stacked.shape[-1]
+    stacked = stacked.reshape(8, chunks, planes, lanes).transpose(2, 1, 0, 3)
+    stacked = stacked.reshape(planes, chunks * 8, lanes)
     gathered = lax.all_gather(stacked, "gx", axis=1, tiled=True)
-    gathered = gathered.reshape(gathered.shape[0], device_count, 4, 2, gathered.shape[-1])
+    gathered = gathered.reshape(planes, device_count, chunks, 4, 2, lanes)
     gathered_lower_band, gathered_diagonal, gathered_upper_band, gathered_rhs = (
-        gathered[:, :, k].reshape(gathered.shape[0], 2 * device_count, gathered.shape[-1])
-        for k in range(4)
+        gathered[:, :, :, k].reshape(planes, 2 * chunks * device_count, lanes) for k in range(4)
     )
     boundary_rows_gathered = parallel_cyclic_reduction(
         gathered_lower_band, gathered_diagonal, gathered_upper_band, (gathered_rhs,), 1
     )[0]
-    ends = lax.dynamic_slice_in_dim(boundary_rows_gathered, 2 * place, 2, 1)
-    interior = (
-        particular_solution + first_row_response * ends[:, 0:1] + last_row_response * ends[:, 1:2]
-    )
-    return jnp.concatenate([ends[:, 0:1], interior, ends[:, 1:2]], 1)
+    ends = lax.dynamic_slice_in_dim(boundary_rows_gathered, 2 * chunks * place, 2 * chunks, 1)
+    ends = ends.reshape(planes, chunks, 2, lanes).transpose(2, 1, 0, 3)
+    ends = ends.reshape(2, chunks * planes, lanes)
+    start_value, end_value = ends[0], ends[1]
+    solved = part + first * start_value[None] + last * end_value[None]
+    row = lax.broadcasted_iota(jnp.int32, (rows, 1, 1), 0)
+    solved = jnp.where(row == 0, start_value[None], solved)
+    solved = jnp.where(row == rows - 1, end_value[None], solved)
+    return from_chunks(solved, chunks)
 
 
 def solution(mesh):

time: 55.1 us -> 50.9 us (0.924)
  other arithmetic: 9.54 us -> 3.93 us
  Pallas kernels: 0 us -> 4.03 us
  local copies, waits for them, and re-layouts: 12.8 us -> 9.45 us
  blocking collectives: 19.3 us -> 20 us
    pallas_call x0 -> x1, Pallas kernels: none -> 4.03 us  [local_solve(): pl.pallas_call(thomas_kernel, out_shape=(shape, shape, shape), scratch_sh...]
    add x11 -> x4, other arithmetic: 4.48 us -> 0.46 us  [combine_rows(): value + factor_low * lower_value + factor_high * upper_value]
    transpose x0 -> x2, local copies, waits for them, and re-layouts: none -> 3.06 us  [the longest x1 2.18 us: to_chunks(): values.transpose(2, 1, 0, 3)]
    slice x40 -> x13, local copies, waits for them, and re-layouts: 2.66 us -> 0.21 us  [rows_below(): lax.slice_in_dim(values, 0, length - stride, axis=sweep_direction)]
    slice x26 -> x11, local copies, waits for them, and re-layouts: 2.09 us -> 0.19 us  [rows_above(): lax.slice_in_dim(values, stride, length, axis=sweep_direction)]
    add x2 -> x0, other arithmetic: 1.2 us -> none  [the longest x1 1.11 us: shards(): diag_full = 1.0 + 2.0 * diffusion_number]
    slice x3 -> x7, local copies, waits for them, and re-layouts: 1.34 us -> 0.27 us  [the longest x1 0.24 us: shards(): gathered[:, :, :, k].reshape(planes, 2 * chunks * device_count, lanes)]
    mul x0 -> x1, other arithmetic: none -> 0.85 us  [shards(): super_last = -rate_last * high_scale]
  transfers between devices with their start and end apart: 4 -> 4, of which waited for: 0 -> 0; matrix products, arithmetic and copies ran while one was open for 12% -> 8% of each run, Pallas kernels for 0% -> 0%
where the time goes in v2:
time: 50.9 us; the launch traced here: 50.4 us
  blocking collectives  20 us (39%)
  starting transfers between devices  12.4 us (24%)
  local copies, waits for them, and re-layouts  9.45 us (19%)
  Pallas kernels  4.03 us (8%)
  other arithmetic  3.93 us (8%)
  between operations  0.52 us (1%)
    all_gather x1, blocking collectives, shards(): gathered = lax.all_gather(stacked, 'gx', axis=1, tiled=True)  20 us
    ppermute x2, starting transfers between devices, padded_2(): lax.ppermute(head, axis, [((i + 1) % count, i) for i in range(ends)])  8.41 us
    pallas_call x1, Pallas kernels, local_solve(): pl.pallas_call(thomas_kernel, out_shape=(shape, shape, shape), scratch_sh...  4.03 us
    ppermute x2, starting transfers between devices, padded_2(): lax.ppermute(tail, axis, [(i, (i + 1) % count) for i in range(ends)])  4.03 us
    unnamed x14, local copies, waits for them, and re-layouts  3.19 us
    transpose x1, local copies, waits for them, and re-layouts, to_chunks(): values.transpose(2, 1, 0, 3)  2.18 us
    slice x2, local copies, waits for them, and re-layouts, padded_2(): head = lax.slice_in_dim(cells, 0, width, axis=dim)  1.87 us
    add x1, other arithmetic, build_rhs(): field - transport + 0.05 * (curve_y + curve_z)  1.14 us
  transfers between devices with their start and end apart: 4, of which 0 were waited for; matrix products, arithmetic and copies ran while one was open for 8% of the time, Pallas kernels for 0%

profile of v2, /device:TPU:1, one launch (start us, length us, event | category | flops | bytes accessed | tf_op | source)
XLA Modules:
  0.0 50.4 jit_solution(3513658561004448686)
XLA Ops:
  0.0 1.1 %fusion.29 = (f32[2,256,128]{2,1,0:T(8,128)S(1)}, f32[2,256,128]{2,1,0:T(8,128)S(1)}) fusion(f32[4,256,128]{2,1,0:T(8,128)} %param.3), kind=kLoop, calls=%fused_computation.98 | loop fusion | bytes 1048576 | tf_op jit(solution)/shard_map/slice | solution.py:13
  1.1 2.1 %collective-permute-start.3 = (f32[2,256,128]{2,1,0:T(8,128)S(1)}, f32[2,256,128]{2,1,0:T(8,128)S(1)}, u32[]{:S(2)}, u32[]{:S(2)}) collective-permute-start(f32[2,256,128]{2,1,0:T(8,128)S(1)} %get-tuple-element.44), channel_id=1, source_target_pairs={{0,1},{1,2},{2,3},{3,4},{4,5},{5,6},{6,7},{7,8},{8,9},{9,10},{10,1... | collective-permute-start | bytes 786440 | tf_op jit(solution)/shard_map/ppermute | solution.py:17
  3.2 3.8 %collective-permute-start.2 = (f32[2,256,128]{2,1,0:T(8,128)S(1)}, f32[2,256,128]{2,1,0:T(8,128)S(1)}, u32[]{:S(2)}, u32[]{:S(2)}) collective-permute-start(f32[2,256,128]{2,1,0:T(8,128)S(1)} %get-tuple-element.43), channel_id=1, source_target_pairs={{1,0},{2,1},{3,2},{4,3},{5,4},{6,5},{7,6},{8,7},{9,8},{10,9},{11,1... | collective-permute-start | bytes 786440 | tf_op jit(solution)/shard_map/ppermute | solution.py:19
  7.0 0.7 %fusion.31 = (f32[4,2,128]{2,1,0:T(2,128)S(1)}, f32[4,2,128]{2,1,0:T(2,128)S(1)}) fusion(f32[4,256,128]{2,1,0:T(8,128)} %param.3), kind=kLoop, calls=%fused_computation.100 | loop fusion | bytes 16384 | tf_op jit(solution)/shard_map/slice | solution.py:13
  7.8 4.6 %collective-permute-start = (f32[4,2,128]{2,1,0:T(2,128)S(1)}, f32[4,2,128]{2,1,0:T(2,128)S(1)}, u32[]{:S(2)}, u32[]{:S(2)}) collective-permute-start(f32[4,2,128]{2,1,0:T(2,128)S(1)} %get-tuple-element.50), channel_id=1, source_target_pairs={{16,0},{32,16},{48,32},{64,48},{80,64},{96,80},{112,96},{128,112},... | collective-permute-start | bytes 12296 | tf_op jit(solution)/shard_map/ppermute | solution.py:19
  12.4 1.9 %collective-permute-start.1 = (f32[4,2,128]{2,1,0:T(2,128)S(1)}, f32[4,2,128]{2,1,0:T(2,128)S(1)}, u32[]{:S(2)}, u32[]{:S(2)}) collective-permute-start(f32[4,2,128]{2,1,0:T(2,128)S(1)} %get-tuple-element.51), channel_id=1, source_target_pairs={{0,16},{16,32},{32,48},{48,64},{64,80},{80,96},{96,112},{112,128},... | collective-permute-start | bytes 12296 | tf_op jit(solution)/shard_map/ppermute | solution.py:17
  14.4 2.2 %copy.19 = f32[128,2,4,128]{3,2,1,0:T(4,128)} copy(f32[128,2,4,128]{3,0,1,2:T(8,128)} %bitcast.63) | data formatting | bytes 1048576 | tf_op jit(solution)/shard_map/transpose | solution.py:112
  16.5 0.9 %negate_multiply_fusion = (f32[1,2,4,128]{3,0,1,2:T(1,128)S(1)}, f32[1,2,4,128]{3,0,1,2:T(1,128)S(1)}, f32[1,2,4,128]{3,0,1,2:T(1,128)S(1)}, f32[1,2,4,128]{3,0,1,2:T(1,128)S(1)}) fusion(f32[2,4]{0,1:T(4,128)S(1)} %get-tuple-element.106, f32[128,2,4,128]{3,0,1,2:T(8,128)} %bitcast.64, f32[2,4]{0,1:T(4,128)S(1)} %get-tuple-element.105), kind=kLoop, calls=%fused_computation.83 | loop fusion | flops 4096 | bytes 24640 | tf_op jit(solution)/shard_map/mul | solution.py:203
  17.4 0.2 fusion.30
  17.7 0.1 constant_dynamic-update-slice_fusion.3
  17.9 1.2 %copy-done.2 = f32[3,4,256,128]{3,2,1,0:T(8,128)S(1)} copy-done((f32[3,4,256,128]{3,2,1,0:T(8,128)S(1)}, f32[3,4,256,128]{3,2,1,0:T(8,128)}, u32[]{:S(2)}) %copy-start.2) | copy-done | bytes 1572888
  19.0 1.1 %fusion.10 = f32[4,256,128]{2,1,0:T(8,128)S(1)} fusion(f32[4,256,128]{2,1,0:T(8,128)S(1)} %copy-done, f32[4,2,128]{2,1,0:T(2,128)S(1)} %collective-permute-done.1, f32[4,258,128]{2,1,0:T(8,128)S(1)} %constant_dynamic-update-slice_fusion, f32[4,256,2]{2,1,0:T(8,128)S(1)} %get-tuple-element.49, f32[4,256,2]{2,1,0:T(8,128)S(1)} %get-tuple-element.48, ...), kind=kLoop, calls=%fused_computation.16 | loop fusion | flops 6029312 | bytes 5787648 | tf_op jit(solution)/shard_map/add | solution.py:44
  20.2 0.3 copy.33
  20.5 0.8 %copy-done.1 = f32[4,2,128,128]{3,0,1,2:T(4,128)} copy-done((f32[4,2,128,128]{3,0,1,2:T(4,128)}, f32[4,2,128,128]{3,0,1,2:T(4,128)S(1)}, u32[]{:S(2)}) %copy-start.1) | copy-done | bytes 524312
  21.3 4.0 %shard_map.37 = (f32[128,8,128]{2,1,0:T(8,128)}, f32[128,8,128]{2,1,0:T(8,128)}, f32[128,8,128]{2,1,0:T(8,128)}) custom-call(f32[128,8,128]{2,1,0:T(8,128)} %bitcast.56, f32[128,8,128]{2,1,0:T(8,128)} %bitcast.54), custom_call_target="tpu_custom_call" | custom-call | tf_op jit(solution)/shard_map/pallas_call | solution.py:172
  25.4 0.7 %multiply_subtract_fusion.1 = (f32[1,8,128]{2,1,0:T(8,128)S(1)}, f32[1,8,128]{2,1,0:T(8,128)S(1)}, f32[1,8,128]{2,1,0:T(8,128)S(1)}, f32[1,8,128]{2,1,0:T(8,128)...) fusion(f32[1,8,128]{2,1,0:T(8,128)S(1)} %bitcast.69, f32[128,8,128]{2,1,0:T(8,128)} %get-tuple-element.8, ...), kind=kLoop, calls=%fused_computation.86 | loop fusion | flops 16384 | bytes 65536 | tf_op jit(solution)/shard_map/sub | solution.py:198
  26.2 0.1 stack.29
  26.2 20.0 %all_gather.3 = f32[4,256,128]{2,1,0:T(8,128)S(1)} all-gather(f32[4,16,128]{2,1,0:T(8,128)S(1)} %bitcast.65), channel_id=1, replica_groups=mesh['gx'=16,'gy'=16] {'gx'}, dimensions={1}, use_global_device_ids=true | all-gather | bytes 557056 | tf_op jit(solution)/shard_map/all_gather | solution.py:211
  46.3 0.2 fusion.27
  46.6 0.1 multiply_add_fusion.8
  46.8 0.1 multiply_add_fusion.7
  47.0 0.1 multiply_add_fusion.6
  47.1 0.1 multiply_add_fusion.5
  47.3 0.1 multiply_add_fusion.4
  47.4 0.1 multiply_add_fusion.3
  47.7 0.1 multiply_add_fusion.1
  47.9 0.1 multiply_add_fusion
  48.1 0.8 %copy-done.3 = f32[128,8,128]{2,1,0:T(8,128)S(1)} copy-done((f32[128,8,128]{2,1,0:T(8,128)S(1)}, f32[128,8,128]{2,1,0:T(8,128)}, u32[]{:S(2)}) %copy-start.3) | copy-done | bytes 524312
  48.9 0.2 copy-done.4
  49.0 0.2 copy-done.5
  49.2 0.3 select_select_fusion
  49.5 0.9 %copy.30 = f32[4,2,128,128]{3,2,1,0:T(8,128)} copy(f32[4,2,128,128]{3,0,1,2:T(4,128)S(1)} %bitcast.58) | data formatting | bytes 1048576 | tf_op jit(solution)/shard_map/transpose | solution.py:118
  (54 shorter events, 0.6 us)
Async XLA Ops:
  0.0 17.4 %copy-start = (f32[4,256,128]{2,1,0:T(8,128)S(1)}, f32[4,256,128]{2,1,0:T(8,128)}, u32[]{:S(2)}) copy-start(f32[4,256,128]{2,1,0:T(8,128)} %param.3) | copy-start | bytes 1572868
  1.1 16.5 %collective-permute-start.3 = (f32[2,256,128]{2,1,0:T(8,128)S(1)}, f32[2,256,128]{2,1,0:T(8,128)S(1)}, u32[]{:S(2)}, u32[]{:S(2)}) collective-permute-start(f32[2,256,128]{2,1,0:T(8,128)S(1)} %get-tuple-element.44), channel_id=1, source_target_pairs={{0,1},{1,2},{2,3},{3,4},{4,5},{5,6},{6,7},{7,8},{8,9},{9,10},{10,1... | collective-permute-start | bytes 786440 | tf_op jit(solution)/shard_map/ppermute | solution.py:17
  3.2 14.5 %collective-permute-start.2 = (f32[2,256,128]{2,1,0:T(8,128)S(1)}, f32[2,256,128]{2,1,0:T(8,128)S(1)}, u32[]{:S(2)}, u32[]{:S(2)}) collective-permute-start(f32[2,256,128]{2,1,0:T(8,128)S(1)} %get-tuple-element.43), channel_id=1, source_target_pairs={{1,0},{2,1},{3,2},{4,3},{5,4},{6,5},{7,6},{8,7},{9,8},{10,9},{11,1... | collective-permute-start | bytes 786440 | tf_op jit(solution)/shard_map/ppermute | solution.py:19
  7.8 10.0 %collective-permute-start = (f32[4,2,128]{2,1,0:T(2,128)S(1)}, f32[4,2,128]{2,1,0:T(2,128)S(1)}, u32[]{:S(2)}, u32[]{:S(2)}) collective-permute-start(f32[4,2,128]{2,1,0:T(2,128)S(1)} %get-tuple-element.50), channel_id=1, source_target_pairs={{16,0},{32,16},{48,32},{64,48},{80,64},{96,80},{112,96},{128,112},... | collective-permute-start | bytes 12296 | tf_op jit(solution)/shard_map/ppermute | solution.py:19
  12.4 5.4 %collective-permute-start.1 = (f32[4,2,128]{2,1,0:T(2,128)S(1)}, f32[4,2,128]{2,1,0:T(2,128)S(1)}, u32[]{:S(2)}, u32[]{:S(2)}) collective-permute-start(f32[4,2,128]{2,1,0:T(2,128)S(1)} %get-tuple-element.51), channel_id=1, source_target_pairs={{0,16},{16,32},{32,48},{48,64},{64,80},{80,96},{96,112},{112,128},... | collective-permute-start | bytes 12296 | tf_op jit(solution)/shard_map/ppermute | solution.py:17
  17.6 1.4 %copy-start.2 = (f32[3,4,256,128]{3,2,1,0:T(8,128)S(1)}, f32[3,4,256,128]{3,2,1,0:T(8,128)}, u32[]{:S(2)}) copy-start(f32[3,4,256,128]{3,2,1,0:T(8,128)} %param.4) | copy-start | bytes 4718596
  20.5 0.8 %copy-start.1 = (f32[4,2,128,128]{3,0,1,2:T(4,128)}, f32[4,2,128,128]{3,0,1,2:T(4,128)S(1)}, u32[]{:S(2)}) copy-start(f32[4,2,128,128]{3,0,1,2:T(4,128)S(1)} %copy.33) | copy-start | bytes 1572868
  47.8 1.0 %copy-start.3 = (f32[128,8,128]{2,1,0:T(8,128)S(1)}, f32[128,8,128]{2,1,0:T(8,128)}, u32[]{:S(2)}) copy-start(f32[128,8,128]{2,1,0:T(8,128)} %get-tuple-element.10) | copy-start | bytes 1572868
  47.8 1.2 %copy-start.4 = (f32[128,8,128]{2,1,0:T(8,128)S(1)}, f32[128,8,128]{2,1,0:T(8,128)}, u32[]{:S(2)}) copy-start(f32[128,8,128]{2,1,0:T(8,128)} %get-tuple-element.8) | copy-start | bytes 1572868
  47.8 1.3 %copy-start.5 = (f32[128,8,128]{2,1,0:T(8,128)S(1)}, f32[128,8,128]{2,1,0:T(8,128)}, u32[]{:S(2)}) copy-start(f32[128,8,128]{2,1,0:T(8,128)} %get-tuple-element.9) | copy-start | bytes 1572868

commit v3 on v2

--- a/solution.py
+++ b/solution.py
@@ -208,7 +208,9 @@
     lanes = stacked.shape[-1]
     stacked = stacked.reshape(8, chunks, planes, lanes).transpose(2, 1, 0, 3)
     stacked = stacked.reshape(planes, chunks * 8, lanes)
-    gathered = lax.all_gather(stacked, "gx", axis=1, tiled=True)
+    copies = jnp.broadcast_to(stacked[None], (device_count,) + stacked.shape)
+    gathered = lax.all_to_all(copies, "gx", 0, 0, tiled=True)
+    gathered = gathered.transpose(1, 0, 2, 3)
     gathered = gathered.reshape(planes, device_count, chunks, 4, 2, lanes)
     gathered_lower_band, gathered_diagonal, gathered_upper_band, gathered_rhs = (
         gathered[:, :, :, k].reshape(planes, 2 * chunks * device_count, lanes) for k in range(4)

time: 50.9 us -> 57 us (1.12)
  blocking collectives: 20 us -> 0 us
  waiting for transfers between devices: 0.01 us -> 17.2 us
  starting transfers between devices: 12.4 us -> 20.1 us
  local copies, waits for them, and re-layouts: 9.45 us -> 10.7 us
    all_gather x1 -> x0, blocking collectives: 20 us -> none  [shards(): gathered = lax.all_gather(stacked, 'gx', axis=1, tiled=True)]
    all_to_all x0 -> x1, waiting for transfers between devices: none -> 17.2 us  [shards(): gathered = lax.all_to_all(copies, 'gx', 0, 0, tiled=True)]
    all_to_all x0 -> x1, starting transfers between devices: none -> 7.62 us  [shards(): gathered = lax.all_to_all(copies, 'gx', 0, 0, tiled=True)]
    broadcast_in_dim x0 -> x1, local copies, waits for them, and re-layouts: none -> 0.85 us  [shards(): copies = jnp.broadcast_to(stacked[None], (device_count,) + stacked.shape)]
  transfers between devices with their start and end apart: 4 -> 5, of which waited for: 0 -> 1; matrix products, arithmetic and copies ran while one was open for 8% -> 7% of each run, Pallas kernels for 0% -> 0%
where the time goes in v3:
time: 57 us; the launch traced here: 56.5 us
  starting transfers between devices  20.1 us (35%)
  waiting for transfers between devices  17.2 us (30%)
  local copies, waits for them, and re-layouts  10.7 us (19%)
  Pallas kernels  4.02 us (7%)
  other arithmetic  3.94 us (7%)
    all_to_all x1, waiting for transfers between devices, shards(): gathered = lax.all_to_all(copies, 'gx', 0, 0, tiled=True)  17.2 us
    ppermute x2, starting transfers between devices, padded_2(): lax.ppermute(head, axis, [((i + 1) % count, i) for i in range(ends)])  8.41 us
    all_to_all x1, starting transfers between devices, shards(): gathered = lax.all_to_all(copies, 'gx', 0, 0, tiled=True)  7.62 us
    ppermute x2, starting transfers between devices, padded_2(): lax.ppermute(tail, axis, [(i, (i + 1) % count) for i in range(ends)])  4.03 us
    pallas_call x1, Pallas kernels, local_solve(): pl.pallas_call(thomas_kernel, out_shape=(shape, shape, shape), scratch_sh...  4.02 us
    unnamed x14, local copies, waits for them, and re-layouts  3.18 us
    transpose x1, local copies, waits for them, and re-layouts, to_chunks(): values.transpose(2, 1, 0, 3)  2.18 us
    slice x2, local copies, waits for them, and re-layouts, padded_2(): head = lax.slice_in_dim(cells, 0, width, axis=dim)  1.87 us
  transfers between devices with their start and end apart: 5, of which 1 were waited for; matrix products, arithmetic and copies ran while one was open for 7% of the time, Pallas kernels for 0%

profile of v3, /device:TPU:1, one launch (start us, length us, event | category | flops | bytes accessed | tf_op | source)
XLA Modules:
  0.0 56.5 jit_solution(5358914911447352143)
XLA Ops:
  0.0 1.1 %fusion.29 = (f32[2,256,128]{2,1,0:T(8,128)S(1)}, f32[2,256,128]{2,1,0:T(8,128)S(1)}) fusion(f32[4,256,128]{2,1,0:T(8,128)} %param.3), kind=kLoop, calls=%fused_computation.98 | loop fusion | bytes 1048576 | tf_op jit(solution)/shard_map/slice | solution.py:13
  1.1 2.1 %collective-permute-start.3 = (f32[2,256,128]{2,1,0:T(8,128)S(1)}, f32[2,256,128]{2,1,0:T(8,128)S(1)}, u32[]{:S(2)}, u32[]{:S(2)}) collective-permute-start(f32[2,256,128]{2,1,0:T(8,128)S(1)} %get-tuple-element.44), channel_id=1, source_target_pairs={{0,1},{1,2},{2,3},{3,4},{4,5},{5,6},{6,7},{7,8},{8,9},{9,10},{10,1... | collective-permute-start | bytes 786440 | tf_op jit(solution)/shard_map/ppermute | solution.py:17
  3.2 3.8 %collective-permute-start.2 = (f32[2,256,128]{2,1,0:T(8,128)S(1)}, f32[2,256,128]{2,1,0:T(8,128)S(1)}, u32[]{:S(2)}, u32[]{:S(2)}) collective-permute-start(f32[2,256,128]{2,1,0:T(8,128)S(1)} %get-tuple-element.43), channel_id=1, source_target_pairs={{1,0},{2,1},{3,2},{4,3},{5,4},{6,5},{7,6},{8,7},{9,8},{10,9},{11,1... | collective-permute-start | bytes 786440 | tf_op jit(solution)/shard_map/ppermute | solution.py:19
  7.0 0.7 %fusion.31 = (f32[4,2,128]{2,1,0:T(2,128)S(1)}, f32[4,2,128]{2,1,0:T(2,128)S(1)}) fusion(f32[4,256,128]{2,1,0:T(8,128)} %param.3), kind=kLoop, calls=%fused_computation.100 | loop fusion | bytes 16384 | tf_op jit(solution)/shard_map/slice | solution.py:13
  7.8 4.6 %collective-permute-start = (f32[4,2,128]{2,1,0:T(2,128)S(1)}, f32[4,2,128]{2,1,0:T(2,128)S(1)}, u32[]{:S(2)}, u32[]{:S(2)}) collective-permute-start(f32[4,2,128]{2,1,0:T(2,128)S(1)} %get-tuple-element.50), channel_id=1, source_target_pairs={{16,0},{32,16},{48,32},{64,48},{80,64},{96,80},{112,96},{128,112},... | collective-permute-start | bytes 12296 | tf_op jit(solution)/shard_map/ppermute | solution.py:19
  12.4 1.9 %collective-permute-start.1 = (f32[4,2,128]{2,1,0:T(2,128)S(1)}, f32[4,2,128]{2,1,0:T(2,128)S(1)}, u32[]{:S(2)}, u32[]{:S(2)}) collective-permute-start(f32[4,2,128]{2,1,0:T(2,128)S(1)} %get-tuple-element.51), channel_id=1, source_target_pairs={{0,16},{16,32},{32,48},{48,64},{64,80},{80,96},{96,112},{112,128},... | collective-permute-start | bytes 12296 | tf_op jit(solution)/shard_map/ppermute | solution.py:17
  14.3 2.2 %copy.36 = f32[128,2,4,128]{3,2,1,0:T(4,128)} copy(f32[128,2,4,128]{3,0,1,2:T(8,128)} %bitcast.65) | data formatting | bytes 1048576 | tf_op jit(solution)/shard_map/transpose | solution.py:112
  16.5 0.9 %negate_multiply_fusion = (f32[1,2,4,128]{3,0,1,2:T(1,128)S(1)}, f32[1,2,4,128]{3,0,1,2:T(1,128)S(1)}, f32[1,2,4,128]{3,0,1,2:T(1,128)S(1)}, f32[1,2,4,128]{3,0,1,2:T(1,128)S(1)}) fusion(f32[2,4]{0,1:T(4,128)S(1)} %get-tuple-element.106, f32[128,2,4,128]{3,0,1,2:T(8,128)} %bitcast.66, f32[2,4]{0,1:T(4,128)S(1)} %get-tuple-element.105), kind=kLoop, calls=%fused_computation.83 | loop fusion | flops 4096 | bytes 24640 | tf_op jit(solution)/shard_map/mul | solution.py:203
  17.4 0.2 fusion.30
  17.7 0.1 constant_dynamic-update-slice_fusion.3
  17.8 1.2 %copy-done.2 = f32[3,4,256,128]{3,2,1,0:T(8,128)S(1)} copy-done((f32[3,4,256,128]{3,2,1,0:T(8,128)S(1)}, f32[3,4,256,128]{3,2,1,0:T(8,128)}, u32[]{:S(2)}) %copy-start.2) | copy-done | bytes 1572888
  19.0 1.1 %fusion.10 = f32[4,256,128]{2,1,0:T(8,128)S(1)} fusion(f32[4,256,128]{2,1,0:T(8,128)S(1)} %copy-done, f32[4,2,128]{2,1,0:T(2,128)S(1)} %collective-permute-done.1, f32[4,258,128]{2,1,0:T(8,128)S(1)} %constant_dynamic-update-slice_fusion, f32[4,256,2]{2,1,0:T(8,128)S(1)} %get-tuple-element.49, f32[4,256,2]{2,1,0:T(8,128)S(1)} %get-tuple-element.48, ...), kind=kLoop, calls=%fused_computation.16 | loop fusion | flops 6029312 | bytes 5787648 | tf_op jit(solution)/shard_map/add | solution.py:44
  20.2 0.3 copy.55
  20.5 0.8 %copy-done.1 = f32[4,2,128,128]{3,0,1,2:T(4,128)} copy-done((f32[4,2,128,128]{3,0,1,2:T(4,128)}, f32[4,2,128,128]{3,0,1,2:T(4,128)S(1)}, u32[]{:S(2)}) %copy-start.1) | copy-done | bytes 524312
  21.3 4.0 %shard_map.37 = (f32[128,8,128]{2,1,0:T(8,128)}, f32[128,8,128]{2,1,0:T(8,128)}, f32[128,8,128]{2,1,0:T(8,128)}) custom-call(f32[128,8,128]{2,1,0:T(8,128)} %bitcast.62, f32[128,8,128]{2,1,0:T(8,128)} %bitcast.56), custom_call_target="tpu_custom_call" | custom-call | tf_op jit(solution)/shard_map/pallas_call | solution.py:172
  25.3 0.7 %multiply_subtract_fusion.1 = (f32[1,8,128]{2,1,0:T(8,128)S(1)}, f32[1,8,128]{2,1,0:T(8,128)S(1)}, f32[1,8,128]{2,1,0:T(8,128)S(1)}, f32[1,8,128]{2,1,0:T(8,128)...) fusion(f32[1,8,128]{2,1,0:T(8,128)S(1)} %bitcast.71, f32[128,8,128]{2,1,0:T(8,128)} %get-tuple-element.8, ...), kind=kLoop, calls=%fused_computation.86 | loop fusion | flops 16384 | bytes 65536 | tf_op jit(solution)/shard_map/sub | solution.py:198
  26.2 0.8 %broadcast_in_dim.54 = f32[16,4,16,128]{3,2,1,0:T(8,128)} broadcast(f32[4,16,128]{2,1,0:T(8,128)S(1)} %bitcast.67), dimensions={1,2,3} | broadcast | bytes 557056 | tf_op jit(solution)/shard_map/broadcast_in_dim | solution.py:211
  27.0 7.6 %all-to-all-start = ((f32[16,4,16,128]{3,2,1,0:T(8,128)}), f32[16,4,16,128]{3,2,1,0:T(8,128)S(1)}, u32[]{:S(2)}, u32[]{:S(2)}) async-start(f32[16,4,16,128]{3,2,1,0:T(8,128)} %broadcast_in_dim.54), calls=%async_computation | async-start | bytes 1048576 | tf_op jit(solution)/shard_map/all_to_all | solution.py:212
  34.7 17.2 %all-to-all-done = f32[16,4,16,128]{3,2,1,0:T(8,128)S(1)} async-done(((f32[16,4,16,128]{3,2,1,0:T(8,128)}), f32[16,4,16,128]{3,2,1,0:T(8,128)S(1)}, u32[]{:S(2)}, u32[]{:S(2)}) %all-to-all-start) | async-done | bytes 524320 | tf_op jit(solution)/shard_map/all_to_all | solution.py:212
  51.9 0.3 copy.45
  52.6 0.1 multiply_add_fusion.8
  52.8 0.1 multiply_add_fusion.7
  53.0 0.1 multiply_add_fusion.6
  53.1 0.1 multiply_add_fusion.5
  53.3 0.1 multiply_add_fusion.4
  53.5 0.1 multiply_add_fusion.3
  53.7 0.1 multiply_add_fusion.1
  54.1 0.8 %copy-done.3 = f32[128,8,128]{2,1,0:T(8,128)S(1)} copy-done((f32[128,8,128]{2,1,0:T(8,128)S(1)}, f32[128,8,128]{2,1,0:T(8,128)}, u32[]{:S(2)}) %copy-start.3) | copy-done | bytes 524312
  54.9 0.2 copy-done.4
  55.1 0.2 copy-done.5
  55.2 0.3 select_select_fusion
  55.6 0.9 %copy.52 = f32[4,2,128,128]{3,2,1,0:T(8,128)} copy(f32[4,2,128,128]{3,0,1,2:T(4,128)S(1)} %bitcast.64) | data formatting | bytes 1048576 | tf_op jit(solution)/shard_map/transpose | solution.py:118
  (61 shorter events, 1.1 us)
Async XLA Ops:
  0.0 17.4 %copy-start = (f32[4,256,128]{2,1,0:T(8,128)S(1)}, f32[4,256,128]{2,1,0:T(8,128)}, u32[]{:S(2)}) copy-start(f32[4,256,128]{2,1,0:T(8,128)} %param.3) | copy-start | bytes 1572868
  1.1 16.5 %collective-permute-start.3 = (f32[2,256,128]{2,1,0:T(8,128)S(1)}, f32[2,256,128]{2,1,0:T(8,128)S(1)}, u32[]{:S(2)}, u32[]{:S(2)}) collective-permute-start(f32[2,256,128]{2,1,0:T(8,128)S(1)} %get-tuple-element.44), channel_id=1, source_target_pairs={{0,1},{1,2},{2,3},{3,4},{4,5},{5,6},{6,7},{7,8},{8,9},{9,10},{10,1... | collective-permute-start | bytes 786440 | tf_op jit(solution)/shard_map/ppermute | solution.py:17
  3.2 14.5 %collective-permute-start.2 = (f32[2,256,128]{2,1,0:T(8,128)S(1)}, f32[2,256,128]{2,1,0:T(8,128)S(1)}, u32[]{:S(2)}, u32[]{:S(2)}) collective-permute-start(f32[2,256,128]{2,1,0:T(8,128)S(1)} %get-tuple-element.43), channel_id=1, source_target_pairs={{1,0},{2,1},{3,2},{4,3},{5,4},{6,5},{7,6},{8,7},{9,8},{10,9},{11,1... | collective-permute-start | bytes 786440 | tf_op jit(solution)/shard_map/ppermute | solution.py:19
  7.8 10.0 %collective-permute-start = (f32[4,2,128]{2,1,0:T(2,128)S(1)}, f32[4,2,128]{2,1,0:T(2,128)S(1)}, u32[]{:S(2)}, u32[]{:S(2)}) collective-permute-start(f32[4,2,128]{2,1,0:T(2,128)S(1)} %get-tuple-element.50), channel_id=1, source_target_pairs={{16,0},{32,16},{48,32},{64,48},{80,64},{96,80},{112,96},{128,112},... | collective-permute-start | bytes 12296 | tf_op jit(solution)/shard_map/ppermute | solution.py:19
  12.4 5.4 %collective-permute-start.1 = (f32[4,2,128]{2,1,0:T(2,128)S(1)}, f32[4,2,128]{2,1,0:T(2,128)S(1)}, u32[]{:S(2)}, u32[]{:S(2)}) collective-permute-start(f32[4,2,128]{2,1,0:T(2,128)S(1)} %get-tuple-element.51), channel_id=1, source_target_pairs={{0,16},{16,32},{32,48},{48,64},{64,80},{80,96},{96,112},{112,128},... | collective-permute-start | bytes 12296 | tf_op jit(solution)/shard_map/ppermute | solution.py:17
  17.6 1.4 %copy-start.2 = (f32[3,4,256,128]{3,2,1,0:T(8,128)S(1)}, f32[3,4,256,128]{3,2,1,0:T(8,128)}, u32[]{:S(2)}) copy-start(f32[3,4,256,128]{3,2,1,0:T(8,128)} %param.4) | copy-start | bytes 4718596
  20.5 0.8 %copy-start.1 = (f32[4,2,128,128]{3,0,1,2:T(4,128)}, f32[4,2,128,128]{3,0,1,2:T(4,128)S(1)}, u32[]{:S(2)}) copy-start(f32[4,2,128,128]{3,0,1,2:T(4,128)S(1)} %copy.55) | copy-start | bytes 1572868
  27.0 24.8 %all-to-all-start = ((f32[16,4,16,128]{3,2,1,0:T(8,128)}), f32[16,4,16,128]{3,2,1,0:T(8,128)S(1)}, u32[]{:S(2)}, u32[]{:S(2)}) async-start(f32[16,4,16,128]{3,2,1,0:T(8,128)} %broadcast_in_dim.54), calls=%async_computation | async-start | bytes 1048576 | tf_op jit(solution)/shard_map/all_to_all | solution.py:212
  53.9 1.0 %copy-start.3 = (f32[128,8,128]{2,1,0:T(8,128)S(1)}, f32[128,8,128]{2,1,0:T(8,128)}, u32[]{:S(2)}) copy-start(f32[128,8,128]{2,1,0:T(8,128)} %get-tuple-element.10) | copy-start | bytes 1572868
  53.9 1.2 %copy-start.4 = (f32[128,8,128]{2,1,0:T(8,128)S(1)}, f32[128,8,128]{2,1,0:T(8,128)}, u32[]{:S(2)}) copy-start(f32[128,8,128]{2,1,0:T(8,128)} %get-tuple-element.8) | copy-start | bytes 1572868
  53.9 1.3 %copy-start.5 = (f32[128,8,128]{2,1,0:T(8,128)S(1)}, f32[128,8,128]{2,1,0:T(8,128)}, u32[]{:S(2)}) copy-start(f32[128,8,128]{2,1,0:T(8,128)} %get-tuple-element.9) | copy-start | bytes 1572868

commit v4 on v2

--- a/solution.py
+++ b/solution.py
@@ -179,11 +179,11 @@
 def shards(field, courant, diffusion_number):
     chunks = 2
     y_padded = padded_2(field, (("gy", 0),), 2, True)
-    x_padded = padded_2(field, (("gx", 1),), 2, False)
+    x_padded = jnp.pad(field, ((0, 0), (2, 2), (0, 0)))
     rhs = build_rhs(field, courant, y_padded, x_padded)
     place = lax.axis_index("gx")
     device_count = lax.axis_size("gx")
-    planes = field.shape[0]
+    planes, length, lanes = field.shape
     rate = to_chunks(diffusion_number, chunks)
     right = to_chunks(rhs, chunks)
     part, first, last = local_solve(rate, right)
@@ -205,22 +205,68 @@
     stacked = jnp.stack(
         [sub_first, sub_last, diag_first, diag_last, super_first, super_last, right_first, right_last]
     )
-    lanes = stacked.shape[-1]
     stacked = stacked.reshape(8, chunks, planes, lanes).transpose(2, 1, 0, 3)
     stacked = stacked.reshape(planes, chunks * 8, lanes)
-    gathered = lax.all_gather(stacked, "gx", axis=1, tiled=True)
-    gathered = gathered.reshape(planes, device_count, chunks, 4, 2, lanes)
+    speed = courant[0]
+    lead_scale = speed[:, 1] / diffusion_number[:, 1]
+    tail_scale = speed[:, length - 2] / diffusion_number[:, length - 2]
+    lead_first = first[1, :planes] * rate_first[:planes]
+    lead_last = first[rows - 2, :planes] * rate_last[:planes]
+    tail_first = last[1, planes:] * rate_first[planes:]
+    tail_last = last[rows - 2, planes:] * rate_last[planes:]
+    extras = jnp.stack(
+        [
+            (8.0 * speed[:, 0] - lead_first * lead_scale) / 12.0,
+            -speed[:, 0] / 12.0,
+            -lead_last * lead_scale / 12.0,
+            tail_first * tail_scale / 12.0,
+            (tail_last * tail_scale - 8.0 * speed[:, length - 1]) / 12.0,
+            speed[:, length - 1] / 12.0,
+            field[:, 0],
+            field[:, 1],
+            field[:, length - 2],
+            field[:, length - 1],
+        ],
+        1,
+    )
+    width = stacked.shape[1] + extras.shape[1]
+    gathered = lax.all_gather(jnp.concatenate([stacked, extras], 1), "gx", axis=1, tiled=True)
+    gathered = gathered.reshape(planes, device_count, width, lanes)
+    extras = gathered[:, :, chunks * 8 :]
+    gathered = gathered[:, :, : chunks * 8].reshape(planes, device_count, chunks, 4, 2, lanes)
+    edge = jnp.zeros((planes, 1, lanes), jnp.float32)
+    left_1 = jnp.concatenate([edge, extras[:, :-1, 9]], 1)
+    left_2 = jnp.concatenate([edge, extras[:, :-1, 8]], 1)
+    right_1 = jnp.concatenate([extras[:, 1:, 6], edge], 1)
+    right_2 = jnp.concatenate([extras[:, 1:, 7], edge], 1)
+    correction = jnp.stack(
+        [
+            extras[:, :, 0] * left_1 + extras[:, :, 1] * left_2,
+            extras[:, :, 2] * left_1,
+            extras[:, :, 3] * right_1,
+            extras[:, :, 4] * right_1 + extras[:, :, 5] * right_2,
+        ],
+        2,
+    ).reshape(planes, device_count, chunks, 2, lanes)
     gathered_lower_band, gathered_diagonal, gathered_upper_band, gathered_rhs = (
         gathered[:, :, :, k].reshape(planes, 2 * chunks * device_count, lanes) for k in range(4)
     )
+    gathered_rhs = (gathered[:, :, :, 3] + correction).reshape(planes, 2 * chunks * device_count, lanes)
     boundary_rows_gathered = parallel_cyclic_reduction(
         gathered_lower_band, gathered_diagonal, gathered_upper_band, (gathered_rhs,), 1
     )[0]
     ends = lax.dynamic_slice_in_dim(boundary_rows_gathered, 2 * chunks * place, 2 * chunks, 1)
     ends = ends.reshape(planes, chunks, 2, lanes).transpose(2, 1, 0, 3)
     ends = ends.reshape(2, chunks * planes, lanes)
+    own_left = lax.dynamic_slice_in_dim(left_1, place, 1, 1)[:, 0]
+    own_right = lax.dynamic_slice_in_dim(right_1, place, 1, 1)[:, 0]
+    lead_shift = -lead_scale * own_left / 12.0
+    tail_shift = tail_scale * own_right / 12.0
+    zero = jnp.zeros_like(lead_shift)
+    lead_shift = jnp.concatenate([lead_shift, zero], 0)
+    tail_shift = jnp.concatenate([zero, tail_shift], 0)
     start_value, end_value = ends[0], ends[1]
-    solved = part + first * start_value[None] + last * end_value[None]
+    solved = part + first * (start_value + lead_shift)[None] + last * (end_value + tail_shift)[None]
     row = lax.broadcasted_iota(jnp.int32, (rows, 1, 1), 0)
     solved = jnp.where(row == 0, start_value[None], solved)
     solved = jnp.where(row == rows - 1, end_value[None], solved)

time: 50.9 us -> 60 us (1.18)
  waiting for transfers between devices: 0.01 us -> 7.07 us
  starting transfers between devices: 12.4 us -> 5.75 us
  other arithmetic: 3.93 us -> 8.68 us
  blocking collectives: 20 us -> 24 us
    ppermute x2 -> x1, waiting for transfers between devices: 0.01 us -> 5.24 us  [padded_2(): lax.ppermute(tail, axis, [(i, (i + 1) % count) for i in range(ends)])]
    ppermute x2 -> x1, starting transfers between devices: 4.03 us -> 0.01 us  [padded_2(): lax.ppermute(tail, axis, [(i, (i + 1) % count) for i in range(ends)])]
    all_gather x1, blocking collectives: 20 us -> 24 us  [shards(): lax.all_gather(jnp.concatenate([stacked, extras], 1), 'gx', axis=1, tiled...]
    add x1, other arithmetic: 1.14 us -> 4.32 us  [build_rhs(): field - transport + 0.05 * (curve_y + curve_z)]
    ppermute x2 -> x1, starting transfers between devices: 8.41 us -> 5.75 us  [padded_2(): lax.ppermute(head, axis, [((i + 1) % count, i) for i in range(ends)])]
    transpose x1, local copies, waits for them, and re-layouts: 2.18 us -> 0.01 us  [shards(): stacked = stacked.reshape(8, chunks, planes, lanes).transpose(2, 1, 0, 3)]
    ppermute x2 -> x1, waiting for transfers between devices: 0.01 us -> 1.83 us  [padded_2(): lax.ppermute(head, axis, [((i + 1) % count, i) for i in range(ends)])]
    div x0 -> x3, other arithmetic: none -> 1.48 us  [the longest x1 0.75 us: shards(): speed[:, length - 1] / 12.0]
  transfers between devices with their start and end apart: 4 -> 2, of which waited for: 0 -> 2; matrix products, arithmetic and copies ran while one was open for 8% -> 6% of each run, Pallas kernels for 0% -> 0%
where the time goes in v4:
time: 60 us; the launch traced here: 59.6 us
  blocking collectives  24 us (40%)
  local copies, waits for them, and re-layouts  9.54 us (16%)
  other arithmetic  8.68 us (14%)
  waiting for transfers between devices  7.07 us (12%)
  starting transfers between devices  5.75 us (10%)
  Pallas kernels  4.04 us (7%)
    all_gather x1, blocking collectives, shards(): lax.all_gather(jnp.concatenate([stacked, extras], 1), 'gx', axis=1, tiled...  24 us
    ppermute x1, starting transfers between devices, padded_2(): lax.ppermute(head, axis, [((i + 1) % count, i) for i in range(ends)])  5.75 us
    ppermute x1, waiting for transfers between devices, padded_2(): lax.ppermute(tail, axis, [(i, (i + 1) % count) for i in range(ends)])  5.24 us
    add x1, other arithmetic, build_rhs(): field - transport + 0.05 * (curve_y + curve_z)  4.32 us
    pallas_call x1, Pallas kernels, local_solve(): pl.pallas_call(thomas_kernel, out_shape=(shape, shape, shape), scratch_sh...  4.04 us
    unnamed x23, local copies, waits for them, and re-layouts  3.9 us
    ppermute x1, waiting for transfers between devices, padded_2(): lax.ppermute(head, axis, [((i + 1) % count, i) for i in range(ends)])  1.83 us
    slice x1, local copies, waits for them, and re-layouts, build_rhs(): transport = courant[0] * grad_x + courant[1] * grad_y + courant[2] * grad_z  1.52 us
  transfers between devices with their start and end apart: 2, of which 2 were waited for; matrix products, arithmetic and copies ran while one was open for 6% of the time, Pallas kernels for 0%

profile of v4, /device:TPU:1, one launch (start us, length us, event | category | flops | bytes accessed | tf_op | source)
XLA Modules:
  0.0 59.6 jit_solution(4229732995306605927)
XLA Ops:
  0.0 1.4 %copy.91 = f32[4,256,128]{2,0,1:T(4,128)S(1)} copy(f32[4,256,128]{2,1,0:T(8,128)} %param.3) | data formatting | bytes 1048576 | tf_op args[0]
  1.4 1.0 %fusion.59 = (f32[2,256,128]{2,0,1:T(2,128)}, f32[2,256,128]{2,0,1:T(2,128)}) fusion(f32[4,256,128]{2,0,1:T(4,128)S(1)} %copy.91), kind=kLoop, calls=%fused_computation.161 | loop fusion | bytes 1048576 | tf_op jit(solution)/shard_map/slice | solution.py:14
  2.4 5.7 %collective-permute-start = (f32[2,256,128]{2,0,1:T(2,128)}, f32[2,256,128]{2,0,1:T(2,128)S(1)}, u32[]{:S(2)}, u32[]{:S(2)}) collective-permute-start(f32[2,256,128]{2,0,1:T(2,128)} %get-tuple-element.74), channel_id=1, source_target_pairs={{1,0},{2,1},{3,2},{4,3},{5,4},{6,5},{7,6},{8,7},{9,8},{10,9},{11,1... | collective-permute-start | bytes 786440 | tf_op jit(solution)/shard_map/ppermute | solution.py:19
  8.1 0.7 %fusion.55 = (f32[4,2,128]{2,1,0:T(2,128)S(1)}, f32[4,2,128]{2,1,0:T(2,128)S(1)}) fusion(f32[4,256,128]{2,1,0:T(8,128)} %param.3), kind=kLoop, calls=%fused_computation.157 | loop fusion | bytes 16384 | tf_op jit(solution)/shard_map/slice | solution.py:227
  8.9 1.5 %fusion.53 = (f32[1,4,256,128]{3,2,1,0:T(8,128)S(1)}, f32[1,4,256,128]{3,2,1,0:T(8,128)S(1)}, f32[1,4,256,128]{3,2,1,0:T(8,128)S(1)}) fusion(f32[3,4,256,128]{3,2,1,0:T(8,128)} %param.4), kind=kLoop, calls=%fused_computation.155 | loop fusion | bytes 3145728 | tf_op jit(solution)/shard_map/slice | solution.py:43
  10.5 0.3 copy.173
  10.8 0.3 copy.170
  11.3 0.3 fusion.60
  11.6 1.8 %collective-permute-done = f32[2,256,128]{2,0,1:T(2,128)S(1)} collective-permute-done((f32[2,256,128]{2,0,1:T(2,128)}, f32[2,256,128]{2,0,1:T(2,128)S(1)}, u32[]{:S(2)}, u32[]{:S(2)}) %collective-permute-start) | collective-permute-done | bytes 262176 | tf_op jit(solution)/shard_map/ppermute | solution.py:19
  13.4 5.2 %collective-permute-done.1 = f32[2,256,128]{2,0,1:T(2,128)} collective-permute-done((f32[2,256,128]{2,0,1:T(2,128)}, f32[2,256,128]{2,0,1:T(2,128)}, u32[]{:S(2)}, u32[]{:S(2)}) %collective-permute-start.1) | collective-permute-done | bytes 262176 | tf_op jit(solution)/shard_map/ppermute | solution.py:17
  18.7 4.3 %fusion.8 = f32[4,256,128]{2,0,1:T(4,128)S(1)} fusion(f32[4,256,128]{2,0,1:T(4,128)S(1)} %copy.91, f32[1,4,256,128]{3,2,1,0:T(8,128)S(1)} %get-tuple-element.29, f32[1,4,256,128]{3,2,1,0:T(8,128)S(1)} %get-tuple-element.28, f32[4,256,2]{2,0,1:T(4,128)S(1)} %get-tuple-element.76, f32[4,256,2]{2,0,1:T(4,128)S(1)} %get-tuple-element.75, ...), kind=kLoop, calls=%fused_computation.21 | loop fusion | flops 6291456 | bytes 3162112 | tf_op jit(solution)/shard_map/add | solution.py:44
  23.0 0.1 copy.172
  23.1 0.8 %copy-done.1 = f32[4,2,128,128]{3,0,1,2:T(4,128)} copy-done((f32[4,2,128,128]{3,0,1,2:T(4,128)}, f32[4,2,128,128]{3,0,1,2:T(4,128)S(1)}, u32[]{:S(2)}) %copy-start.1) | copy-done | bytes 524312
  23.9 4.0 %shard_map.37 = (f32[128,8,128]{2,1,0:T(8,128)}, f32[128,8,128]{2,1,0:T(8,128)}, f32[128,8,128]{2,1,0:T(8,128)}) custom-call(f32[128,8,128]{2,1,0:T(8,128)} %bitcast.211, f32[128,8,128]{2,1,0:T(8,128)} %bitcast.216), custom_call_target="tpu_custom_call" | custom-call | tf_op jit(solution)/shard_map/pallas_call | solution.py:172
  27.9 0.7 %multiply_subtract_fusion.1 = (f32[1,8,128]{2,1,0:T(8,128)S(1)}, f32[1,8,128]{2,1,0:T(8,128)S(1)}, f32[1,8,128]{2,1,0:T(8,128)S(1)}, f32[1,8,128]{2,1,0:T(8,128)...) fusion(f32[1,8,128]{2,1,0:T(8,128)S(1)} %bitcast.243, f32[128,8,128]{2,1,0:T(8,128)} %get-tuple-element.8, ...), kind=kLoop, calls=%fused_computation.120 | loop fusion | flops 16384 | bytes 65536 | tf_op jit(solution)/shard_map/sub | solution.py:198
  28.7 0.8 %constant_dynamic-update-slice_fusion.2 = f32[8,2,4,128]{3,2,1,0:T(4,128)S(1)} fusion(f32[8,2,4,128]{3,2,1,0:T(4,128)S(1)} %constant_dynamic-update-slice_fusion.3, f32[2,4]{1,0:T(2,128)S(1)} %compare_select_fusion, f32[128,2,4,128]{3,2,1,0:T(4,128)} %bitcast.212), kind=kLoop, calls=%fused_computation.95 | loop fusion | flops 2048 | bytes 9216
  29.5 0.8 %slice_multiply_fusion.2 = (f32[4,1,128]{2,0,1:T(4,128)S(1)}, f32[4,1,128]{2,0,1:T(4,128)S(1)}, f32[4,1,128]{2,0,1:T(4,128)S(1)}, f32[4,1,128]{2,0,1:T(4,128)S(1...) fusion(f32[4,256,128]{2,0,1:T(4,128)S(1)} %bitcast.222, f32[4,1,128]{2,0,1:T(4,128)S(1)} %bitcast.247, ...), kind=kLoop, calls=%fused_computation.150 | loop fusion | flops 8704 | bytes 36864 | tf_op jit(solution)/shard_map/div | solution.py:224
  30.2 0.7 %fusion.52 = f32[4,1,128]{2,0,1:T(4,128)S(1)} fusion(f32[4,1,128]{2,0,1:T(4,128)S(1)} %get-tuple-element.53, f32[128,2,4,128]{3,2,1,0:T(4,128)} %bitcast.214, f32[128,8,128]{2,1,0:T(8,128)} %get-tuple-element.8, f32[4,256,128]{2,0,1:T(4,128)S(1)} %bitcast.223), kind=kLoop, calls=%fused_computation.144 | loop fusion | flops 2560 | bytes 10240 | tf_op jit(solution)/shard_map/div | solution.py:219
  31.0 24.0 %all_gather.3 = f32[4,416,128]{2,0,1:T(4,128)S(1)} all-gather(f32[4,26,128]{2,0,1:T(4,128)S(1)} %copy.106), channel_id=1, replica_groups=mesh['gx'=16,'gy'=16] {'gx'}, dimensions={1}, use_global_device_ids=true | all-gather | bytes 905216 | tf_op jit(solution)/shard_map/all_gather | solution.py:233
  55.2 0.1 copy.118
  55.8 0.1 multiply_add_fusion.8
  55.9 0.1 multiply_add_fusion.7
  56.1 0.1 multiply_add_fusion.6
  56.3 0.1 multiply_add_fusion.5
  56.5 0.1 multiply_add_fusion.4
  56.6 0.1 multiply_add_fusion.3
  56.9 0.1 multiply_add_fusion.1
  57.3 0.7 %copy-done.2 = f32[128,8,128]{2,1,0:T(8,128)S(1)} copy-done((f32[128,8,128]{2,1,0:T(8,128)S(1)}, f32[128,8,128]{2,1,0:T(8,128)}, u32[]{:S(2)}) %copy-start.2) | copy-done | bytes 524312
  58.0 0.2 copy-done.3
  58.2 0.2 copy-done.4
  58.4 0.3 select_select_fusion
  58.7 0.9 %copy.124 = f32[4,2,128,128]{3,2,1,0:T(8,128)} copy(f32[4,2,128,128]{3,0,1,2:T(4,128)S(1)} %bitcast.220) | data formatting | bytes 1048576 | tf_op jit(solution)/shard_map/transpose | solution.py:118
  (66 shorter events, 1.3 us)
Async XLA Ops:
  2.4 11.1 %collective-permute-start = (f32[2,256,128]{2,0,1:T(2,128)}, f32[2,256,128]{2,0,1:T(2,128)S(1)}, u32[]{:S(2)}, u32[]{:S(2)}) collective-permute-start(f32[2,256,128]{2,0,1:T(2,128)} %get-tuple-element.74), channel_id=1, source_target_pairs={{1,0},{2,1},{3,2},{4,3},{5,4},{6,5},{7,6},{8,7},{9,8},{10,9},{11,1... | collective-permute-start | bytes 786440 | tf_op jit(solution)/shard_map/ppermute | solution.py:19
  8.1 10.5 %collective-permute-start.1 = (f32[2,256,128]{2,0,1:T(2,128)}, f32[2,256,128]{2,0,1:T(2,128)}, u32[]{:S(2)}, u32[]{:S(2)}) collective-permute-start(f32[2,256,128]{2,0,1:T(2,128)} %get-tuple-element.73), channel_id=1, source_target_pairs={{0,1},{1,2},{2,3},{3,4},{4,5},{5,6},{6,7},{7,8},{8,9},{9,10},{10,1... | collective-permute-start | bytes 786440 | tf_op jit(solution)/shard_map/ppermute | solution.py:17
  8.9 1.5 %copy-start.5 = (f32[4,256,128]{2,1,0:T(8,128)S(1)}, f32[4,256,128]{2,1,0:T(8,128)}, u32[]{:S(2)}) copy-start(f32[4,256,128]{2,1,0:T(8,128)} %param.5) | copy-start | bytes 1572868
  10.8 0.8 %copy-start = (f32[4,2,128,128]{3,0,1,2:T(4,128)}, f32[4,2,128,128]{3,0,1,2:T(4,128)S(1)}, u32[]{:S(2)}) copy-start(f32[4,2,128,128]{3,0,1,2:T(4,128)S(1)} %copy.173) | copy-start | bytes 1572868
  23.1 0.8 %copy-start.1 = (f32[4,2,128,128]{3,0,1,2:T(4,128)}, f32[4,2,128,128]{3,0,1,2:T(4,128)S(1)}, u32[]{:S(2)}) copy-start(f32[4,2,128,128]{3,0,1,2:T(4,128)S(1)} %copy.172) | copy-start | bytes 1572868
  57.0 1.0 %copy-start.2 = (f32[128,8,128]{2,1,0:T(8,128)S(1)}, f32[128,8,128]{2,1,0:T(8,128)}, u32[]{:S(2)}) copy-start(f32[128,8,128]{2,1,0:T(8,128)} %get-tuple-element.8) | copy-start | bytes 1572868
  57.0 1.2 %copy-start.3 = (f32[128,8,128]{2,1,0:T(8,128)S(1)}, f32[128,8,128]{2,1,0:T(8,128)}, u32[]{:S(2)}) copy-start(f32[128,8,128]{2,1,0:T(8,128)} %get-tuple-element.9) | copy-start | bytes 1572868
  57.0 1.3 %copy-start.4 = (f32[128,8,128]{2,1,0:T(8,128)S(1)}, f32[128,8,128]{2,1,0:T(8,128)}, u32[]{:S(2)}) copy-start(f32[128,8,128]{2,1,0:T(8,128)} %get-tuple-element.10) | copy-start | bytes 1572868

commit v5 on v2

--- a/solution.py
+++ b/solution.py
@@ -119,74 +119,99 @@
     return values.reshape(planes, chunks * rows, lanes)
 
 
-def thomas_kernel(rate_ref, right_ref, part_ref, first_ref, last_ref, ratio_ref):
+def factor_kernel(rate_ref, ratio_ref, inverse_ref, first_ref, last_ref):
     rows = rate_ref.shape[0]
     zero = jnp.zeros(rate_ref.shape[1:], jnp.float32)
     rate = rate_ref[1]
     inverse = 1.0 / (1.0 + 2.0 * rate)
     ratio = -rate * inverse
-    part = right_ref[1] * inverse
     first = rate * inverse
     ratio_ref[1] = ratio
-    part_ref[1] = part
+    inverse_ref[1] = inverse
     first_ref[1] = first
 
     def forward(i, carry):
-        ratio, part, first, _ = carry
+        ratio, first, _ = carry
         rate = rate_ref[i]
         inverse = 1.0 / ((1.0 + 2.0 * rate) + rate * ratio)
         ratio = -rate * inverse
-        part = (right_ref[i] + rate * part) * inverse
         first = rate * first * inverse
         ratio_ref[i] = ratio
-        part_ref[i] = part
+        inverse_ref[i] = inverse
         first_ref[i] = first
-        return ratio, part, first, inverse
-
-    _, part, first, inverse = lax.fori_loop(
-        2, rows - 1, forward, (ratio, part, first, zero), unroll=8
-    )
+        return ratio, first, inverse
+
+    _, first, inverse = lax.fori_loop(2, rows - 1, forward, (ratio, first, zero), unroll=8)
     last = rate_ref[rows - 2] * inverse
     last_ref[rows - 2] = last
 
     def backward(j, carry):
-        part, first, last = carry
+        first, last = carry
         i = rows - 3 - j
         ratio = ratio_ref[i]
-        part = part_ref[i] - ratio * part
         first = first_ref[i] - ratio * first
         last = -ratio * last
-        part_ref[i] = part
         first_ref[i] = first
         last_ref[i] = last
-        return part, first, last
-
-    lax.fori_loop(0, rows - 3, backward, (part, first, last), unroll=8)
-    for ref in (part_ref, first_ref, last_ref):
+        return first, last
+
+    lax.fori_loop(0, rows - 3, backward, (first, last), unroll=8)
+    for ref in (ratio_ref, inverse_ref, first_ref, last_ref):
         ref[0] = zero
         ref[rows - 1] = zero
 
 
-def local_solve(rate, right):
+def substitute_kernel(rate_ref, ratio_ref, inverse_ref, right_ref, part_ref):
+    rows = rate_ref.shape[0]
+    zero = jnp.zeros(rate_ref.shape[1:], jnp.float32)
+    part = right_ref[1] * inverse_ref[1]
+    part_ref[1] = part
+
+    def forward(i, part):
+        part = (right_ref[i] + rate_ref[i] * part) * inverse_ref[i]
+        part_ref[i] = part
+        return part
+
+    part = lax.fori_loop(2, rows - 1, forward, part, unroll=8)
+
+    def backward(j, part):
+        i = rows - 3 - j
+        part = part_ref[i] - ratio_ref[i] * part
+        part_ref[i] = part
+        return part
+
+    lax.fori_loop(0, rows - 3, backward, part, unroll=8)
+    part_ref[0] = zero
+    part_ref[rows - 1] = zero
+
+
+def local_factor(rate):
     shape = jax.ShapeDtypeStruct(rate.shape, jnp.float32)
-    return pl.pallas_call(
-        thomas_kernel,
-        out_shape=(shape, shape, shape),
-        scratch_shapes=[pltpu.VMEM(rate.shape, jnp.float32)],
-    )(rate, right)
+    return pl.pallas_call(factor_kernel, out_shape=(shape,) * 4)(rate)
+
+
+def local_substitute(rate, ratio, inverse, right):
+    shape = jax.ShapeDtypeStruct(rate.shape, jnp.float32)
+    return pl.pallas_call(substitute_kernel, out_shape=shape)(rate, ratio, inverse, right)
 
 
 def shards(field, courant, diffusion_number):
     chunks = 2
     y_padded = padded_2(field, (("gy", 0),), 2, True)
     x_padded = padded_2(field, (("gx", 1),), 2, False)
-    rhs = build_rhs(field, courant, y_padded, x_padded)
+    flat = jnp.zeros_like(field[:2])
+    own_rhs = build_rhs(field, courant, jnp.concatenate([flat, field, flat], 0), x_padded)
+    own_rhs = lax.optimization_barrier(own_rhs)
+    halo_only = jnp.concatenate([y_padded[:2], jnp.zeros_like(field), y_padded[-2:]], 0)
+    grad_y, curve_y = difference_pair(halo_only, 0, field.shape[0])
+    rhs = own_rhs + (0.05 * curve_y - courant[1] * grad_y)
     place = lax.axis_index("gx")
     device_count = lax.axis_size("gx")
     planes = field.shape[0]
     rate = to_chunks(diffusion_number, chunks)
     right = to_chunks(rhs, chunks)
-    part, first, last = local_solve(rate, right)
+    ratio, inverse, first, last = local_factor(rate)
+    part = local_substitute(rate, ratio, inverse, right)
     rows = rate.shape[0]
     low_open = (place > 0).astype(jnp.float32)
     high_open = (place < device_count - 1).astype(jnp.float32)

time: 50.9 us -> 57.1 us (1.12)
  Pallas kernels: 4.03 us -> 7.1 us
  other arithmetic: 3.93 us -> 6.38 us
  local copies, waits for them, and re-layouts: 9.45 us -> 10.3 us
  starting transfers between devices: 12.4 us -> 11.8 us
    pallas_call x1 -> x2, Pallas kernels: 4.03 us -> 7.1 us  [the longest x1 3.96 us: local_factor(): return pl.pallas_call(factor_kernel, out_shape=(shape,) * 4)(rate)]
    ppermute x2, starting transfers between devices: 4.03 us -> 1.92 us  [padded_2(): lax.ppermute(tail, axis, [(i, (i + 1) % count) for i in range(ends)])]
    slice x0 -> x1, local copies, waits for them, and re-layouts: none -> 1.77 us  [padded_2(): lax.slice_in_dim(cells, cells.shape[dim] - width, cells.shape[dim], axis=...]
    ppermute x2, starting transfers between devices: 8.41 us -> 9.84 us  [padded_2(): lax.ppermute(head, axis, [((i + 1) % count, i) for i in range(ends)])]
    add x0 -> x1, other arithmetic: none -> 1.31 us  [shards(): rhs = own_rhs + (0.05 * curve_y - courant[1] * grad_y)]
    add x1, other arithmetic: 1.14 us -> 2.3 us  [build_rhs(): field - transport + 0.05 * (curve_y + curve_z)]
    slice x2 -> x1, local copies, waits for them, and re-layouts: 1.87 us -> 0.8 us  [padded_2(): head = lax.slice_in_dim(cells, 0, width, axis=dim)]
    slice x1, local copies, waits for them, and re-layouts: 0.2 us -> 0.95 us  [build_rhs(): z_padded = jnp.concatenate([field[:, :, -2:], field, field[:, :, :2]], 2)]
  transfers between devices with their start and end apart: 4 -> 4, of which waited for: 0 -> 0; matrix products, arithmetic and copies ran while one was open for 8% -> 16% of each run, Pallas kernels for 0% -> 7%
where the time goes in v5:
time: 57.1 us; the launch traced here: 56.6 us
  blocking collectives  20.5 us (36%)
  starting transfers between devices  11.8 us (21%)
  local copies, waits for them, and re-layouts  10.3 us (18%)
  Pallas kernels  7.1 us (12%)
  other arithmetic  6.38 us (11%)
    all_gather x1, blocking collectives, shards(): gathered = lax.all_gather(stacked, 'gx', axis=1, tiled=True)  20.5 us
    ppermute x2, starting transfers between devices, padded_2(): lax.ppermute(head, axis, [((i + 1) % count, i) for i in range(ends)])  9.84 us
    pallas_call x1, Pallas kernels, local_factor(): return pl.pallas_call(factor_kernel, out_shape=(shape,) * 4)(rate)  3.96 us
    pallas_call x1, Pallas kernels, local_substitute(): pl.pallas_call(substitute_kernel, out_shape=shape)  3.13 us
    unnamed x13, local copies, waits for them, and re-layouts  2.64 us
    add x1, other arithmetic, build_rhs(): field - transport + 0.05 * (curve_y + curve_z)  2.3 us
    transpose x1, local copies, waits for them, and re-layouts, to_chunks(): values.transpose(2, 1, 0, 3)  2.18 us
    ppermute x2, starting transfers between devices, padded_2(): lax.ppermute(tail, axis, [(i, (i + 1) % count) for i in range(ends)])  1.92 us
  transfers between devices with their start and end apart: 4, of which 0 were waited for; matrix products, arithmetic and copies ran while one was open for 16% of the time, Pallas kernels for 7%

profile of v5, /device:TPU:1, one launch (start us, length us, event | category | flops | bytes accessed | tf_op | source)
XLA Modules:
  0.0 56.6 jit_solution(10737757943623825607)
XLA Ops:
  0.0 0.8 %fusion.35 = (f32[4,2,128]{2,1,0:T(2,128)S(1)}, f32[4,2,128]{2,1,0:T(2,128)S(1)}) fusion(f32[4,256,128]{2,1,0:T(8,128)} %param.3), kind=kLoop, calls=%fused_computation.109 | loop fusion | bytes 16384 | tf_op jit(solution)/shard_map/slice | solution.py:13
  0.8 5.1 %collective-permute-start = (f32[4,2,128]{2,1,0:T(2,128)S(1)}, f32[4,2,128]{2,1,0:T(2,128)S(1)}, u32[]{:S(2)}, u32[]{:S(2)}) collective-permute-start(f32[4,2,128]{2,1,0:T(2,128)S(1)} %get-tuple-element.49), channel_id=1, source_target_pairs={{16,0},{32,16},{48,32},{64,48},{80,64},{96,80},{112,96},{128,112},... | collective-permute-start | bytes 12296 | tf_op jit(solution)/shard_map/ppermute | solution.py:19
  5.9 1.9 %collective-permute-start.1 = (f32[4,2,128]{2,1,0:T(2,128)S(1)}, f32[4,2,128]{2,1,0:T(2,128)S(1)}, u32[]{:S(2)}, u32[]{:S(2)}) collective-permute-start(f32[4,2,128]{2,1,0:T(2,128)S(1)} %get-tuple-element.50), channel_id=1, source_target_pairs={{0,16},{16,32},{32,48},{48,64},{64,80},{80,96},{96,112},{112,128},... | collective-permute-start | bytes 12296 | tf_op jit(solution)/shard_map/ppermute | solution.py:17
  7.8 1.8 %fusion.33 = (f32[2,256,128]{2,1,0:T(8,128)S(1)}, f32[2,256,128]{2,1,0:T(8,128)}) fusion(f32[4,256,128]{2,1,0:T(8,128)} %param.3), kind=kLoop, calls=%fused_computation.107 | loop fusion | bytes 1048576 | tf_op jit(solution)/shard_map/slice | solution.py:14
  9.6 4.7 %collective-permute-start.2 = (f32[2,256,128]{2,1,0:T(8,128)}, f32[2,256,128]{2,1,0:T(8,128)}, u32[]{:S(2)}, u32[]{:S(2)}) collective-permute-start(f32[2,256,128]{2,1,0:T(8,128)} %get-tuple-element.46), channel_id=1, source_target_pairs={{1,0},{2,1},{3,2},{4,3},{5,4},{6,5},{7,6},{8,7},{9,8},{10,9},{11,1... | collective-permute-start | bytes 786440 | tf_op jit(solution)/shard_map/ppermute | solution.py:19
  14.4 1.1 %constant_dynamic-update-slice_fusion.1 = f32[4,258,128]{2,1,0:T(8,128)S(1)} fusion(f32[4,256,128]{2,1,0:T(8,128)} %param.3), kind=kLoop, calls=%fused_computation.87 | loop fusion | bytes 1048576
  15.5 1.0 %fusion.34 = (f32[4,256,2]{2,1,0:T(8,128)S(1)}, f32[4,256,2]{2,1,0:T(8,128)}) fusion(f32[4,256,128]{2,1,0:T(8,128)S(1)} %copy-done), kind=kLoop, calls=%fused_computation.108 | loop fusion | bytes 32768 | tf_op jit(solution)/shard_map/slice | solution.py:39
  16.4 0.9 %negate_multiply_fusion = (f32[1,2,4,128]{3,0,1,2:T(1,128)S(1)}, f32[1,2,4,128]{3,0,1,2:T(1,128)S(1)}, f32[1,2,4,128]{3,0,1,2:T(1,128)S(1)}, f32[1,2,4,128]{3,0,1,2:T(1,128)S(1)}) fusion(f32[2,4]{0,1:T(4,128)S(1)} %get-tuple-element.105, f32[128,2,4,128]{3,0,1,2:T(8,128)} %bitcast.69, f32[2,4]{0,1:T(4,128)S(1)} %get-tuple-element.104), kind=kLoop, calls=%fused_computation.92 | loop fusion | flops 4096 | bytes 24640 | tf_op jit(solution)/shard_map/mul | solution.py:228
  17.3 2.2 %copy.19 = f32[128,2,4,128]{3,2,1,0:T(4,128)} copy(f32[128,2,4,128]{3,0,1,2:T(8,128)} %bitcast.70) | data formatting | bytes 1048576 | tf_op jit(solution)/shard_map/transpose | solution.py:112
  19.5 4.0 %shard_map.37 = (f32[128,8,128]{2,1,0:T(8,128)}, f32[128,8,128]{2,1,0:T(8,128)}, f32[128,8,128]{2,1,0:T(8,128)}, f32[128,8,128]{2,1,0:T(8,128)}) custom-call(f32[128,8,128]{2,1,0:T(8,128)} %bitcast.52), custom_call_target="tpu_custom_call" | custom-call | tf_op jit(solution)/shard_map/pallas_call | solution.py:190
  23.5 2.3 %fusion.10 = f32[4,256,128]{2,1,0:T(8,128)S(1)} fusion(f32[4,256,128]{2,1,0:T(8,128)S(1)} %copy-done, f32[4,2,128]{2,1,0:T(2,128)S(1)} %collective-permute-done.1, f32[4,258,128]{2,1,0:T(8,128)S(1)} %constant_dynamic-update-slice_fusion, f32[4,256,2]{2,1,0:T(8,128)} %get-tuple-element.48, f32[4,256,2]{2,1,0:T(8,128)S(1)} %get-tuple-element.47, ...), kind=kLoop, calls=%fused_computation.24 | loop fusion | flops 6029312 | bytes 3690496 | tf_op jit(solution)/shard_map/add | solution.py:44
  25.8 1.3 %fusion.15 = f32[4,256,128]{2,1,0:T(8,128)S(1)} fusion(f32[4,256,128]{2,1,0:T(8,128)S(1)} %fusion.10, f32[2,256,128]{2,1,0:T(8,128)} %collective-permute-done.2, f32[2,256,128]{2,1,0:T(8,128)} %collective-permute-done.3, f32[3,4,256,128]{3,2,1,0:T(8,128)S(1)} %copy-done.1), kind=kLoop, calls=%fused_computation.35 | loop fusion | flops 1703936 | bytes 2097152 | tf_op jit(solution)/shard_map/add | solution.py:207
  27.1 0.3 copy.33
  27.5 0.8 %copy-done.2 = f32[4,2,128,128]{3,0,1,2:T(4,128)} copy-done((f32[4,2,128,128]{3,0,1,2:T(4,128)}, f32[4,2,128,128]{3,0,1,2:T(4,128)S(1)}, u32[]{:S(2)}) %copy-start.2) | copy-done | bytes 524312
  28.3 3.1 %shard_map.38 = f32[128,8,128]{2,1,0:T(8,128)} custom-call(f32[128,8,128]{2,1,0:T(8,128)} %bitcast.53, f32[128,8,128]{2,1,0:T(8,128)} %get-tuple-element.11.ratio_ref, f32[128,8,128]{2,1,0:T(8,128)} %get-tuple-element.12.inverse_ref, f32[128,8,128]{2,1,0:T(8,128)} %bitcast.61), custom_call_target="tpu_custom_call" | custom-call | tf_op jit(solution)/shard_map/pallas_call | solution.py:195
  31.4 0.7 %multiply_subtract_fusion.1 = (f32[1,8,128]{2,1,0:T(8,128)S(1)}, f32[1,8,128]{2,1,0:T(8,128)S(1)}, f32[1,8,128]{2,1,0:T(8,128)S(1)}, f32[1,8,128]{2,1,0:T(8,128)...) fusion(f32[1,8,128]{2,1,0:T(8,128)S(1)} %bitcast.76, f32[128,8,128]{2,1,0:T(8,128)S(1)} %copy-done.4, ...), kind=kLoop, calls=%fused_computation.95 | loop fusion | flops 16384 | bytes 65536 | tf_op jit(solution)/shard_map/sub | solution.py:223
  32.2 0.1 stack.29
  32.2 20.5 %all_gather.3 = f32[4,256,128]{2,1,0:T(8,128)S(1)} all-gather(f32[4,16,128]{2,1,0:T(8,128)S(1)} %bitcast.71), channel_id=1, replica_groups=mesh['gx'=16,'gy'=16] {'gx'}, dimensions={1}, use_global_device_ids=true | all-gather | bytes 557056 | tf_op jit(solution)/shard_map/all_gather | solution.py:236
  52.7 0.2 fusion.31
  53.1 0.1 multiply_add_fusion.8
  53.2 0.1 multiply_add_fusion.7
  53.4 0.1 multiply_add_fusion.6
  53.6 0.1 multiply_add_fusion.5
  53.8 0.1 multiply_add_fusion.4
  53.9 0.1 multiply_add_fusion.3
  54.1 0.1 multiply_add_fusion.2
  54.2 0.1 multiply_add_fusion.1
  54.3 0.1 multiply_add_fusion
  54.5 0.1 fusion.23
  54.6 0.8 %copy-done.3 = f32[128,8,128]{2,1,0:T(8,128)S(1)} copy-done((f32[128,8,128]{2,1,0:T(8,128)S(1)}, f32[128,8,128]{2,1,0:T(8,128)}, u32[]{:S(2)}) %copy-start.3) | copy-done | bytes 524312
  55.3 0.3 select_select_fusion
  55.7 0.9 %copy.30 = f32[4,2,128,128]{3,2,1,0:T(8,128)} copy(f32[4,2,128,128]{3,0,1,2:T(4,128)S(1)} %bitcast.63) | data formatting | bytes 1048576 | tf_op jit(solution)/shard_map/transpose | solution.py:118
  (54 shorter events, 0.5 us)
Async XLA Ops:
  0.0 15.4 %copy-start = (f32[4,256,128]{2,1,0:T(8,128)S(1)}, f32[4,256,128]{2,1,0:T(8,128)}, u32[]{:S(2)}) copy-start(f32[4,256,128]{2,1,0:T(8,128)} %param.3) | copy-start | bytes 1572868
  0.8 22.6 %collective-permute-start = (f32[4,2,128]{2,1,0:T(2,128)S(1)}, f32[4,2,128]{2,1,0:T(2,128)S(1)}, u32[]{:S(2)}, u32[]{:S(2)}) collective-permute-start(f32[4,2,128]{2,1,0:T(2,128)S(1)} %get-tuple-element.49), channel_id=1, source_target_pairs={{16,0},{32,16},{48,32},{64,48},{80,64},{96,80},{112,96},{128,112},... | collective-permute-start | bytes 12296 | tf_op jit(solution)/shard_map/ppermute | solution.py:19
  5.9 17.5 %collective-permute-start.1 = (f32[4,2,128]{2,1,0:T(2,128)S(1)}, f32[4,2,128]{2,1,0:T(2,128)S(1)}, u32[]{:S(2)}, u32[]{:S(2)}) collective-permute-start(f32[4,2,128]{2,1,0:T(2,128)S(1)} %get-tuple-element.50), channel_id=1, source_target_pairs={{0,16},{16,32},{32,48},{48,64},{64,80},{80,96},{96,112},{112,128},... | collective-permute-start | bytes 12296 | tf_op jit(solution)/shard_map/ppermute | solution.py:17
  9.6 16.2 %collective-permute-start.2 = (f32[2,256,128]{2,1,0:T(8,128)}, f32[2,256,128]{2,1,0:T(8,128)}, u32[]{:S(2)}, u32[]{:S(2)}) collective-permute-start(f32[2,256,128]{2,1,0:T(8,128)} %get-tuple-element.46), channel_id=1, source_target_pairs={{1,0},{2,1},{3,2},{4,3},{5,4},{6,5},{7,6},{8,7},{9,8},{10,9},{11,1... | collective-permute-start | bytes 786440 | tf_op jit(solution)/shard_map/ppermute | solution.py:19
  14.4 11.4 %collective-permute-start.3 = (f32[2,256,128]{2,1,0:T(8,128)S(1)}, f32[2,256,128]{2,1,0:T(8,128)}, u32[]{:S(2)}, u32[]{:S(2)}) collective-permute-start(f32[2,256,128]{2,1,0:T(8,128)S(1)} %get-tuple-element.45), channel_id=1, source_target_pairs={{0,1},{1,2},{2,3},{3,4},{4,5},{5,6},{6,7},{7,8},{8,9},{9,10},{10,1... | collective-permute-start | bytes 786440 | tf_op jit(solution)/shard_map/ppermute | solution.py:17
  15.4 8.0 %copy-start.1 = (f32[3,4,256,128]{3,2,1,0:T(8,128)S(1)}, f32[3,4,256,128]{3,2,1,0:T(8,128)}, u32[]{:S(2)}) copy-start(f32[3,4,256,128]{3,2,1,0:T(8,128)} %param.4) | copy-start | bytes 4718596
  27.5 0.8 %copy-start.2 = (f32[4,2,128,128]{3,0,1,2:T(4,128)}, f32[4,2,128,128]{3,0,1,2:T(4,128)S(1)}, u32[]{:S(2)}) copy-start(f32[4,2,128,128]{3,0,1,2:T(4,128)S(1)} %copy.33) | copy-start | bytes 1572868
  27.5 3.9 %copy-start.4 = (f32[128,8,128]{2,1,0:T(8,128)S(1)}, f32[128,8,128]{2,1,0:T(8,128)}, u32[]{:S(2)}) copy-start(f32[128,8,128]{2,1,0:T(8,128)} %get-tuple-element.9) | copy-start | bytes 1572868
  27.5 3.9 %copy-start.5 = (f32[128,8,128]{2,1,0:T(8,128)S(1)}, f32[128,8,128]{2,1,0:T(8,128)}, u32[]{:S(2)}) copy-start(f32[128,8,128]{2,1,0:T(8,128)} %get-tuple-element.10) | copy-start | bytes 1572868
  54.3 1.0 %copy-start.3 = (f32[128,8,128]{2,1,0:T(8,128)S(1)}, f32[128,8,128]{2,1,0:T(8,128)}, u32[]{:S(2)}) copy-start(f32[128,8,128]{2,1,0:T(8,128)} %shard_map.38) | copy-start | bytes 1572868

commit v6 on v2

--- a/solution.py
+++ b/solution.py
@@ -106,74 +106,72 @@
     return tuple((value / main_diagonal for value in right_hand_sides))
 
 
-def to_chunks(values, chunks):
-    planes, length, lanes = values.shape
-    values = values.reshape(planes, chunks, length // chunks, lanes)
-    return values.transpose(2, 1, 0, 3).reshape(length // chunks, chunks * planes, lanes)
-
-
-def from_chunks(values, chunks):
-    rows, sublanes, lanes = values.shape
-    planes = sublanes // chunks
-    values = values.reshape(rows, chunks, planes, lanes).transpose(2, 1, 0, 3)
-    return values.reshape(planes, chunks * rows, lanes)
-
-
-def thomas_kernel(rate_ref, right_ref, part_ref, first_ref, last_ref, ratio_ref):
-    rows = rate_ref.shape[0]
-    zero = jnp.zeros(rate_ref.shape[1:], jnp.float32)
-    rate = rate_ref[1]
+def thomas_kernel(rate_ref, right_ref, part_ref, first_ref, last_ref, ratio_ref, ahead_ref, lead_ref):
+    rows = ratio_ref.shape[0]
+    sublanes = ratio_ref.shape[1]
+
+    def at(i):
+        return pl.ds(i, sublanes, stride=rows)
+
+    zero = jnp.zeros(ratio_ref.shape[1:], jnp.float32)
+    rate = rate_ref[at(1)]
     inverse = 1.0 / (1.0 + 2.0 * rate)
     ratio = -rate * inverse
-    part = right_ref[1] * inverse
+    part = right_ref[at(1)] * inverse
     first = rate * inverse
     ratio_ref[1] = ratio
-    part_ref[1] = part
-    first_ref[1] = first
+    ahead_ref[1] = part
+    lead_ref[1] = first
 
     def forward(i, carry):
         ratio, part, first, _ = carry
-        rate = rate_ref[i]
+        rate = rate_ref[at(i)]
         inverse = 1.0 / ((1.0 + 2.0 * rate) + rate * ratio)
         ratio = -rate * inverse
-        part = (right_ref[i] + rate * part) * inverse
+        part = (right_ref[at(i)] + rate * part) * inverse
         first = rate * first * inverse
         ratio_ref[i] = ratio
-        part_ref[i] = part
-        first_ref[i] = first
+        ahead_ref[i] = part
+        lead_ref[i] = first
         return ratio, part, first, inverse
 
     _, part, first, inverse = lax.fori_loop(
         2, rows - 1, forward, (ratio, part, first, zero), unroll=8
     )
-    last = rate_ref[rows - 2] * inverse
-    last_ref[rows - 2] = last
+    last = rate_ref[at(rows - 2)] * inverse
+    part_ref[at(rows - 2)] = part
+    first_ref[at(rows - 2)] = first
+    last_ref[at(rows - 2)] = last
 
     def backward(j, carry):
         part, first, last = carry
         i = rows - 3 - j
         ratio = ratio_ref[i]
-        part = part_ref[i] - ratio * part
-        first = first_ref[i] - ratio * first
+        part = ahead_ref[i] - ratio * part
+        first = lead_ref[i] - ratio * first
         last = -ratio * last
-        part_ref[i] = part
-        first_ref[i] = first
-        last_ref[i] = last
+        part_ref[at(i)] = part
+        first_ref[at(i)] = first
+        last_ref[at(i)] = last
         return part, first, last
 
     lax.fori_loop(0, rows - 3, backward, (part, first, last), unroll=8)
     for ref in (part_ref, first_ref, last_ref):
-        ref[0] = zero
-        ref[rows - 1] = zero
-
-
-def local_solve(rate, right):
-    shape = jax.ShapeDtypeStruct(rate.shape, jnp.float32)
-    return pl.pallas_call(
+        ref[at(0)] = zero
+        ref[at(rows - 1)] = zero
+
+
+def local_solve(rate, right, chunks):
+    planes, length, lanes = rate.shape
+    rows = length // chunks
+    flat = jax.ShapeDtypeStruct((planes * length, lanes), jnp.float32)
+    scratch = pltpu.VMEM((rows, planes * chunks, lanes), jnp.float32)
+    outs = pl.pallas_call(
         thomas_kernel,
-        out_shape=(shape, shape, shape),
-        scratch_shapes=[pltpu.VMEM(rate.shape, jnp.float32)],
-    )(rate, right)
+        out_shape=(flat, flat, flat),
+        scratch_shapes=[scratch, scratch, scratch],
+    )(rate.reshape(planes * length, lanes), right.reshape(planes * length, lanes))
+    return tuple(out.reshape(planes, chunks, rows, lanes) for out in outs)
 
 
 def shards(field, courant, diffusion_number):
@@ -184,29 +182,28 @@
     place = lax.axis_index("gx")
     device_count = lax.axis_size("gx")
     planes = field.shape[0]
-    rate = to_chunks(diffusion_number, chunks)
-    right = to_chunks(rhs, chunks)
-    part, first, last = local_solve(rate, right)
-    rows = rate.shape[0]
+    part, first, last = local_solve(diffusion_number, rhs, chunks)
+    rows = part.shape[2]
+    rate = diffusion_number.reshape(planes, chunks, rows, -1)
+    right = rhs.reshape(planes, chunks, rows, -1)
     low_open = (place > 0).astype(jnp.float32)
     high_open = (place < device_count - 1).astype(jnp.float32)
-    chunk_of = lax.broadcasted_iota(jnp.int32, (chunks, planes, 1), 0).reshape(chunks * planes, 1)
+    chunk_of = lax.broadcasted_iota(jnp.int32, (1, chunks, 1), 1)
     low_scale = jnp.where(chunk_of == 0, low_open, 1.0)
     high_scale = jnp.where(chunk_of == chunks - 1, high_open, 1.0)
-    rate_first, rate_last = rate[0], rate[rows - 1]
+    rate_first, rate_last = rate[:, :, 0], rate[:, :, rows - 1]
     sub_first = -rate_first * low_scale
-    diag_first = (1.0 + 2.0 * rate_first) - rate_first * first[1]
-    super_first = -rate_first * last[1]
-    right_first = right[0] + rate_first * part[1]
-    sub_last = -rate_last * first[rows - 2]
-    diag_last = (1.0 + 2.0 * rate_last) - rate_last * last[rows - 2]
+    diag_first = (1.0 + 2.0 * rate_first) - rate_first * first[:, :, 1]
+    super_first = -rate_first * last[:, :, 1]
+    right_first = right[:, :, 0] + rate_first * part[:, :, 1]
+    sub_last = -rate_last * first[:, :, rows - 2]
+    diag_last = (1.0 + 2.0 * rate_last) - rate_last * last[:, :, rows - 2]
     super_last = -rate_last * high_scale
-    right_last = right[rows - 1] + rate_last * part[rows - 2]
+    right_last = right[:, :, rows - 1] + rate_last * part[:, :, rows - 2]
     stacked = jnp.stack(
-        [sub_first, sub_last, diag_first, diag_last, super_first, super_last, right_first, right_last]
+        [sub_first, sub_last, diag_first, diag_last, super_first, super_last, right_first, right_last], 2
     )
     lanes = stacked.shape[-1]
-    stacked = stacked.reshape(8, chunks, planes, lanes).transpose(2, 1, 0, 3)
     stacked = stacked.reshape(planes, chunks * 8, lanes)
     gathered = lax.all_gather(stacked, "gx", axis=1, tiled=True)
     gathered = gathered.reshape(planes, device_count, chunks, 4, 2, lanes)
@@ -217,14 +214,13 @@
         gathered_lower_band, gathered_diagonal, gathered_upper_band, (gathered_rhs,), 1
     )[0]
     ends = lax.dynamic_slice_in_dim(boundary_rows_gathered, 2 * chunks * place, 2 * chunks, 1)
-    ends = ends.reshape(planes, chunks, 2, lanes).transpose(2, 1, 0, 3)
-    ends = ends.reshape(2, chunks * planes, lanes)
-    start_value, end_value = ends[0], ends[1]
-    solved = part + first * start_value[None] + last * end_value[None]
-    row = lax.broadcasted_iota(jnp.int32, (rows, 1, 1), 0)
-    solved = jnp.where(row == 0, start_value[None], solved)
-    solved = jnp.where(row == rows - 1, end_value[None], solved)
-    return from_chunks(solved, chunks)
+    ends = ends.reshape(planes, chunks, 2, 1, lanes)
+    start_value, end_value = ends[:, :, 0], ends[:, :, 1]
+    solved = part + first * start_value + last * end_value
+    row = lax.broadcasted_iota(jnp.int32, (1, 1, rows, 1), 2)
+    solved = jnp.where(row == 0, start_value, solved)
+    solved = jnp.where(row == rows - 1, end_value, solved)
+    return solved.reshape(planes, chunks * rows, lanes)
 
 
 def solution(mesh):

time: 50.9 us -> 49.2 us (0.967)
  local copies, waits for them, and re-layouts: 9.45 us -> 4.61 us
  blocking collectives: 20 us -> 21 us
  Pallas kernels: 4.03 us -> 5.01 us
  other arithmetic: 3.93 us -> 4.74 us
  waiting for transfers between devices: 0.01 us -> 0.64 us
    transpose x2 -> x0, local copies, waits for them, and re-layouts: 3.06 us -> none  [the longest x1 2.18 us: to_chunks(): values.transpose(2, 1, 0, 3)]
    unnamed x14 -> x12, local copies, waits for them, and re-layouts: 3.19 us -> 1.79 us
    add x0 -> x1, other arithmetic: none -> 0.98 us  [shards(): right_last = right[:, :, rows - 1] + rate_last * part[:, :, rows - 2]]
    pallas_call x1, Pallas kernels: 4.03 us -> 5.01 us  [local_solve(): pl.pallas_call(thomas_kernel, out_shape=(flat, flat, flat), scratch_shape...]
    all_gather x1, blocking collectives: 20 us -> 21 us  [shards(): gathered = lax.all_gather(stacked, 'gx', axis=1, tiled=True)]
    mul x1 -> x0, other arithmetic: 0.85 us -> none  [shards(): super_last = -rate_last * high_scale]
    add x1, other arithmetic: 1.14 us -> 1.92 us  [build_rhs(): field - transport + 0.05 * (curve_y + curve_z)]
    sub x1 -> x0, other arithmetic: 0.71 us -> none  [shards(): diag_first = 1.0 + 2.0 * rate_first - rate_first * first[1]]
  transfers between devices with their start and end apart: 4 -> 4, of which waited for: 0 -> 1; matrix products, arithmetic and copies ran while one was open for 8% -> 2% of each run, Pallas kernels for 0% -> 0%
where the time goes in v6:
time: 49.2 us; the launch traced here: 48.8 us
  blocking collectives  21 us (43%)
  starting transfers between devices  12.4 us (25%)
  Pallas kernels  5.01 us (10%)
  other arithmetic  4.74 us (10%)
  local copies, waits for them, and re-layouts  4.61 us (9%)
  waiting for transfers between devices  0.64 us (1%)
    all_gather x1, blocking collectives, shards(): gathered = lax.all_gather(stacked, 'gx', axis=1, tiled=True)  21 us
    ppermute x2, starting transfers between devices, padded_2(): lax.ppermute(head, axis, [((i + 1) % count, i) for i in range(ends)])  8.41 us
    pallas_call x1, Pallas kernels, local_solve(): pl.pallas_call(thomas_kernel, out_shape=(flat, flat, flat), scratch_shape...  5.01 us
    ppermute x2, starting transfers between devices, padded_2(): lax.ppermute(tail, axis, [(i, (i + 1) % count) for i in range(ends)])  4.03 us
    add x1, other arithmetic, build_rhs(): field - transport + 0.05 * (curve_y + curve_z)  1.92 us
    slice x2, local copies, waits for them, and re-layouts, padded_2(): head = lax.slice_in_dim(cells, 0, width, axis=dim)  1.87 us
    unnamed x12, local copies, waits for them, and re-layouts  1.79 us
  transfers between devices with their start and end apart: 4, of which 1 were waited for; matrix products, arithmetic and copies ran while one was open for 2% of the time, Pallas kernels for 0%

profile of v6, /device:TPU:1, one launch (start us, length us, event | category | flops | bytes accessed | tf_op | source)
XLA Modules:
  0.0 48.8 jit_solution(16716802215269643239)
XLA Ops:
  0.0 1.1 %fusion.32 = (f32[2,256,128]{2,1,0:T(8,128)S(1)}, f32[2,256,128]{2,1,0:T(8,128)S(1)}) fusion(f32[4,256,128]{2,1,0:T(8,128)} %param.3), kind=kLoop, calls=%fused_computation.105 | loop fusion | bytes 1048576 | tf_op jit(solution)/shard_map/slice | solution.py:13
  1.1 2.1 %collective-permute-start.3 = (f32[2,256,128]{2,1,0:T(8,128)S(1)}, f32[2,256,128]{2,1,0:T(8,128)S(1)}, u32[]{:S(2)}, u32[]{:S(2)}) collective-permute-start(f32[2,256,128]{2,1,0:T(8,128)S(1)} %get-tuple-element.42), channel_id=1, source_target_pairs={{0,1},{1,2},{2,3},{3,4},{4,5},{5,6},{6,7},{7,8},{8,9},{9,10},{10,1... | collective-permute-start | bytes 786440 | tf_op jit(solution)/shard_map/ppermute | solution.py:17
  3.2 3.8 %collective-permute-start.2 = (f32[2,256,128]{2,1,0:T(8,128)S(1)}, f32[2,256,128]{2,1,0:T(8,128)S(1)}, u32[]{:S(2)}, u32[]{:S(2)}) collective-permute-start(f32[2,256,128]{2,1,0:T(8,128)S(1)} %get-tuple-element.41), channel_id=1, source_target_pairs={{1,0},{2,1},{3,2},{4,3},{5,4},{6,5},{7,6},{8,7},{9,8},{10,9},{11,1... | collective-permute-start | bytes 786440 | tf_op jit(solution)/shard_map/ppermute | solution.py:19
  7.0 0.7 %fusion.34 = (f32[4,2,128]{2,1,0:T(2,128)S(1)}, f32[4,2,128]{2,1,0:T(2,128)S(1)}) fusion(f32[4,256,128]{2,1,0:T(8,128)} %param.3), kind=kLoop, calls=%fused_computation.107 | loop fusion | bytes 16384 | tf_op jit(solution)/shard_map/slice | solution.py:13
  7.8 4.6 %collective-permute-start = (f32[4,2,128]{2,1,0:T(2,128)S(1)}, f32[4,2,128]{2,1,0:T(2,128)S(1)}, u32[]{:S(2)}, u32[]{:S(2)}) collective-permute-start(f32[4,2,128]{2,1,0:T(2,128)S(1)} %get-tuple-element.48), channel_id=1, source_target_pairs={{16,0},{32,16},{48,32},{64,48},{80,64},{96,80},{112,96},{128,112},... | collective-permute-start | bytes 12296 | tf_op jit(solution)/shard_map/ppermute | solution.py:19
  12.4 1.9 %collective-permute-start.1 = (f32[4,2,128]{2,1,0:T(2,128)S(1)}, f32[4,2,128]{2,1,0:T(2,128)S(1)}, u32[]{:S(2)}, u32[]{:S(2)}) collective-permute-start(f32[4,2,128]{2,1,0:T(2,128)S(1)} %get-tuple-element.49), channel_id=1, source_target_pairs={{0,16},{16,32},{32,48},{48,64},{64,80},{80,96},{96,112},{112,128},... | collective-permute-start | bytes 12296 | tf_op jit(solution)/shard_map/ppermute | solution.py:17
  14.4 0.2 fusion.33
  14.6 0.0 collective-permute-done.3
  14.7 0.1 constant_dynamic-update-slice_fusion.3
  14.8 0.0 collective-permute-done.2
  14.8 0.6 %collective-permute-done.1 = f32[4,2,128]{2,1,0:T(2,128)S(1)} collective-permute-done((f32[4,2,128]{2,1,0:T(2,128)S(1)}, f32[4,2,128]{2,1,0:T(2,128)S(1)}, u32[]{:S(2)}, u32[]{:S(2)}) %collective-permute-start.1) | collective-permute-done | bytes 4128 | tf_op jit(solution)/shard_map/ppermute | solution.py:17
  15.5 0.6 %copy-done.1 = f32[3,4,256,128]{3,2,1,0:T(8,128)S(1)} copy-done((f32[3,4,256,128]{3,2,1,0:T(8,128)S(1)}, f32[3,4,256,128]{3,2,1,0:T(8,128)}, u32[]{:S(2)}) %copy-start.1) | copy-done | bytes 1572888
  16.0 1.9 %fusion.10 = f32[4,256,128]{2,1,0:T(8,128)} fusion(f32[4,256,128]{2,1,0:T(8,128)S(1)} %copy-done, f32[4,2,128]{2,1,0:T(2,128)S(1)} %collective-permute-done.1, f32[4,258,128]{2,1,0:T(8,128)S(1)} %constant_dynamic-update-slice_fusion, f32[4,256,2]{2,1,0:T(8,128)S(1)} %get-tuple-element.47, f32[4,256,2]{2,1,0:T(8,128)S(1)} %get-tuple-element.46, ...), kind=kLoop, calls=%fused_computation.20 | loop fusion | flops 6029312 | bytes 5787648 | tf_op jit(solution)/shard_map/add | solution.py:44
  17.9 5.0 %shard_map.37 = (f32[1024,128]{1,0:T(8,128)}, f32[1024,128]{1,0:T(8,128)}, f32[1024,128]{1,0:T(8,128)}) custom-call(f32[1024,128]{1,0:T(8,128)} %bitcast.64, f32[1024,128]{1,0:T(8,128)} %bitcast.57), custom_call_target="tpu_custom_call" | custom-call | tf_op jit(solution)/shard_map/pallas_call | solution.py:169
  23.0 1.0 %fusion.27 = (f32[4,2,1,128]{3,2,1,0:T(1,128)S(1)}, f32[4,2,1,128]{3,2,1,0:T(1,128)S(1)}, f32[4,2,1,128]{3,2,1,0:T(1,128)S(1)}, f32[4,2,1,128]{3,2,1,0:T(1,128)S...) fusion(f32[4,2,128,128]{3,2,1,0:T(8,128)} %bitcast.66, ...), kind=kLoop, calls=%fused_computation.87 | loop fusion | flops 18432 | bytes 73744 | tf_op jit(solution)/shard_map/add | solution.py:202
  23.9 0.1 stack.2
  24.0 21.0 %all_gather.3 = f32[4,256,128]{2,1,0:T(8,128)S(1)} all-gather(f32[4,16,128]{2,1,0:T(8,128)S(1)} %bitcast.72), channel_id=1, replica_groups=mesh['gx'=16,'gy'=16] {'gx'}, dimensions={1}, use_global_device_ids=true | all-gather | bytes 557056 | tf_op jit(solution)/shard_map/all_gather | solution.py:208
  45.0 0.2 fusion.31
  45.3 0.1 multiply_add_fusion.8
  45.5 0.1 multiply_add_fusion.7
  45.7 0.1 multiply_add_fusion.6
  45.8 0.1 multiply_add_fusion.5
  46.0 0.1 multiply_add_fusion.4
  46.2 0.1 multiply_add_fusion.3
  46.3 0.1 multiply_add_fusion.2
  46.4 0.1 multiply_add_fusion.1
  46.6 0.1 multiply_add_fusion
  46.7 0.1 fusion.23
  46.8 0.8 %copy-done.2 = f32[1024,128]{1,0:T(8,128)S(1)} copy-done((f32[1024,128]{1,0:T(8,128)S(1)}, f32[1024,128]{1,0:T(8,128)}, u32[]{:S(2)}) %copy-start.2) | copy-done | bytes 524312
  47.6 0.2 copy-done.3
  47.7 0.2 copy-done.4
  47.9 0.9 %bitcast_select_fusion.1 = f32[4,256,128]{2,1,0:T(8,128)} fusion(f32[4,256,128]{2,1,0:T(8,128)S(1)} %bitcast.71, f32[4,256,128]{2,1,0:T(8,128)S(1)} %bitcast.67, f32[4,256,128]{2,1,0:T(8,128)S(1)} %bitcast.69, f32[4,2,128]{2,1,0:T(2,128)S(1)} %bitcast.75, f32[4,2,128]{2,1,0:T(2,128)S(1)} %bitcast.74, pred[256]{0:T(512)(128)(4,1)S(1)} %get-tuple-element.101, ...), kind=kLoop, calls=%fused_computation.6 | loop fusion | flops 786432 | bytes 2105856 | tf_op jit(solution)/shard_map/jit(_where)/select_n | solution.py:222
  (39 shorter events, 0.5 us)
Async XLA Ops:
  0.0 14.4 %copy-start = (f32[4,256,128]{2,1,0:T(8,128)S(1)}, f32[4,256,128]{2,1,0:T(8,128)}, u32[]{:S(2)}) copy-start(f32[4,256,128]{2,1,0:T(8,128)} %param.3) | copy-start | bytes 1572868
  1.1 13.5 %collective-permute-start.3 = (f32[2,256,128]{2,1,0:T(8,128)S(1)}, f32[2,256,128]{2,1,0:T(8,128)S(1)}, u32[]{:S(2)}, u32[]{:S(2)}) collective-permute-start(f32[2,256,128]{2,1,0:T(8,128)S(1)} %get-tuple-element.42), channel_id=1, source_target_pairs={{0,1},{1,2},{2,3},{3,4},{4,5},{5,6},{6,7},{7,8},{8,9},{9,10},{10,1... | collective-permute-start | bytes 786440 | tf_op jit(solution)/shard_map/ppermute | solution.py:17
  3.2 11.5 %collective-permute-start.2 = (f32[2,256,128]{2,1,0:T(8,128)S(1)}, f32[2,256,128]{2,1,0:T(8,128)S(1)}, u32[]{:S(2)}, u32[]{:S(2)}) collective-permute-start(f32[2,256,128]{2,1,0:T(8,128)S(1)} %get-tuple-element.41), channel_id=1, source_target_pairs={{1,0},{2,1},{3,2},{4,3},{5,4},{6,5},{7,6},{8,7},{9,8},{10,9},{11,1... | collective-permute-start | bytes 786440 | tf_op jit(solution)/shard_map/ppermute | solution.py:19
  7.8 7.0 %collective-permute-start = (f32[4,2,128]{2,1,0:T(2,128)S(1)}, f32[4,2,128]{2,1,0:T(2,128)S(1)}, u32[]{:S(2)}, u32[]{:S(2)}) collective-permute-start(f32[4,2,128]{2,1,0:T(2,128)S(1)} %get-tuple-element.48), channel_id=1, source_target_pairs={{16,0},{32,16},{48,32},{64,48},{80,64},{96,80},{112,96},{128,112},... | collective-permute-start | bytes 12296 | tf_op jit(solution)/shard_map/ppermute | solution.py:19
  12.4 3.1 %collective-permute-start.1 = (f32[4,2,128]{2,1,0:T(2,128)S(1)}, f32[4,2,128]{2,1,0:T(2,128)S(1)}, u32[]{:S(2)}, u32[]{:S(2)}) collective-permute-start(f32[4,2,128]{2,1,0:T(2,128)S(1)} %get-tuple-element.49), channel_id=1, source_target_pairs={{0,16},{16,32},{32,48},{48,64},{64,80},{80,96},{96,112},{112,128},... | collective-permute-start | bytes 12296 | tf_op jit(solution)/shard_map/ppermute | solution.py:17
  14.6 1.4 %copy-start.1 = (f32[3,4,256,128]{3,2,1,0:T(8,128)S(1)}, f32[3,4,256,128]{3,2,1,0:T(8,128)}, u32[]{:S(2)}) copy-start(f32[3,4,256,128]{3,2,1,0:T(8,128)} %param.4) | copy-start | bytes 4718596
  46.5 1.0 %copy-start.2 = (f32[1024,128]{1,0:T(8,128)S(1)}, f32[1024,128]{1,0:T(8,128)}, u32[]{:S(2)}) copy-start(f32[1024,128]{1,0:T(8,128)} %get-tuple-element.10) | copy-start | bytes 1572868
  46.6 1.2 %copy-start.3 = (f32[1024,128]{1,0:T(8,128)S(1)}, f32[1024,128]{1,0:T(8,128)}, u32[]{:S(2)}) copy-start(f32[1024,128]{1,0:T(8,128)} %get-tuple-element.8) | copy-start | bytes 1572868
  46.6 1.3 %copy-start.4 = (f32[1024,128]{1,0:T(8,128)S(1)}, f32[1024,128]{1,0:T(8,128)}, u32[]{:S(2)}) copy-start(f32[1024,128]{1,0:T(8,128)} %get-tuple-element.9) | copy-start | bytes 1572868

commit v7 on v6

--- a/solution.py
+++ b/solution.py
@@ -175,7 +175,7 @@
 
 
 def shards(field, courant, diffusion_number):
-    chunks = 2
+    chunks = 4
     y_padded = padded_2(field, (("gy", 0),), 2, True)
     x_padded = padded_2(field, (("gx", 1),), 2, False)
     rhs = build_rhs(field, courant, y_padded, x_padded)

time: 49.2 us -> 84 us (1.71)
  waiting for transfers between devices: 0.64 us -> 39.7 us
  blocking collectives: 21 us -> 0 us
  between operations: 0.43 us -> 13.9 us
  local copies, waits for them, and re-layouts: 4.61 us -> 7.27 us
  other arithmetic: 4.74 us -> 5.92 us
    all_gather x0 -> x1, waiting for transfers between devices: none -> 39 us  [shards(): gathered = lax.all_gather(stacked, 'gx', axis=1, tiled=True)]
    all_gather x1 -> x0, blocking collectives: 21 us -> none  [shards(): gathered = lax.all_gather(stacked, 'gx', axis=1, tiled=True)]
    slice x1, local copies, waits for them, and re-layouts: 0.24 us -> 1.56 us  [shards(): gathered[:, :, :, k].reshape(planes, 2 * chunks * device_count, lanes)]
  transfers between devices with their start and end apart: 4 -> 5, of which waited for: 1 -> 2; matrix products, arithmetic and copies ran while one was open for 2% -> 2% of each run, Pallas kernels for 0% -> 0%
where the time goes in v7:
time: 84 us; the launch traced here: 83.7 us
  waiting for transfers between devices  39.7 us (47%)
  between operations  13.9 us (17%)
  starting transfers between devices  12.4 us (15%)
  local copies, waits for them, and re-layouts  7.27 us (9%)
  other arithmetic  5.92 us (7%)
  Pallas kernels  4.47 us (5%)
    all_gather x1, waiting for transfers between devices, shards(): gathered = lax.all_gather(stacked, 'gx', axis=1, tiled=True)  39 us
    ppermute x2, starting transfers between devices, padded_2(): lax.ppermute(head, axis, [((i + 1) % count, i) for i in range(ends)])  8.41 us
    pallas_call x1, Pallas kernels, local_solve(): pl.pallas_call(thomas_kernel, out_shape=(flat, flat, flat), scratch_shape...  4.47 us
    ppermute x2, starting transfers between devices, padded_2(): lax.ppermute(tail, axis, [(i, (i + 1) % count) for i in range(ends)])  4.03 us
    add x1, other arithmetic, build_rhs(): field - transport + 0.05 * (curve_y + curve_z)  1.92 us
    slice x2, local copies, waits for them, and re-layouts, padded_2(): head = lax.slice_in_dim(cells, 0, width, axis=dim)  1.86 us
    unnamed x12, local copies, waits for them, and re-layouts  1.81 us
  transfers between devices with their start and end apart: 5, of which 2 were waited for; matrix products, arithmetic and copies ran while one was open for 2% of the time, Pallas kernels for 0%

profile of v7, /device:TPU:1, one launch (start us, length us, event | category | flops | bytes accessed | tf_op | source)
XLA Modules:
  0.0 83.7 jit_solution(12589886822440810679)
XLA Ops:
  6.5 1.1 %fusion.32 = (f32[2,256,128]{2,1,0:T(8,128)S(1)}, f32[2,256,128]{2,1,0:T(8,128)S(1)}) fusion(f32[4,256,128]{2,1,0:T(8,128)} %param.3), kind=kLoop, calls=%fused_computation.109 | loop fusion | bytes 1048576 | tf_op jit(solution)/shard_map/slice | solution.py:13
  7.7 2.1 %collective-permute-start.3 = (f32[2,256,128]{2,1,0:T(8,128)S(1)}, f32[2,256,128]{2,1,0:T(8,128)S(1)}, u32[]{:S(2)}, u32[]{:S(2)}) collective-permute-start(f32[2,256,128]{2,1,0:T(8,128)S(1)} %get-tuple-element.45), channel_id=1, source_target_pairs={{0,1},{1,2},{2,3},{3,4},{4,5},{5,6},{6,7},{7,8},{8,9},{9,10},{10,1... | collective-permute-start | bytes 786440 | tf_op jit(solution)/shard_map/ppermute | solution.py:17
  9.8 3.8 %collective-permute-start.2 = (f32[2,256,128]{2,1,0:T(8,128)S(1)}, f32[2,256,128]{2,1,0:T(8,128)S(1)}, u32[]{:S(2)}, u32[]{:S(2)}) collective-permute-start(f32[2,256,128]{2,1,0:T(8,128)S(1)} %get-tuple-element.44), channel_id=1, source_target_pairs={{1,0},{2,1},{3,2},{4,3},{5,4},{6,5},{7,6},{8,7},{9,8},{10,9},{11,1... | collective-permute-start | bytes 786440 | tf_op jit(solution)/shard_map/ppermute | solution.py:19
  13.6 0.7 fusion.34
  14.3 4.6 %collective-permute-start = (f32[4,2,128]{2,1,0:T(2,128)S(1)}, f32[4,2,128]{2,1,0:T(2,128)S(1)}, u32[]{:S(2)}, u32[]{:S(2)}) collective-permute-start(f32[4,2,128]{2,1,0:T(2,128)S(1)} %get-tuple-element.51), channel_id=1, source_target_pairs={{16,0},{32,16},{48,32},{64,48},{80,64},{96,80},{112,96},{128,112},... | collective-permute-start | bytes 12296 | tf_op jit(solution)/shard_map/ppermute | solution.py:19
  18.9 1.9 %collective-permute-start.1 = (f32[4,2,128]{2,1,0:T(2,128)S(1)}, f32[4,2,128]{2,1,0:T(2,128)S(1)}, u32[]{:S(2)}, u32[]{:S(2)}) collective-permute-start(f32[4,2,128]{2,1,0:T(2,128)S(1)} %get-tuple-element.52), channel_id=1, source_target_pairs={{0,16},{16,32},{32,48},{48,64},{64,80},{80,96},{96,112},{112,128},... | collective-permute-start | bytes 12296 | tf_op jit(solution)/shard_map/ppermute | solution.py:17
  20.9 0.2 fusion.33
  21.1 0.1 constant_dynamic-update-slice_fusion.3
  21.3 0.7 collective-permute-done.1
  22.0 0.5 copy-done.1
  22.5 1.9 %fusion.10 = f32[4,256,128]{2,1,0:T(8,128)} fusion(f32[4,256,128]{2,1,0:T(8,128)S(1)} %copy-done, f32[4,2,128]{2,1,0:T(2,128)S(1)} %collective-permute-done.1, f32[4,258,128]{2,1,0:T(8,128)S(1)} %constant_dynamic-update-slice_fusion, f32[4,256,2]{2,1,0:T(8,128)S(1)} %get-tuple-element.50, f32[4,256,2]{2,1,0:T(8,128)S(1)} %get-tuple-element.49, ...), kind=kLoop, calls=%fused_computation.20 | loop fusion | flops 6029312 | bytes 5787648 | tf_op jit(solution)/shard_map/add | solution.py:44
  24.4 4.5 %shard_map.37 = (f32[1024,128]{1,0:T(8,128)}, f32[1024,128]{1,0:T(8,128)}, f32[1024,128]{1,0:T(8,128)}) custom-call(f32[1024,128]{1,0:T(8,128)} %bitcast.60, f32[1024,128]{1,0:T(8,128)} %bitcast.57), custom_call_target="tpu_custom_call" | custom-call | tf_op jit(solution)/shard_map/pallas_call | solution.py:169
  28.9 1.2 %fusion.27 = (f32[4,4,1,128]{3,2,1,0:T(1,128)S(1)}, f32[4,4,1,128]{3,2,1,0:T(1,128)S(1)}, f32[4,4,1,128]{3,2,1,0:T(1,128)S(1)}, f32[4,4,1,128]{3,2,1,0:T(1,128)S...) fusion(f32[4,4,64,128]{3,2,1,0:T(8,128)} %bitcast.62, ...), kind=kLoop, calls=%fused_computation.93 | loop fusion | flops 36864 | bytes 147488 | tf_op jit(solution)/shard_map/add | solution.py:202
  30.1 0.7 stack.2
  31.0 0.1 broadcast_in_dim.64
  31.1 39.0 %all-gather.2.cloned.1.call-done = f32[4,512,128]{2,1,0:T(8,128)} async-done(((f32[4,32,128]{2,1,0:T(8,128)}), f32[4,512,128]{2,1,0:T(8,128)}) %all-gather.2.cloned.1.call-update) | async-done | bytes 1048592 | tf_op jit(solution)/shard_map/all_gather | solution.py:208
  70.1 1.6 %fusion.31 = (f32[4,16,4,1,2,128]{5,4,3,2,1,0:T(2,128)S(1)}, f32[4,16,4,1,2,128]{5,4,3,2,1,0:T(2,128)S(1)}, f32[4,16,4,1,2,128]{5,4,3,2,1,0:T(2,128)S(1)}, f32[4,16,4,1,2,128]{5,4,3,2,1,0:T(2,128)S(1)}) fusion(f32[4,16,4,4,2,128]{5,4,3,2,1,0:T(2,128)} %bitcast.59), kind=kLoop, calls=%fused_computation.108 | loop fusion | bytes 2097152 | tf_op jit(solution)/shard_map/slice | solution.py:211
  71.8 0.2 multiply_add_fusion.10
  72.1 0.2 multiply_add_fusion.9
  72.5 0.1 multiply_add_fusion.8
  72.7 0.2 multiply_add_fusion.7
  73.0 0.1 multiply_add_fusion.6
  73.3 0.2 multiply_add_fusion.5
  73.6 0.1 multiply_add_fusion.4
  73.7 0.2 multiply_add_fusion.3
  74.0 0.1 multiply_add_fusion.2
  74.2 0.2 multiply_add_fusion.1
  74.4 0.1 pad_multiply_fusion.1
  74.7 0.8 %copy-done.2 = f32[1024,128]{1,0:T(8,128)S(1)} copy-done((f32[1024,128]{1,0:T(8,128)S(1)}, f32[1024,128]{1,0:T(8,128)}, u32[]{:S(2)}) %copy-start.2) | copy-done | bytes 524312
  75.6 0.2 copy-done.3
  75.7 0.2 copy-done.4
  75.9 0.9 %bitcast_select_fusion.1 = f32[4,256,128]{2,1,0:T(8,128)} fusion(f32[4,256,128]{2,1,0:T(8,128)S(1)} %bitcast.67, f32[4,256,128]{2,1,0:T(8,128)S(1)} %bitcast.63, f32[4,256,128]{2,1,0:T(8,128)S(1)} %bitcast.65, f32[4,4,128]{2,1,0:T(4,128)S(1)} %bitcast.71, f32[4,4,128]{2,1,0:T(4,128)S(1)} %bitcast.70, pred[256]{0:T(512)(128)(4,1)S(1)} %broadcast_in_dim.64, ...), kind=kLoop, calls=%fused_computation.6 | loop fusion | flops 786432 | bytes 2114048 | tf_op jit(solution)/shard_map/jit(_where)/select_n | solution.py:222
  (50 shorter events, 1.1 us)
Async XLA Ops:
  6.5 14.4 %copy-start = (f32[4,256,128]{2,1,0:T(8,128)S(1)}, f32[4,256,128]{2,1,0:T(8,128)}, u32[]{:S(2)}) copy-start(f32[4,256,128]{2,1,0:T(8,128)} %param.3) | copy-start | bytes 1572868
  6.5 63.6 %all-gather.2.cloned.1.call-start = ((), (), s32[]{:S(2)}) async-start(), calls=%async_computation | async-start | bytes 1114112 | tf_op jit(solution)/shard_map/all_gather | solution.py:208
  7.7 13.4 %collective-permute-start.3 = (f32[2,256,128]{2,1,0:T(8,128)S(1)}, f32[2,256,128]{2,1,0:T(8,128)S(1)}, u32[]{:S(2)}, u32[]{:S(2)}) collective-permute-start(f32[2,256,128]{2,1,0:T(8,128)S(1)} %get-tuple-element.45), channel_id=1, source_target_pairs={{0,1},{1,2},{2,3},{3,4},{4,5},{5,6},{6,7},{7,8},{8,9},{9,10},{10,1... | collective-permute-start | bytes 786440 | tf_op jit(solution)/shard_map/ppermute | solution.py:17
  9.8 11.5 %collective-permute-start.2 = (f32[2,256,128]{2,1,0:T(8,128)S(1)}, f32[2,256,128]{2,1,0:T(8,128)S(1)}, u32[]{:S(2)}, u32[]{:S(2)}) collective-permute-start(f32[2,256,128]{2,1,0:T(8,128)S(1)} %get-tuple-element.44), channel_id=1, source_target_pairs={{1,0},{2,1},{3,2},{4,3},{5,4},{6,5},{7,6},{8,7},{9,8},{10,9},{11,1... | collective-permute-start | bytes 786440 | tf_op jit(solution)/shard_map/ppermute | solution.py:19
  14.3 7.0 %collective-permute-start = (f32[4,2,128]{2,1,0:T(2,128)S(1)}, f32[4,2,128]{2,1,0:T(2,128)S(1)}, u32[]{:S(2)}, u32[]{:S(2)}) collective-permute-start(f32[4,2,128]{2,1,0:T(2,128)S(1)} %get-tuple-element.51), channel_id=1, source_target_pairs={{16,0},{32,16},{48,32},{64,48},{80,64},{96,80},{112,96},{128,112},... | collective-permute-start | bytes 12296 | tf_op jit(solution)/shard_map/ppermute | solution.py:19
  18.9 3.1 %collective-permute-start.1 = (f32[4,2,128]{2,1,0:T(2,128)S(1)}, f32[4,2,128]{2,1,0:T(2,128)S(1)}, u32[]{:S(2)}, u32[]{:S(2)}) collective-permute-start(f32[4,2,128]{2,1,0:T(2,128)S(1)} %get-tuple-element.52), channel_id=1, source_target_pairs={{0,16},{16,32},{32,48},{48,64},{64,80},{80,96},{96,112},{112,128},... | collective-permute-start | bytes 12296 | tf_op jit(solution)/shard_map/ppermute | solution.py:17
  21.1 1.4 %copy-start.1 = (f32[3,4,256,128]{3,2,1,0:T(8,128)S(1)}, f32[3,4,256,128]{3,2,1,0:T(8,128)}, u32[]{:S(2)}) copy-start(f32[3,4,256,128]{3,2,1,0:T(8,128)} %param.4) | copy-start | bytes 4718596
  74.5 1.0 %copy-start.2 = (f32[1024,128]{1,0:T(8,128)S(1)}, f32[1024,128]{1,0:T(8,128)}, u32[]{:S(2)}) copy-start(f32[1024,128]{1,0:T(8,128)} %get-tuple-element.10) | copy-start | bytes 1572868
  74.5 1.2 %copy-start.3 = (f32[1024,128]{1,0:T(8,128)S(1)}, f32[1024,128]{1,0:T(8,128)}, u32[]{:S(2)}) copy-start(f32[1024,128]{1,0:T(8,128)} %get-tuple-element.8) | copy-start | bytes 1572868
  74.6 1.3 %copy-start.4 = (f32[1024,128]{1,0:T(8,128)S(1)}, f32[1024,128]{1,0:T(8,128)}, u32[]{:S(2)}) copy-start(f32[1024,128]{1,0:T(8,128)} %get-tuple-element.9) | copy-start | bytes 1572868
Sparse Core Ops, SparseCore 0:
  31.0 39.0 all-gather.1

commit v8 on v6

--- a/solution.py
+++ b/solution.py
@@ -106,7 +106,7 @@
     return tuple((value / main_diagonal for value in right_hand_sides))
 
 
-def thomas_kernel(rate_ref, right_ref, part_ref, first_ref, last_ref, ratio_ref, ahead_ref, lead_ref):
+def factor_kernel(rate_ref, ratio_ref, inverse_ref, first_ref, last_ref, lead_ref):
     rows = ratio_ref.shape[0]
     sublanes = ratio_ref.shape[1]
 
@@ -117,61 +117,93 @@
     rate = rate_ref[at(1)]
     inverse = 1.0 / (1.0 + 2.0 * rate)
     ratio = -rate * inverse
-    part = right_ref[at(1)] * inverse
     first = rate * inverse
     ratio_ref[1] = ratio
-    ahead_ref[1] = part
+    inverse_ref[1] = inverse
     lead_ref[1] = first
 
     def forward(i, carry):
-        ratio, part, first, _ = carry
+        ratio, first, _ = carry
         rate = rate_ref[at(i)]
         inverse = 1.0 / ((1.0 + 2.0 * rate) + rate * ratio)
         ratio = -rate * inverse
-        part = (right_ref[at(i)] + rate * part) * inverse
         first = rate * first * inverse
         ratio_ref[i] = ratio
-        ahead_ref[i] = part
+        inverse_ref[i] = inverse
         lead_ref[i] = first
-        return ratio, part, first, inverse
-
-    _, part, first, inverse = lax.fori_loop(
-        2, rows - 1, forward, (ratio, part, first, zero), unroll=8
-    )
+        return ratio, first, inverse
+
+    _, first, inverse = lax.fori_loop(2, rows - 1, forward, (ratio, first, zero), unroll=8)
     last = rate_ref[at(rows - 2)] * inverse
-    part_ref[at(rows - 2)] = part
     first_ref[at(rows - 2)] = first
     last_ref[at(rows - 2)] = last
 
     def backward(j, carry):
-        part, first, last = carry
+        first, last = carry
         i = rows - 3 - j
         ratio = ratio_ref[i]
-        part = ahead_ref[i] - ratio * part
         first = lead_ref[i] - ratio * first
         last = -ratio * last
-        part_ref[at(i)] = part
         first_ref[at(i)] = first
         last_ref[at(i)] = last
-        return part, first, last
-
-    lax.fori_loop(0, rows - 3, backward, (part, first, last), unroll=8)
-    for ref in (part_ref, first_ref, last_ref):
+        return first, last
+
+    lax.fori_loop(0, rows - 3, backward, (first, last), unroll=8)
+    for ref in (first_ref, last_ref):
         ref[at(0)] = zero
         ref[at(rows - 1)] = zero
 
 
-def local_solve(rate, right, chunks):
+def substitute_kernel(rate_ref, right_ref, ratio_ref, inverse_ref, part_ref, ahead_ref):
+    rows = ratio_ref.shape[0]
+    sublanes = ratio_ref.shape[1]
+
+    def at(i):
+        return pl.ds(i, sublanes, stride=rows)
+
+    zero = jnp.zeros(ratio_ref.shape[1:], jnp.float32)
+    part = right_ref[at(1)] * inverse_ref[1]
+    ahead_ref[1] = part
+
+    def forward(i, part):
+        part = (right_ref[at(i)] + rate_ref[at(i)] * part) * inverse_ref[i]
+        ahead_ref[i] = part
+        return part
+
+    part = lax.fori_loop(2, rows - 1, forward, part, unroll=8)
+    part_ref[at(rows - 2)] = part
+
+    def backward(j, part):
+        i = rows - 3 - j
+        part = ahead_ref[i] - ratio_ref[i] * part
+        part_ref[at(i)] = part
+        return part
+
+    lax.fori_loop(0, rows - 3, backward, part, unroll=8)
+    part_ref[at(0)] = zero
+    part_ref[at(rows - 1)] = zero
+
+
+def local_factor(rate, chunks):
     planes, length, lanes = rate.shape
     rows = length // chunks
     flat = jax.ShapeDtypeStruct((planes * length, lanes), jnp.float32)
-    scratch = pltpu.VMEM((rows, planes * chunks, lanes), jnp.float32)
-    outs = pl.pallas_call(
-        thomas_kernel,
-        out_shape=(flat, flat, flat),
-        scratch_shapes=[scratch, scratch, scratch],
-    )(rate.reshape(planes * length, lanes), right.reshape(planes * length, lanes))
-    return tuple(out.reshape(planes, chunks, rows, lanes) for out in outs)
+    table = jax.ShapeDtypeStruct((rows, planes * chunks, lanes), jnp.float32)
+    return pl.pallas_call(
+        factor_kernel,
+        out_shape=(table, table, flat, flat),
+        scratch_shapes=[pltpu.VMEM(table.shape, jnp.float32)],
+    )(rate.reshape(planes * length, lanes))
+
+
+def local_substitute(rate, right, ratio, inverse):
+    planes, length, lanes = rate.shape
+    flat = jax.ShapeDtypeStruct((planes * length, lanes), jnp.float32)
+    return pl.pallas_call(
+        substitute_kernel,
+        out_shape=flat,
+        scratch_shapes=[pltpu.VMEM(ratio.shape, jnp.float32)],
+    )(rate.reshape(planes * length, lanes), right.reshape(planes * length, lanes), ratio, inverse)
 
 
 def shards(field, courant, diffusion_number):
@@ -182,8 +214,10 @@
     place = lax.axis_index("gx")
     device_count = lax.axis_size("gx")
     planes = field.shape[0]
-    part, first, last = local_solve(diffusion_number, rhs, chunks)
-    rows = part.shape[2]
+    ratio, inverse, first, last = local_factor(diffusion_number, chunks)
+    part = local_substitute(diffusion_number, rhs, ratio, inverse)
+    rows = ratio.shape[0]
+    part, first, last = (value.reshape(planes, chunks, rows, -1) for value in (part, first, last))
     rate = diffusion_number.reshape(planes, chunks, rows, -1)
     right = rhs.reshape(planes, chunks, rows, -1)
     low_open = (place > 0).astype(jnp.float32)

time: 49.2 us -> 50.9 us (1.035)
  Pallas kernels: 5.01 us -> 7.96 us
  blocking collectives: 21 us -> 20 us
  waiting for transfers between devices: 0.64 us -> 0.01 us
    pallas_call x1 -> x2, Pallas kernels: 5.01 us -> 7.96 us  [the longest x1 4.43 us: local_factor(): pl.pallas_call(factor_kernel, out_shape=(table, table, flat, flat), scrat...]
    all_gather x1, blocking collectives: 21 us -> 20 us  [shards(): gathered = lax.all_gather(stacked, 'gx', axis=1, tiled=True)]
    ppermute x2, waiting for transfers between devices: 0.64 us -> 0.01 us  [padded_2(): lax.ppermute(tail, axis, [(i, (i + 1) % count) for i in range(ends)])]
  transfers between devices with their start and end apart: 4 -> 4, of which waited for: 1 -> 0; matrix products, arithmetic and copies ran while one was open for 2% -> 2% of each run, Pallas kernels for 0% -> 9%
where the time goes in v8:
time: 50.9 us; the launch traced here: 50.5 us
  blocking collectives  20 us (39%)
  starting transfers between devices  12.4 us (24%)
  Pallas kernels  7.96 us (16%)
  local copies, waits for them, and re-layouts  4.94 us (10%)
  other arithmetic  4.69 us (9%)
    all_gather x1, blocking collectives, shards(): gathered = lax.all_gather(stacked, 'gx', axis=1, tiled=True)  20 us
    ppermute x2, starting transfers between devices, padded_2(): lax.ppermute(head, axis, [((i + 1) % count, i) for i in range(ends)])  8.41 us
    pallas_call x1, Pallas kernels, local_factor(): pl.pallas_call(factor_kernel, out_shape=(table, table, flat, flat), scrat...  4.43 us
    ppermute x2, starting transfers between devices, padded_2(): lax.ppermute(tail, axis, [(i, (i + 1) % count) for i in range(ends)])  4.03 us
    pallas_call x1, Pallas kernels, local_substitute(): pl.pallas_call(substitute_kernel, out_shape=flat, scratch_shapes=[pltpu.V...  3.53 us
    unnamed x12, local copies, waits for them, and re-layouts  2.12 us
    add x1, other arithmetic, build_rhs(): field - transport + 0.05 * (curve_y + curve_z)  1.92 us
    slice x2, local copies, waits for them, and re-layouts, padded_2(): head = lax.slice_in_dim(cells, 0, width, axis=dim)  1.87 us
  transfers between devices with their start and end apart: 4, of which 0 were waited for; matrix products, arithmetic and copies ran while one was open for 2% of the time, Pallas kernels for 9%

profile of v8, /device:TPU:1, one launch (start us, length us, event | category | flops | bytes accessed | tf_op | source)
XLA Modules:
  0.0 50.5 jit_solution(11011100592812087309)
XLA Ops:
  0.0 1.1 %fusion.32 = (f32[2,256,128]{2,1,0:T(8,128)S(1)}, f32[2,256,128]{2,1,0:T(8,128)S(1)}) fusion(f32[4,256,128]{2,1,0:T(8,128)} %param.3), kind=kLoop, calls=%fused_computation.105 | loop fusion | bytes 1048576 | tf_op jit(solution)/shard_map/slice | solution.py:13
  1.1 2.1 %collective-permute-start.3 = (f32[2,256,128]{2,1,0:T(8,128)S(1)}, f32[2,256,128]{2,1,0:T(8,128)S(1)}, u32[]{:S(2)}, u32[]{:S(2)}) collective-permute-start(f32[2,256,128]{2,1,0:T(8,128)S(1)} %get-tuple-element.44), channel_id=1, source_target_pairs={{0,1},{1,2},{2,3},{3,4},{4,5},{5,6},{6,7},{7,8},{8,9},{9,10},{10,1... | collective-permute-start | bytes 786440 | tf_op jit(solution)/shard_map/ppermute | solution.py:17
  3.2 3.8 %collective-permute-start.2 = (f32[2,256,128]{2,1,0:T(8,128)S(1)}, f32[2,256,128]{2,1,0:T(8,128)S(1)}, u32[]{:S(2)}, u32[]{:S(2)}) collective-permute-start(f32[2,256,128]{2,1,0:T(8,128)S(1)} %get-tuple-element.43), channel_id=1, source_target_pairs={{1,0},{2,1},{3,2},{4,3},{5,4},{6,5},{7,6},{8,7},{9,8},{10,9},{11,1... | collective-permute-start | bytes 786440 | tf_op jit(solution)/shard_map/ppermute | solution.py:19
  7.0 0.7 %fusion.34 = (f32[4,2,128]{2,1,0:T(2,128)S(1)}, f32[4,2,128]{2,1,0:T(2,128)S(1)}) fusion(f32[4,256,128]{2,1,0:T(8,128)} %param.3), kind=kLoop, calls=%fused_computation.107 | loop fusion | bytes 16384 | tf_op jit(solution)/shard_map/slice | solution.py:13
  7.8 4.6 %collective-permute-start = (f32[4,2,128]{2,1,0:T(2,128)S(1)}, f32[4,2,128]{2,1,0:T(2,128)S(1)}, u32[]{:S(2)}, u32[]{:S(2)}) collective-permute-start(f32[4,2,128]{2,1,0:T(2,128)S(1)} %get-tuple-element.50), channel_id=1, source_target_pairs={{16,0},{32,16},{48,32},{64,48},{80,64},{96,80},{112,96},{128,112},... | collective-permute-start | bytes 12296 | tf_op jit(solution)/shard_map/ppermute | solution.py:19
  12.4 1.9 %collective-permute-start.1 = (f32[4,2,128]{2,1,0:T(2,128)S(1)}, f32[4,2,128]{2,1,0:T(2,128)S(1)}, u32[]{:S(2)}, u32[]{:S(2)}) collective-permute-start(f32[4,2,128]{2,1,0:T(2,128)S(1)} %get-tuple-element.51), channel_id=1, source_target_pairs={{0,16},{16,32},{32,48},{48,64},{64,80},{80,96},{96,112},{112,128},... | collective-permute-start | bytes 12296 | tf_op jit(solution)/shard_map/ppermute | solution.py:17
  14.4 4.4 %shard_map.37 = (f32[128,8,128]{2,1,0:T(8,128)}, f32[128,8,128]{2,1,0:T(8,128)}, f32[1024,128]{1,0:T(8,128)}, f32[1024,128]{1,0:T(8,128)}) custom-call(f32[1024,128]{1,0:T(8,128)} %bitcast.59), custom_call_target="tpu_custom_call" | custom-call | tf_op jit(solution)/shard_map/pallas_call | solution.py:192
  18.8 0.2 fusion.33
  19.0 0.0 collective-permute-done.3
  19.1 0.1 constant_dynamic-update-slice_fusion.3
  19.2 0.0 collective-permute-done.2
  19.2 0.0 collective-permute-done
  19.2 0.0 collective-permute-done.1
  19.3 1.2 %copy-done.2 = f32[3,4,256,128]{3,2,1,0:T(8,128)S(1)} copy-done((f32[3,4,256,128]{3,2,1,0:T(8,128)S(1)}, f32[3,4,256,128]{3,2,1,0:T(8,128)}, u32[]{:S(2)}) %copy-start.2) | copy-done | bytes 1572888
  20.4 1.9 %fusion.10 = f32[4,256,128]{2,1,0:T(8,128)} fusion(f32[4,256,128]{2,1,0:T(8,128)S(1)} %copy-done, f32[4,2,128]{2,1,0:T(2,128)S(1)} %collective-permute-done.1, f32[4,258,128]{2,1,0:T(8,128)S(1)} %constant_dynamic-update-slice_fusion, f32[4,256,2]{2,1,0:T(8,128)S(1)} %get-tuple-element.49, f32[4,256,2]{2,1,0:T(8,128)S(1)} %get-tuple-element.48, ...), kind=kLoop, calls=%fused_computation.20 | loop fusion | flops 6029312 | bytes 5787648 | tf_op jit(solution)/shard_map/add | solution.py:44
  22.4 3.5 %shard_map.38 = f32[1024,128]{1,0:T(8,128)} custom-call(f32[1024,128]{1,0:T(8,128)} %bitcast.60, f32[1024,128]{1,0:T(8,128)} %bitcast.57, f32[128,8,128]{2,1,0:T(8,128)} %get-tuple-element.11.ratio_ref, f32[128,8,128]{2,1,0:T(8,128)} %get-tuple-element.12.inverse_ref), custom_call_target="tpu_custom_call" | custom-call | tf_op jit(solution)/shard_map/pallas_call | solution.py:202
  25.9 0.9 %fusion.27 = (f32[4,2,1,128]{3,2,1,0:T(1,128)S(1)}, f32[4,2,1,128]{3,2,1,0:T(1,128)S(1)}, f32[4,2,1,128]{3,2,1,0:T(1,128)S(1)}, f32[4,2,1,128]{3,2,1,0:T(1,128)S...) fusion(f32[4,2,128,128]{3,2,1,0:T(8,128)} %bitcast.62, ...), kind=kLoop, calls=%fused_computation.87 | loop fusion | flops 18432 | bytes 73744 | tf_op jit(solution)/shard_map/add | solution.py:236
  26.8 0.1 stack.2
  26.9 20.0 %all_gather.3 = f32[4,256,128]{2,1,0:T(8,128)S(1)} all-gather(f32[4,16,128]{2,1,0:T(8,128)S(1)} %bitcast.73), channel_id=1, replica_groups=mesh['gx'=16,'gy'=16] {'gx'}, dimensions={1}, use_global_device_ids=true | all-gather | bytes 557056 | tf_op jit(solution)/shard_map/all_gather | solution.py:242
  46.9 0.2 fusion.31
  47.3 0.1 multiply_add_fusion.8
  47.4 0.1 multiply_add_fusion.7
  47.6 0.1 multiply_add_fusion.6
  47.8 0.1 multiply_add_fusion.5
  48.0 0.1 multiply_add_fusion.4
  48.1 0.1 multiply_add_fusion.3
  48.3 0.1 multiply_add_fusion.2
  48.4 0.1 multiply_add_fusion.1
  48.5 0.1 multiply_add_fusion
  48.7 0.1 fusion.23
  48.7 0.8 %copy-done.1 = f32[1024,128]{1,0:T(8,128)S(1)} copy-done((f32[1024,128]{1,0:T(8,128)S(1)}, f32[1024,128]{1,0:T(8,128)}, u32[]{:S(2)}) %copy-start.1) | copy-done | bytes 524312
  49.5 0.9 %bitcast_select_fusion.1 = f32[4,256,128]{2,1,0:T(8,128)} fusion(f32[4,256,128]{2,1,0:T(8,128)S(1)} %bitcast.72, f32[4,256,128]{2,1,0:T(8,128)S(1)} %bitcast.63, f32[4,256,128]{2,1,0:T(8,128)S(1)} %bitcast.70, f32[4,2,128]{2,1,0:T(2,128)S(1)} %bitcast.76, f32[4,2,128]{2,1,0:T(2,128)S(1)} %bitcast.75, pred[256]{0:T(512)(128)(4,1)S(1)} %get-tuple-element.103, ...), kind=kLoop, calls=%fused_computation.6 | loop fusion | flops 786432 | bytes 2105856 | tf_op jit(solution)/shard_map/jit(_where)/select_n | solution.py:256
  (40 shorter events, 0.5 us)
Async XLA Ops:
  0.0 18.8 %copy-start = (f32[4,256,128]{2,1,0:T(8,128)S(1)}, f32[4,256,128]{2,1,0:T(8,128)}, u32[]{:S(2)}) copy-start(f32[4,256,128]{2,1,0:T(8,128)} %param.3) | copy-start | bytes 1572868
  1.1 17.9 %collective-permute-start.3 = (f32[2,256,128]{2,1,0:T(8,128)S(1)}, f32[2,256,128]{2,1,0:T(8,128)S(1)}, u32[]{:S(2)}, u32[]{:S(2)}) collective-permute-start(f32[2,256,128]{2,1,0:T(8,128)S(1)} %get-tuple-element.44), channel_id=1, source_target_pairs={{0,1},{1,2},{2,3},{3,4},{4,5},{5,6},{6,7},{7,8},{8,9},{9,10},{10,1... | collective-permute-start | bytes 786440 | tf_op jit(solution)/shard_map/ppermute | solution.py:17
  3.2 15.9 %collective-permute-start.2 = (f32[2,256,128]{2,1,0:T(8,128)S(1)}, f32[2,256,128]{2,1,0:T(8,128)S(1)}, u32[]{:S(2)}, u32[]{:S(2)}) collective-permute-start(f32[2,256,128]{2,1,0:T(8,128)S(1)} %get-tuple-element.43), channel_id=1, source_target_pairs={{1,0},{2,1},{3,2},{4,3},{5,4},{6,5},{7,6},{8,7},{9,8},{10,9},{11,1... | collective-permute-start | bytes 786440 | tf_op jit(solution)/shard_map/ppermute | solution.py:19
  7.8 11.4 %collective-permute-start = (f32[4,2,128]{2,1,0:T(2,128)S(1)}, f32[4,2,128]{2,1,0:T(2,128)S(1)}, u32[]{:S(2)}, u32[]{:S(2)}) collective-permute-start(f32[4,2,128]{2,1,0:T(2,128)S(1)} %get-tuple-element.50), channel_id=1, source_target_pairs={{16,0},{32,16},{48,32},{64,48},{80,64},{96,80},{112,96},{128,112},... | collective-permute-start | bytes 12296 | tf_op jit(solution)/shard_map/ppermute | solution.py:19
  12.4 6.8 %collective-permute-start.1 = (f32[4,2,128]{2,1,0:T(2,128)S(1)}, f32[4,2,128]{2,1,0:T(2,128)S(1)}, u32[]{:S(2)}, u32[]{:S(2)}) collective-permute-start(f32[4,2,128]{2,1,0:T(2,128)S(1)} %get-tuple-element.51), channel_id=1, source_target_pairs={{0,16},{16,32},{32,48},{48,64},{64,80},{80,96},{96,112},{112,128},... | collective-permute-start | bytes 12296 | tf_op jit(solution)/shard_map/ppermute | solution.py:17
  19.0 1.4 %copy-start.2 = (f32[3,4,256,128]{3,2,1,0:T(8,128)S(1)}, f32[3,4,256,128]{3,2,1,0:T(8,128)}, u32[]{:S(2)}) copy-start(f32[3,4,256,128]{3,2,1,0:T(8,128)} %param.4) | copy-start | bytes 4718596
  22.4 3.5 %copy-start.3 = (f32[1024,128]{1,0:T(8,128)S(1)}, f32[1024,128]{1,0:T(8,128)}, u32[]{:S(2)}) copy-start(f32[1024,128]{1,0:T(8,128)} %get-tuple-element.9) | copy-start | bytes 1572868
  22.4 3.5 %copy-start.4 = (f32[1024,128]{1,0:T(8,128)S(1)}, f32[1024,128]{1,0:T(8,128)}, u32[]{:S(2)}) copy-start(f32[1024,128]{1,0:T(8,128)} %get-tuple-element.10) | copy-start | bytes 1572868
  48.5 1.0 %copy-start.1 = (f32[1024,128]{1,0:T(8,128)S(1)}, f32[1024,128]{1,0:T(8,128)}, u32[]{:S(2)}) copy-start(f32[1024,128]{1,0:T(8,128)} %shard_map.38) | copy-start | bytes 1572868

commit v9 on v6

--- a/solution.py
+++ b/solution.py
@@ -178,7 +178,12 @@
     chunks = 2
     y_padded = padded_2(field, (("gy", 0),), 2, True)
     x_padded = padded_2(field, (("gx", 1),), 2, False)
-    rhs = build_rhs(field, courant, y_padded, x_padded)
+    flat = jnp.zeros_like(field[:2])
+    own_rhs = build_rhs(field, courant, jnp.concatenate([flat, field, flat], 0), x_padded)
+    own_rhs = lax.optimization_barrier(own_rhs)
+    halo_only = jnp.concatenate([y_padded[:2], jnp.zeros_like(field), y_padded[-2:]], 0)
+    grad_y, curve_y = difference_pair(halo_only, 0, field.shape[0])
+    rhs = own_rhs + (0.05 * curve_y - courant[1] * grad_y)
     place = lax.axis_index("gx")
     device_count = lax.axis_size("gx")
     planes = field.shape[0]

time: 49.2 us -> 58.5 us (1.19)
  waiting for transfers between devices: 0.64 us -> 6.62 us
  other arithmetic: 4.74 us -> 7.22 us
  local copies, waits for them, and re-layouts: 4.61 us -> 6.54 us
  starting transfers between devices: 12.4 us -> 11.8 us
    ppermute x2, waiting for transfers between devices: 0.64 us -> 5.3 us  [padded_2(): lax.ppermute(tail, axis, [(i, (i + 1) % count) for i in range(ends)])]
    ppermute x2, starting transfers between devices: 4.03 us -> 1.92 us  [padded_2(): lax.ppermute(tail, axis, [(i, (i + 1) % count) for i in range(ends)])]
    add x0 -> x1, other arithmetic: none -> 2.1 us  [shards(): rhs = own_rhs + (0.05 * curve_y - courant[1] * grad_y)]
    slice x0 -> x1, local copies, waits for them, and re-layouts: none -> 1.77 us  [padded_2(): lax.slice_in_dim(cells, cells.shape[dim] - width, cells.shape[dim], axis=...]
    ppermute x2, starting transfers between devices: 8.41 us -> 9.84 us  [padded_2(): lax.ppermute(head, axis, [((i + 1) % count, i) for i in range(ends)])]
    ppermute x2, waiting for transfers between devices: 0.01 us -> 1.32 us  [padded_2(): lax.ppermute(head, axis, [((i + 1) % count, i) for i in range(ends)])]
    slice x2 -> x1, local copies, waits for them, and re-layouts: 1.87 us -> 0.8 us  [padded_2(): head = lax.slice_in_dim(cells, 0, width, axis=dim)]
    slice x1, local copies, waits for them, and re-layouts: 0.2 us -> 0.94 us  [build_rhs(): z_padded = jnp.concatenate([field[:, :, -2:], field, field[:, :, :2]], 2)]
  transfers between devices with their start and end apart: 4 -> 4, of which waited for: 1 -> 2; matrix products, arithmetic and copies ran while one was open for 2% -> 11% of each run, Pallas kernels for 0% -> 0%
where the time goes in v9:
time: 58.5 us; the launch traced here: 58.1 us
  blocking collectives  20.5 us (35%)
  starting transfers between devices  11.8 us (20%)
  other arithmetic  7.22 us (12%)
  waiting for transfers between devices  6.62 us (11%)
  local copies, waits for them, and re-layouts  6.54 us (11%)
  Pallas kernels  4.99 us (9%)
    all_gather x1, blocking collectives, shards(): gathered = lax.all_gather(stacked, 'gx', axis=1, tiled=True)  20.5 us
    ppermute x2, starting transfers between devices, padded_2(): lax.ppermute(head, axis, [((i + 1) % count, i) for i in range(ends)])  9.84 us
    ppermute x2, waiting for transfers between devices, padded_2(): lax.ppermute(tail, axis, [(i, (i + 1) % count) for i in range(ends)])  5.3 us
    pallas_call x1, Pallas kernels, local_solve(): pl.pallas_call(thomas_kernel, out_shape=(flat, flat, flat), scratch_shape...  4.99 us
    unnamed x11, local copies, waits for them, and re-layouts  2.31 us
    add x1, other arithmetic, build_rhs(): field - transport + 0.05 * (curve_y + curve_z)  2.31 us
    add x1, other arithmetic, shards(): rhs = own_rhs + (0.05 * curve_y - courant[1] * grad_y)  2.1 us
    ppermute x2, starting transfers between devices, padded_2(): lax.ppermute(tail, axis, [(i, (i + 1) % count) for i in range(ends)])  1.92 us
  transfers between devices with their start and end apart: 4, of which 2 were waited for; matrix products, arithmetic and copies ran while one was open for 11% of the time, Pallas kernels for 0%

profile of v9, /device:TPU:1, one launch (start us, length us, event | category | flops | bytes accessed | tf_op | source)
XLA Modules:
  0.0 58.1 jit_solution(5980202048964792467)
XLA Ops:
  0.0 0.8 %fusion.36 = (f32[4,2,128]{2,1,0:T(2,128)S(1)}, f32[4,2,128]{2,1,0:T(2,128)S(1)}) fusion(f32[4,256,128]{2,1,0:T(8,128)} %param.3), kind=kLoop, calls=%fused_computation.114 | loop fusion | bytes 16384 | tf_op jit(solution)/shard_map/slice | solution.py:13
  0.8 5.1 %collective-permute-start = (f32[4,2,128]{2,1,0:T(2,128)S(1)}, f32[4,2,128]{2,1,0:T(2,128)S(1)}, u32[]{:S(2)}, u32[]{:S(2)}) collective-permute-start(f32[4,2,128]{2,1,0:T(2,128)S(1)} %get-tuple-element.45), channel_id=1, source_target_pairs={{16,0},{32,16},{48,32},{64,48},{80,64},{96,80},{112,96},{128,112},... | collective-permute-start | bytes 12296 | tf_op jit(solution)/shard_map/ppermute | solution.py:19
  5.9 1.9 %collective-permute-start.1 = (f32[4,2,128]{2,1,0:T(2,128)S(1)}, f32[4,2,128]{2,1,0:T(2,128)S(1)}, u32[]{:S(2)}, u32[]{:S(2)}) collective-permute-start(f32[4,2,128]{2,1,0:T(2,128)S(1)} %get-tuple-element.46), channel_id=1, source_target_pairs={{0,16},{16,32},{32,48},{48,64},{64,80},{80,96},{96,112},{112,128},... | collective-permute-start | bytes 12296 | tf_op jit(solution)/shard_map/ppermute | solution.py:17
  7.8 1.8 %fusion.34 = (f32[2,256,128]{2,1,0:T(8,128)S(1)}, f32[2,256,128]{2,1,0:T(8,128)}) fusion(f32[4,256,128]{2,1,0:T(8,128)} %param.3), kind=kLoop, calls=%fused_computation.112 | loop fusion | bytes 1048576 | tf_op jit(solution)/shard_map/slice | solution.py:14
  9.6 4.7 %collective-permute-start.2 = (f32[2,256,128]{2,1,0:T(8,128)}, f32[2,256,128]{2,1,0:T(8,128)}, u32[]{:S(2)}, u32[]{:S(2)}) collective-permute-start(f32[2,256,128]{2,1,0:T(8,128)} %get-tuple-element.42), channel_id=1, source_target_pairs={{1,0},{2,1},{3,2},{4,3},{5,4},{6,5},{7,6},{8,7},{9,8},{10,9},{11,1... | collective-permute-start | bytes 786440 | tf_op jit(solution)/shard_map/ppermute | solution.py:19
  14.3 0.0 collective-permute-start.3
  14.4 1.2 %constant_dynamic-update-slice_fusion.1 = f32[4,258,128]{2,1,0:T(8,128)S(1)} fusion(f32[4,256,128]{2,1,0:T(8,128)} %param.3), kind=kLoop, calls=%fused_computation.92 | loop fusion | bytes 1048576
  15.6 0.9 %fusion.35 = (f32[4,256,2]{2,1,0:T(8,128)S(1)}, f32[4,256,2]{2,1,0:T(8,128)}) fusion(f32[4,256,128]{2,1,0:T(8,128)S(1)} %copy-done), kind=kLoop, calls=%fused_computation.113 | loop fusion | bytes 32768 | tf_op jit(solution)/shard_map/slice | solution.py:39
  16.6 0.0 collective-permute-done.1
  16.6 2.3 %fusion.10 = f32[4,256,128]{2,1,0:T(8,128)S(1)} fusion(f32[4,256,128]{2,1,0:T(8,128)S(1)} %copy-done, f32[4,2,128]{2,1,0:T(2,128)S(1)} %collective-permute-done.1, f32[4,258,128]{2,1,0:T(8,128)S(1)} %constant_dynamic-update-slice_fusion, f32[4,256,2]{2,1,0:T(8,128)} %get-tuple-element.44, f32[4,256,2]{2,1,0:T(8,128)S(1)} %get-tuple-element.43, ...), kind=kLoop, calls=%fused_computation.28 | loop fusion | flops 6029312 | bytes 3690496 | tf_op jit(solution)/shard_map/add | solution.py:44
  18.9 1.3 %collective-permute-done.2 = f32[2,256,128]{2,1,0:T(8,128)} collective-permute-done((f32[2,256,128]{2,1,0:T(8,128)}, f32[2,256,128]{2,1,0:T(8,128)}, u32[]{:S(2)}, u32[]{:S(2)}) %collective-permute-start.2) | collective-permute-done | bytes 262176 | tf_op jit(solution)/shard_map/ppermute | solution.py:19
  20.2 5.3 %collective-permute-done.3 = f32[2,256,128]{2,1,0:T(8,128)} collective-permute-done((f32[2,256,128]{2,1,0:T(8,128)S(1)}, f32[2,256,128]{2,1,0:T(8,128)}, u32[]{:S(2)}, u32[]{:S(2)}) %collective-permute-start.3) | collective-permute-done | bytes 262176 | tf_op jit(solution)/shard_map/ppermute | solution.py:17
  25.5 2.1 %fusion.17 = f32[4,256,128]{2,1,0:T(8,128)} fusion(f32[4,256,128]{2,1,0:T(8,128)S(1)} %fusion.10, f32[2,256,128]{2,1,0:T(8,128)} %collective-permute-done.2, f32[2,256,128]{2,1,0:T(8,128)} %collective-permute-done.3, f32[3,4,256,128]{3,2,1,0:T(8,128)S(1)} %copy-done.1), kind=kLoop, calls=%fused_computation.41 | loop fusion | flops 1703936 | bytes 2097152 | tf_op jit(solution)/shard_map/add | solution.py:186
  27.6 5.0 %shard_map.37 = (f32[1024,128]{1,0:T(8,128)}, f32[1024,128]{1,0:T(8,128)}, f32[1024,128]{1,0:T(8,128)}) custom-call(f32[1024,128]{1,0:T(8,128)} %bitcast.69, f32[1024,128]{1,0:T(8,128)} %bitcast.62), custom_call_target="tpu_custom_call" | custom-call | tf_op jit(solution)/shard_map/pallas_call | solution.py:169
  32.6 1.0 %fusion.29 = (f32[4,2,1,128]{3,2,1,0:T(1,128)S(1)}, f32[4,2,1,128]{3,2,1,0:T(1,128)S(1)}, f32[4,2,1,128]{3,2,1,0:T(1,128)S(1)}, f32[4,2,1,128]{3,2,1,0:T(1,128)S...) fusion(f32[4,2,128,128]{3,2,1,0:T(8,128)} %bitcast.71, ...), kind=kLoop, calls=%fused_computation.94 | loop fusion | flops 18432 | bytes 73744 | tf_op jit(solution)/shard_map/add | solution.py:207
  33.6 0.1 stack.2
  33.7 20.5 %all_gather.3 = f32[4,256,128]{2,1,0:T(8,128)S(1)} all-gather(f32[4,16,128]{2,1,0:T(8,128)S(1)} %bitcast.77), channel_id=1, replica_groups=mesh['gx'=16,'gy'=16] {'gx'}, dimensions={1}, use_global_device_ids=true | all-gather | bytes 557056 | tf_op jit(solution)/shard_map/all_gather | solution.py:213
  54.2 0.2 fusion.33
  54.5 0.1 multiply_add_fusion.8
  54.7 0.1 multiply_add_fusion.7
  54.9 0.1 multiply_add_fusion.6
  55.0 0.1 multiply_add_fusion.5
  55.2 0.1 multiply_add_fusion.4
  55.4 0.1 multiply_add_fusion.3
  55.5 0.1 multiply_add_fusion.2
  55.6 0.1 multiply_add_fusion.1
  55.8 0.1 multiply_add_fusion
  55.9 0.1 fusion.25
  56.0 0.8 %copy-done.2 = f32[1024,128]{1,0:T(8,128)S(1)} copy-done((f32[1024,128]{1,0:T(8,128)S(1)}, f32[1024,128]{1,0:T(8,128)}, u32[]{:S(2)}) %copy-start.2) | copy-done | bytes 524312
  56.8 0.2 copy-done.3
  57.0 0.2 copy-done.4
  57.1 0.9 %bitcast_select_fusion.1 = f32[4,256,128]{2,1,0:T(8,128)} fusion(f32[4,256,128]{2,1,0:T(8,128)S(1)} %bitcast.76, f32[4,256,128]{2,1,0:T(8,128)S(1)} %bitcast.72, f32[4,256,128]{2,1,0:T(8,128)S(1)} %bitcast.74, f32[4,2,128]{2,1,0:T(2,128)S(1)} %bitcast.80, f32[4,2,128]{2,1,0:T(2,128)S(1)} %bitcast.79, pred[256]{0:T(512)(128)(4,1)S(1)} %get-tuple-element.98, ...), kind=kLoop, calls=%fused_computation.14 | loop fusion | flops 786432 | bytes 2105856 | tf_op jit(solution)/shard_map/jit(_where)/select_n | solution.py:227
  (38 shorter events, 0.5 us)
Async XLA Ops:
  0.0 15.6 %copy-start = (f32[4,256,128]{2,1,0:T(8,128)S(1)}, f32[4,256,128]{2,1,0:T(8,128)}, u32[]{:S(2)}) copy-start(f32[4,256,128]{2,1,0:T(8,128)} %param.3) | copy-start | bytes 1572868
  0.8 15.8 %collective-permute-start = (f32[4,2,128]{2,1,0:T(2,128)S(1)}, f32[4,2,128]{2,1,0:T(2,128)S(1)}, u32[]{:S(2)}, u32[]{:S(2)}) collective-permute-start(f32[4,2,128]{2,1,0:T(2,128)S(1)} %get-tuple-element.45), channel_id=1, source_target_pairs={{16,0},{32,16},{48,32},{64,48},{80,64},{96,80},{112,96},{128,112},... | collective-permute-start | bytes 12296 | tf_op jit(solution)/shard_map/ppermute | solution.py:19
  5.9 10.7 %collective-permute-start.1 = (f32[4,2,128]{2,1,0:T(2,128)S(1)}, f32[4,2,128]{2,1,0:T(2,128)S(1)}, u32[]{:S(2)}, u32[]{:S(2)}) collective-permute-start(f32[4,2,128]{2,1,0:T(2,128)S(1)} %get-tuple-element.46), channel_id=1, source_target_pairs={{0,16},{16,32},{32,48},{48,64},{64,80},{80,96},{96,112},{112,128},... | collective-permute-start | bytes 12296 | tf_op jit(solution)/shard_map/ppermute | solution.py:17
  9.6 10.6 %collective-permute-start.2 = (f32[2,256,128]{2,1,0:T(8,128)}, f32[2,256,128]{2,1,0:T(8,128)}, u32[]{:S(2)}, u32[]{:S(2)}) collective-permute-start(f32[2,256,128]{2,1,0:T(8,128)} %get-tuple-element.42), channel_id=1, source_target_pairs={{1,0},{2,1},{3,2},{4,3},{5,4},{6,5},{7,6},{8,7},{9,8},{10,9},{11,1... | collective-permute-start | bytes 786440 | tf_op jit(solution)/shard_map/ppermute | solution.py:19
  14.3 2.2 %copy-start.1 = (f32[3,4,256,128]{3,2,1,0:T(8,128)S(1)}, f32[3,4,256,128]{3,2,1,0:T(8,128)}, u32[]{:S(2)}) copy-start(f32[3,4,256,128]{3,2,1,0:T(8,128)} %param.4) | copy-start | bytes 4718596
  14.3 11.2 %collective-permute-start.3 = (f32[2,256,128]{2,1,0:T(8,128)S(1)}, f32[2,256,128]{2,1,0:T(8,128)}, u32[]{:S(2)}, u32[]{:S(2)}) collective-permute-start(f32[2,256,128]{2,1,0:T(8,128)S(1)} %get-tuple-element.41), channel_id=1, source_target_pairs={{0,1},{1,2},{2,3},{3,4},{4,5},{5,6},{6,7},{7,8},{8,9},{9,10},{10,1... | collective-permute-start | bytes 786440 | tf_op jit(solution)/shard_map/ppermute | solution.py:17
  55.8 1.0 %copy-start.2 = (f32[1024,128]{1,0:T(8,128)S(1)}, f32[1024,128]{1,0:T(8,128)}, u32[]{:S(2)}) copy-start(f32[1024,128]{1,0:T(8,128)} %get-tuple-element.10) | copy-start | bytes 1572868
  55.8 1.2 %copy-start.3 = (f32[1024,128]{1,0:T(8,128)S(1)}, f32[1024,128]{1,0:T(8,128)}, u32[]{:S(2)}) copy-start(f32[1024,128]{1,0:T(8,128)} %get-tuple-element.8) | copy-start | bytes 1572868
  55.8 1.3 %copy-start.4 = (f32[1024,128]{1,0:T(8,128)S(1)}, f32[1024,128]{1,0:T(8,128)}, u32[]{:S(2)}) copy-start(f32[1024,128]{1,0:T(8,128)} %get-tuple-element.9) | copy-start | bytes 1572868

commit v10 on v6

--- a/solution.py
+++ b/solution.py
@@ -136,7 +136,7 @@
         return ratio, part, first, inverse
 
     _, part, first, inverse = lax.fori_loop(
-        2, rows - 1, forward, (ratio, part, first, zero), unroll=8
+        2, rows - 1, forward, (ratio, part, first, zero), unroll=True
     )
     last = rate_ref[at(rows - 2)] * inverse
     part_ref[at(rows - 2)] = part
@@ -155,7 +155,7 @@
         last_ref[at(i)] = last
         return part, first, last
 
-    lax.fori_loop(0, rows - 3, backward, (part, first, last), unroll=8)
+    lax.fori_loop(0, rows - 3, backward, (part, first, last), unroll=True)
     for ref in (part_ref, first_ref, last_ref):
         ref[at(0)] = zero
         ref[at(rows - 1)] = zero

time: 49.2 us -> 48.9 us (level)
  no operation moved by 1% of the time
where the time goes in v10:
time: 48.9 us; the launch traced here: 48.5 us
  blocking collectives  21 us (43%)
  starting transfers between devices  12.4 us (25%)
  other arithmetic  4.74 us (10%)
  Pallas kernels  4.71 us (10%)
  local copies, waits for them, and re-layouts  4.61 us (9%)
  waiting for transfers between devices  0.64 us (1%)
    all_gather x1, blocking collectives, shards(): gathered = lax.all_gather(stacked, 'gx', axis=1, tiled=True)  21 us
    ppermute x2, starting transfers between devices, padded_2(): lax.ppermute(head, axis, [((i + 1) % count, i) for i in range(ends)])  8.41 us
    pallas_call x1, Pallas kernels, local_solve(): pl.pallas_call(thomas_kernel, out_shape=(flat, flat, flat), scratch_shape...  4.71 us
    ppermute x2, starting transfers between devices, padded_2(): lax.ppermute(tail, axis, [(i, (i + 1) % count) for i in range(ends)])  4.03 us
    add x1, other arithmetic, build_rhs(): field - transport + 0.05 * (curve_y + curve_z)  1.92 us
    slice x2, local copies, waits for them, and re-layouts, padded_2(): head = lax.slice_in_dim(cells, 0, width, axis=dim)  1.87 us
    unnamed x12, local copies, waits for them, and re-layouts  1.79 us
    add x1, other arithmetic, shards(): right_last = right[:, :, rows - 1] + rate_last * part[:, :, rows - 2]  0.98 us
  transfers between devices with their start and end apart: 4, of which 1 were waited for; matrix products, arithmetic and copies ran while one was open for 2% of the time, Pallas kernels for 0%

profile of v10, /device:TPU:1, one launch (start us, length us, event | category | flops | bytes accessed | tf_op | source)
XLA Modules:
  0.0 48.5 jit_solution(14737904745805965785)
XLA Ops:
  0.0 1.1 %fusion.32 = (f32[2,256,128]{2,1,0:T(8,128)S(1)}, f32[2,256,128]{2,1,0:T(8,128)S(1)}) fusion(f32[4,256,128]{2,1,0:T(8,128)} %param.3), kind=kLoop, calls=%fused_computation.105 | loop fusion | bytes 1048576 | tf_op jit(solution)/shard_map/slice | solution.py:13
  1.1 2.1 %collective-permute-start.3 = (f32[2,256,128]{2,1,0:T(8,128)S(1)}, f32[2,256,128]{2,1,0:T(8,128)S(1)}, u32[]{:S(2)}, u32[]{:S(2)}) collective-permute-start(f32[2,256,128]{2,1,0:T(8,128)S(1)} %get-tuple-element.42), channel_id=1, source_target_pairs={{0,1},{1,2},{2,3},{3,4},{4,5},{5,6},{6,7},{7,8},{8,9},{9,10},{10,1... | collective-permute-start | bytes 786440 | tf_op jit(solution)/shard_map/ppermute | solution.py:17
  3.2 3.8 %collective-permute-start.2 = (f32[2,256,128]{2,1,0:T(8,128)S(1)}, f32[2,256,128]{2,1,0:T(8,128)S(1)}, u32[]{:S(2)}, u32[]{:S(2)}) collective-permute-start(f32[2,256,128]{2,1,0:T(8,128)S(1)} %get-tuple-element.41), channel_id=1, source_target_pairs={{1,0},{2,1},{3,2},{4,3},{5,4},{6,5},{7,6},{8,7},{9,8},{10,9},{11,1... | collective-permute-start | bytes 786440 | tf_op jit(solution)/shard_map/ppermute | solution.py:19
  7.0 0.7 %fusion.34 = (f32[4,2,128]{2,1,0:T(2,128)S(1)}, f32[4,2,128]{2,1,0:T(2,128)S(1)}) fusion(f32[4,256,128]{2,1,0:T(8,128)} %param.3), kind=kLoop, calls=%fused_computation.107 | loop fusion | bytes 16384 | tf_op jit(solution)/shard_map/slice | solution.py:13
  7.8 4.6 %collective-permute-start = (f32[4,2,128]{2,1,0:T(2,128)S(1)}, f32[4,2,128]{2,1,0:T(2,128)S(1)}, u32[]{:S(2)}, u32[]{:S(2)}) collective-permute-start(f32[4,2,128]{2,1,0:T(2,128)S(1)} %get-tuple-element.48), channel_id=1, source_target_pairs={{16,0},{32,16},{48,32},{64,48},{80,64},{96,80},{112,96},{128,112},... | collective-permute-start | bytes 12296 | tf_op jit(solution)/shard_map/ppermute | solution.py:19
  12.4 1.9 %collective-permute-start.1 = (f32[4,2,128]{2,1,0:T(2,128)S(1)}, f32[4,2,128]{2,1,0:T(2,128)S(1)}, u32[]{:S(2)}, u32[]{:S(2)}) collective-permute-start(f32[4,2,128]{2,1,0:T(2,128)S(1)} %get-tuple-element.49), channel_id=1, source_target_pairs={{0,16},{16,32},{32,48},{48,64},{64,80},{80,96},{96,112},{112,128},... | collective-permute-start | bytes 12296 | tf_op jit(solution)/shard_map/ppermute | solution.py:17
  14.4 0.2 fusion.33
  14.6 0.0 collective-permute-done.3
  14.7 0.1 constant_dynamic-update-slice_fusion.3
  14.8 0.0 collective-permute-done.2
  14.8 0.6 %collective-permute-done.1 = f32[4,2,128]{2,1,0:T(2,128)S(1)} collective-permute-done((f32[4,2,128]{2,1,0:T(2,128)S(1)}, f32[4,2,128]{2,1,0:T(2,128)S(1)}, u32[]{:S(2)}, u32[]{:S(2)}) %collective-permute-start.1) | collective-permute-done | bytes 4128 | tf_op jit(solution)/shard_map/ppermute | solution.py:17
  15.5 0.6 %copy-done.1 = f32[3,4,256,128]{3,2,1,0:T(8,128)S(1)} copy-done((f32[3,4,256,128]{3,2,1,0:T(8,128)S(1)}, f32[3,4,256,128]{3,2,1,0:T(8,128)}, u32[]{:S(2)}) %copy-start.1) | copy-done | bytes 1572888
  16.0 1.9 %fusion.10 = f32[4,256,128]{2,1,0:T(8,128)} fusion(f32[4,256,128]{2,1,0:T(8,128)S(1)} %copy-done, f32[4,2,128]{2,1,0:T(2,128)S(1)} %collective-permute-done.1, f32[4,258,128]{2,1,0:T(8,128)S(1)} %constant_dynamic-update-slice_fusion, f32[4,256,2]{2,1,0:T(8,128)S(1)} %get-tuple-element.47, f32[4,256,2]{2,1,0:T(8,128)S(1)} %get-tuple-element.46, ...), kind=kLoop, calls=%fused_computation.20 | loop fusion | flops 6029312 | bytes 5787648 | tf_op jit(solution)/shard_map/add | solution.py:44
  17.9 4.7 %shard_map.37 = (f32[1024,128]{1,0:T(8,128)}, f32[1024,128]{1,0:T(8,128)}, f32[1024,128]{1,0:T(8,128)}) custom-call(f32[1024,128]{1,0:T(8,128)} %bitcast.64, f32[1024,128]{1,0:T(8,128)} %bitcast.57), custom_call_target="tpu_custom_call" | custom-call | tf_op jit(solution)/shard_map/pallas_call | solution.py:169
  22.7 1.0 %fusion.27 = (f32[4,2,1,128]{3,2,1,0:T(1,128)S(1)}, f32[4,2,1,128]{3,2,1,0:T(1,128)S(1)}, f32[4,2,1,128]{3,2,1,0:T(1,128)S(1)}, f32[4,2,1,128]{3,2,1,0:T(1,128)S...) fusion(f32[4,2,128,128]{3,2,1,0:T(8,128)} %bitcast.66, ...), kind=kLoop, calls=%fused_computation.87 | loop fusion | flops 18432 | bytes 73744 | tf_op jit(solution)/shard_map/add | solution.py:202
  23.6 0.1 stack.2
  23.7 21.0 %all_gather.3 = f32[4,256,128]{2,1,0:T(8,128)S(1)} all-gather(f32[4,16,128]{2,1,0:T(8,128)S(1)} %bitcast.72), channel_id=1, replica_groups=mesh['gx'=16,'gy'=16] {'gx'}, dimensions={1}, use_global_device_ids=true | all-gather | bytes 557056 | tf_op jit(solution)/shard_map/all_gather | solution.py:208
  44.7 0.2 fusion.31
  45.0 0.1 multiply_add_fusion.8
  45.2 0.1 multiply_add_fusion.7
  45.4 0.1 multiply_add_fusion.6
  45.5 0.1 multiply_add_fusion.5
  45.7 0.1 multiply_add_fusion.4
  45.9 0.1 multiply_add_fusion.3
  46.0 0.1 multiply_add_fusion.2
  46.1 0.1 multiply_add_fusion.1
  46.3 0.1 multiply_add_fusion
  46.4 0.1 fusion.23
  46.5 0.8 %copy-done.2 = f32[1024,128]{1,0:T(8,128)S(1)} copy-done((f32[1024,128]{1,0:T(8,128)S(1)}, f32[1024,128]{1,0:T(8,128)}, u32[]{:S(2)}) %copy-start.2) | copy-done | bytes 524312
  47.3 0.2 copy-done.3
  47.4 0.2 copy-done.4
  47.6 0.9 %bitcast_select_fusion.1 = f32[4,256,128]{2,1,0:T(8,128)} fusion(f32[4,256,128]{2,1,0:T(8,128)S(1)} %bitcast.71, f32[4,256,128]{2,1,0:T(8,128)S(1)} %bitcast.67, f32[4,256,128]{2,1,0:T(8,128)S(1)} %bitcast.69, f32[4,2,128]{2,1,0:T(2,128)S(1)} %bitcast.75, f32[4,2,128]{2,1,0:T(2,128)S(1)} %bitcast.74, pred[256]{0:T(512)(128)(4,1)S(1)} %get-tuple-element.101, ...), kind=kLoop, calls=%fused_computation.6 | loop fusion | flops 786432 | bytes 2105856 | tf_op jit(solution)/shard_map/jit(_where)/select_n | solution.py:222
  (39 shorter events, 0.5 us)
Async XLA Ops:
  0.0 14.4 %copy-start = (f32[4,256,128]{2,1,0:T(8,128)S(1)}, f32[4,256,128]{2,1,0:T(8,128)}, u32[]{:S(2)}) copy-start(f32[4,256,128]{2,1,0:T(8,128)} %param.3) | copy-start | bytes 1572868
  1.1 13.5 %collective-permute-start.3 = (f32[2,256,128]{2,1,0:T(8,128)S(1)}, f32[2,256,128]{2,1,0:T(8,128)S(1)}, u32[]{:S(2)}, u32[]{:S(2)}) collective-permute-start(f32[2,256,128]{2,1,0:T(8,128)S(1)} %get-tuple-element.42), channel_id=1, source_target_pairs={{0,1},{1,2},{2,3},{3,4},{4,5},{5,6},{6,7},{7,8},{8,9},{9,10},{10,1... | collective-permute-start | bytes 786440 | tf_op jit(solution)/shard_map/ppermute | solution.py:17
  3.2 11.5 %collective-permute-start.2 = (f32[2,256,128]{2,1,0:T(8,128)S(1)}, f32[2,256,128]{2,1,0:T(8,128)S(1)}, u32[]{:S(2)}, u32[]{:S(2)}) collective-permute-start(f32[2,256,128]{2,1,0:T(8,128)S(1)} %get-tuple-element.41), channel_id=1, source_target_pairs={{1,0},{2,1},{3,2},{4,3},{5,4},{6,5},{7,6},{8,7},{9,8},{10,9},{11,1... | collective-permute-start | bytes 786440 | tf_op jit(solution)/shard_map/ppermute | solution.py:19
  7.8 7.0 %collective-permute-start = (f32[4,2,128]{2,1,0:T(2,128)S(1)}, f32[4,2,128]{2,1,0:T(2,128)S(1)}, u32[]{:S(2)}, u32[]{:S(2)}) collective-permute-start(f32[4,2,128]{2,1,0:T(2,128)S(1)} %get-tuple-element.48), channel_id=1, source_target_pairs={{16,0},{32,16},{48,32},{64,48},{80,64},{96,80},{112,96},{128,112},... | collective-permute-start | bytes 12296 | tf_op jit(solution)/shard_map/ppermute | solution.py:19
  12.4 3.1 %collective-permute-start.1 = (f32[4,2,128]{2,1,0:T(2,128)S(1)}, f32[4,2,128]{2,1,0:T(2,128)S(1)}, u32[]{:S(2)}, u32[]{:S(2)}) collective-permute-start(f32[4,2,128]{2,1,0:T(2,128)S(1)} %get-tuple-element.49), channel_id=1, source_target_pairs={{0,16},{16,32},{32,48},{48,64},{64,80},{80,96},{96,112},{112,128},... | collective-permute-start | bytes 12296 | tf_op jit(solution)/shard_map/ppermute | solution.py:17
  14.6 1.4 %copy-start.1 = (f32[3,4,256,128]{3,2,1,0:T(8,128)S(1)}, f32[3,4,256,128]{3,2,1,0:T(8,128)}, u32[]{:S(2)}) copy-start(f32[3,4,256,128]{3,2,1,0:T(8,128)} %param.4) | copy-start | bytes 4718596
  46.2 1.0 %copy-start.2 = (f32[1024,128]{1,0:T(8,128)S(1)}, f32[1024,128]{1,0:T(8,128)}, u32[]{:S(2)}) copy-start(f32[1024,128]{1,0:T(8,128)} %get-tuple-element.10) | copy-start | bytes 1572868
  46.3 1.2 %copy-start.3 = (f32[1024,128]{1,0:T(8,128)S(1)}, f32[1024,128]{1,0:T(8,128)}, u32[]{:S(2)}) copy-start(f32[1024,128]{1,0:T(8,128)} %get-tuple-element.8) | copy-start | bytes 1572868
  46.3 1.3 %copy-start.4 = (f32[1024,128]{1,0:T(8,128)S(1)}, f32[1024,128]{1,0:T(8,128)}, u32[]{:S(2)}) copy-start(f32[1024,128]{1,0:T(8,128)} %get-tuple-element.9) | copy-start | bytes 1572868

commit v11 on v10

--- a/solution.py
+++ b/solution.py
@@ -1,3 +1,5 @@
+import functools
+
 import jax
 import jax.numpy as jnp
 from jax import lax
@@ -172,6 +174,56 @@
         scratch_shapes=[scratch, scratch, scratch],
     )(rate.reshape(planes * length, lanes), right.reshape(planes * length, lanes))
     return tuple(out.reshape(planes, chunks, rows, lanes) for out in outs)
+
+
+def finish_kernel(chunks, place_ref, system_ref, part_ref, first_ref, last_ref, out_ref, ratio_ref, value_ref):
+    count, planes, lanes = ratio_ref.shape
+    width = system_ref.shape[0] // planes
+    length = part_ref.shape[0] // planes
+    rows = length // chunks
+
+    def coefficient(row, kind):
+        return system_ref[pl.ds((row // 2) * 8 + kind * 2 + row % 2, planes, stride=width)]
+
+    ratio = value = None
+    for row in range(count):
+        sub, diag, upper, right = (coefficient(row, kind) for kind in range(4))
+        if row == 0:
+            inverse = 1.0 / diag
+            value = right * inverse
+        else:
+            inverse = 1.0 / (diag - sub * ratio)
+            value = (right - sub * value) * inverse
+        ratio = upper * inverse
+        ratio_ref[row] = ratio
+        value_ref[row] = value
+    for row in range(count - 2, -1, -1):
+        value = value_ref[row] - ratio_ref[row] * value
+        value_ref[row] = value
+    own = place_ref[0] * (2 * chunks)
+    for chunk in range(chunks):
+        for plane in range(planes):
+            start_value = value_ref[own + 2 * chunk, pl.ds(plane, 1), :]
+            end_value = value_ref[own + 2 * chunk + 1, pl.ds(plane, 1), :]
+            offset = plane * length + chunk * rows
+            block = pl.ds(offset, rows)
+            out_ref[block] = part_ref[block] + first_ref[block] * start_value + last_ref[block] * end_value
+            out_ref[pl.ds(offset, 1)] = start_value
+            out_ref[pl.ds(offset + rows - 1, 1)] = end_value
+
+
+def finish(place, system, part, first, last, chunks):
+    planes, width, lanes = system.shape
+    count = width // 8 * 2
+    table = pltpu.VMEM((count, planes, lanes), jnp.float32)
+    return pl.pallas_call(
+        functools.partial(finish_kernel, chunks),
+        out_shape=jax.ShapeDtypeStruct(part.shape, jnp.float32),
+        in_specs=[pl.BlockSpec(memory_space=pltpu.SMEM)]
+        + [pl.BlockSpec(memory_space=pltpu.VMEM)] * 4,
+        out_specs=pl.BlockSpec(memory_space=pltpu.VMEM),
+        scratch_shapes=[table, table],
+    )(place.reshape(1).astype(jnp.int32), system.reshape(planes * width, lanes), part, first, last)
 
 
 def shards(field, courant, diffusion_number):
@@ -206,21 +258,10 @@
     lanes = stacked.shape[-1]
     stacked = stacked.reshape(planes, chunks * 8, lanes)
     gathered = lax.all_gather(stacked, "gx", axis=1, tiled=True)
-    gathered = gathered.reshape(planes, device_count, chunks, 4, 2, lanes)
-    gathered_lower_band, gathered_diagonal, gathered_upper_band, gathered_rhs = (
-        gathered[:, :, :, k].reshape(planes, 2 * chunks * device_count, lanes) for k in range(4)
-    )
-    boundary_rows_gathered = parallel_cyclic_reduction(
-        gathered_lower_band, gathered_diagonal, gathered_upper_band, (gathered_rhs,), 1
-    )[0]
-    ends = lax.dynamic_slice_in_dim(boundary_rows_gathered, 2 * chunks * place, 2 * chunks, 1)
-    ends = ends.reshape(planes, chunks, 2, 1, lanes)
-    start_value, end_value = ends[:, :, 0], ends[:, :, 1]
-    solved = part + first * start_value + last * end_value
-    row = lax.broadcasted_iota(jnp.int32, (1, 1, rows, 1), 2)
-    solved = jnp.where(row == 0, start_value, solved)
-    solved = jnp.where(row == rows - 1, end_value, solved)
-    return solved.reshape(planes, chunks * rows, lanes)
+    length = field.shape[1]
+    flat = [value.reshape(planes * length, lanes) for value in (part, first, last)]
+    solved = finish(place, gathered, *flat, chunks)
+    return solved.reshape(planes, length, lanes)
 
 
 def solution(mesh):

time: 48.9 us -> 49.5 us (1.012)
  Pallas kernels: 4.71 us -> 7.81 us
  other arithmetic: 4.74 us -> 2.9 us
  local copies, waits for them, and re-layouts: 4.61 us -> 2.8 us
  blocking collectives: 21 us -> 22.4 us
    pallas_call x0 -> x1, Pallas kernels: none -> 3.11 us  [finish(): pl.pallas_call(functools.partial(finish_kernel, chunks), out_shape=jax.Sh...]
    all_gather x1, blocking collectives: 21 us -> 22.4 us  [shards(): gathered = lax.all_gather(stacked, 'gx', axis=1, tiled=True)]
    unnamed x12 -> x6, local copies, waits for them, and re-layouts: 1.79 us -> 0.64 us
    select_n x1 -> x0, other arithmetic: 0.94 us -> none  [shards(): solved = jnp.where(row == rows - 1, end_value, solved)]
    add x9 -> x0, other arithmetic: 0.84 us -> none  [the longest x4 0.46 us: combine_rows(): value + factor_low * lower_value + factor_high * upper_value]
    slice x26 -> x0, local copies, waits for them, and re-layouts: 0.65 us -> none  [the longest x1 0.24 us: shards(): gathered[:, :, :, k].reshape(planes, 2 * chunks * device_count, lanes)]
where the time goes in v11:
time: 49.5 us; the launch traced here: 49.2 us
  blocking collectives  22.4 us (45%)
  starting transfers between devices  12.4 us (25%)
  Pallas kernels  7.81 us (16%)
  other arithmetic  2.9 us (6%)
  local copies, waits for them, and re-layouts  2.8 us (6%)
  waiting for transfers between devices  0.69 us (1%)
    all_gather x1, blocking collectives, shards(): gathered = lax.all_gather(stacked, 'gx', axis=1, tiled=True)  22.4 us
    ppermute x2, starting transfers between devices, padded_2(): lax.ppermute(head, axis, [((i + 1) % count, i) for i in range(ends)])  8.41 us
    pallas_call x1, Pallas kernels, local_solve(): pl.pallas_call(thomas_kernel, out_shape=(flat, flat, flat), scratch_shape...  4.7 us
    ppermute x2, starting transfers between devices, padded_2(): lax.ppermute(tail, axis, [(i, (i + 1) % count) for i in range(ends)])  4.03 us
    pallas_call x1, Pallas kernels, finish(): pl.pallas_call(functools.partial(finish_kernel, chunks), out_shape=jax.Sh...  3.11 us
    add x1, other arithmetic, build_rhs(): field - transport + 0.05 * (curve_y + curve_z)  1.92 us
    slice x2, local copies, waits for them, and re-layouts, padded_2(): head = lax.slice_in_dim(cells, 0, width, axis=dim)  1.87 us
  transfers between devices with their start and end apart: 4, of which 1 were waited for; matrix products, arithmetic and copies ran while one was open for 2% of the time, Pallas kernels for 0%

profile of v11, /device:TPU:1, one launch (start us, length us, event | category | flops | bytes accessed | tf_op | source)
XLA Modules:
  0.0 49.2 jit_solution(3381287845027108900)
XLA Ops:
  0.0 0.0 copy-start
  0.0 1.1 %fusion.18 = (f32[2,256,128]{2,1,0:T(8,128)S(1)}, f32[2,256,128]{2,1,0:T(8,128)S(1)}) fusion(f32[4,256,128]{2,1,0:T(8,128)} %param.3), kind=kLoop, calls=%fused_computation.45 | loop fusion | bytes 1048576 | tf_op jit(solution)/shard_map/slice | solution.py:15
  1.1 2.1 %collective-permute-start.3 = (f32[2,256,128]{2,1,0:T(8,128)S(1)}, f32[2,256,128]{2,1,0:T(8,128)S(1)}, u32[]{:S(2)}, u32[]{:S(2)}) collective-permute-start(f32[2,256,128]{2,1,0:T(8,128)S(1)} %get-tuple-element.24), channel_id=1, source_target_pairs={{0,1},{1,2},{2,3},{3,4},{4,5},{5,6},{6,7},{7,8},{8,9},{9,10},{10,1... | collective-permute-start | bytes 786440 | tf_op jit(solution)/shard_map/ppermute | solution.py:19
  3.2 3.8 %collective-permute-start.2 = (f32[2,256,128]{2,1,0:T(8,128)S(1)}, f32[2,256,128]{2,1,0:T(8,128)S(1)}, u32[]{:S(2)}, u32[]{:S(2)}) collective-permute-start(f32[2,256,128]{2,1,0:T(8,128)S(1)} %get-tuple-element.23), channel_id=1, source_target_pairs={{1,0},{2,1},{3,2},{4,3},{5,4},{6,5},{7,6},{8,7},{9,8},{10,9},{11,1... | collective-permute-start | bytes 786440 | tf_op jit(solution)/shard_map/ppermute | solution.py:21
  7.0 0.7 %fusion.20 = (f32[4,2,128]{2,1,0:T(2,128)S(1)}, f32[4,2,128]{2,1,0:T(2,128)S(1)}) fusion(f32[4,256,128]{2,1,0:T(8,128)} %param.3), kind=kLoop, calls=%fused_computation.47 | loop fusion | bytes 16384 | tf_op jit(solution)/shard_map/slice | solution.py:15
  7.8 4.6 %collective-permute-start = (f32[4,2,128]{2,1,0:T(2,128)S(1)}, f32[4,2,128]{2,1,0:T(2,128)S(1)}, u32[]{:S(2)}, u32[]{:S(2)}) collective-permute-start(f32[4,2,128]{2,1,0:T(2,128)S(1)} %get-tuple-element.30), channel_id=1, source_target_pairs={{16,0},{32,16},{48,32},{64,48},{80,64},{96,80},{112,96},{128,112},... | collective-permute-start | bytes 12296 | tf_op jit(solution)/shard_map/ppermute | solution.py:21
  12.4 1.9 %collective-permute-start.1 = (f32[4,2,128]{2,1,0:T(2,128)S(1)}, f32[4,2,128]{2,1,0:T(2,128)S(1)}, u32[]{:S(2)}, u32[]{:S(2)}) collective-permute-start(f32[4,2,128]{2,1,0:T(2,128)S(1)} %get-tuple-element.31), channel_id=1, source_target_pairs={{0,16},{16,32},{32,48},{48,64},{64,80},{80,96},{96,112},{112,128},... | collective-permute-start | bytes 12296 | tf_op jit(solution)/shard_map/ppermute | solution.py:19
  14.4 0.0 copy-done
  14.4 0.2 fusion.19
  14.6 0.0 copy-start.1
  14.6 0.0 collective-permute-done.3
  14.6 0.1 constant_dynamic-update-slice_fusion.3
  14.7 0.0 collective-permute-done.2
  14.8 0.0 collective-permute-done
  14.8 0.7 %collective-permute-done.1 = f32[4,2,128]{2,1,0:T(2,128)S(1)} collective-permute-done((f32[4,2,128]{2,1,0:T(2,128)S(1)}, f32[4,2,128]{2,1,0:T(2,128)S(1)}, u32[]{:S(2)}, u32[]{:S(2)}) %collective-permute-start.1) | collective-permute-done | bytes 4128 | tf_op jit(solution)/shard_map/ppermute | solution.py:19
  15.5 0.5 %copy-done.1 = f32[3,4,256,128]{3,2,1,0:T(8,128)S(1)} copy-done((f32[3,4,256,128]{3,2,1,0:T(8,128)S(1)}, f32[3,4,256,128]{3,2,1,0:T(8,128)}, u32[]{:S(2)}) %copy-start.1) | copy-done | bytes 1572888
  16.0 1.9 %fusion.10 = f32[4,256,128]{2,1,0:T(8,128)} fusion(f32[4,256,128]{2,1,0:T(8,128)S(1)} %copy-done, f32[4,2,128]{2,1,0:T(2,128)S(1)} %collective-permute-done.1, f32[4,258,128]{2,1,0:T(8,128)S(1)} %constant_dynamic-update-slice_fusion, f32[4,256,2]{2,1,0:T(8,128)S(1)} %get-tuple-element.29, f32[4,256,2]{2,1,0:T(8,128)S(1)} %get-tuple-element.28, ...), kind=kLoop, calls=%fused_computation.16 | loop fusion | flops 6029312 | bytes 5787648 | tf_op jit(solution)/shard_map/add | solution.py:46
  17.9 4.7 %shard_map.37 = (f32[1024,128]{1,0:T(8,128)}, f32[1024,128]{1,0:T(8,128)}, f32[1024,128]{1,0:T(8,128)}) custom-call(f32[1024,128]{1,0:T(8,128)} %bitcast.24, f32[1024,128]{1,0:T(8,128)} %bitcast.21), custom_call_target="tpu_custom_call" | custom-call | tf_op jit(solution)/shard_map/pallas_call | solution.py:171
  22.6 1.0 %fusion.14 = (f32[4,2,1,128]{3,2,1,0:T(1,128)S(1)}, f32[4,2,1,128]{3,2,1,0:T(1,128)S(1)}, f32[4,2,1,128]{3,2,1,0:T(1,128)S(1)}, f32[4,2,1,128]{3,2,1,0:T(1,128)S...) fusion(f32[4,2,128,128]{3,2,1,0:T(8,128)} %bitcast.26, ...), kind=kLoop, calls=%fused_computation.32 | loop fusion | flops 18432 | bytes 73744 | tf_op jit(solution)/shard_map/add | solution.py:254
  23.6 0.1 stack.2
  23.6 22.4 %all_gather.3 = f32[4,256,128]{2,1,0:T(8,128)} all-gather(f32[4,16,128]{2,1,0:T(8,128)S(1)} %bitcast.29), channel_id=1, replica_groups=mesh['gx'=16,'gy'=16] {'gx'}, dimensions={1}, use_global_device_ids=true | all-gather | bytes 557056 | tf_op jit(solution)/shard_map/all_gather | solution.py:260
  46.1 3.1 %shard_map.38 = f32[1024,128]{1,0:T(8,128)} custom-call(s32[1]{0:T(128)} %bitcast.place_ref, f32[1024,128]{1,0:T(8,128)} %bitcast.23, f32[1024,128]{1,0:T(8,128)} %get-tuple-element.10.part_ref, f32[1024,128]{1,0:T(8,128)} %get-tuple-element.8.first_ref, f32[1024,128]{1,0:T(8,128)} %get-tuple-element.9.last_ref), custom_call_target="tpu_custom_call" | custom-call | tf_op jit(solution)/shard_map/pallas_call | solution.py:219
  (4 shorter events, 0.1 us)
Async XLA Ops:
  0.0 14.4 %copy-start = (f32[4,256,128]{2,1,0:T(8,128)S(1)}, f32[4,256,128]{2,1,0:T(8,128)}, u32[]{:S(2)}) copy-start(f32[4,256,128]{2,1,0:T(8,128)} %param.3) | copy-start | bytes 1572868
  1.1 13.4 %collective-permute-start.3 = (f32[2,256,128]{2,1,0:T(8,128)S(1)}, f32[2,256,128]{2,1,0:T(8,128)S(1)}, u32[]{:S(2)}, u32[]{:S(2)}) collective-permute-start(f32[2,256,128]{2,1,0:T(8,128)S(1)} %get-tuple-element.24), channel_id=1, source_target_pairs={{0,1},{1,2},{2,3},{3,4},{4,5},{5,6},{6,7},{7,8},{8,9},{9,10},{10,1... | collective-permute-start | bytes 786440 | tf_op jit(solution)/shard_map/ppermute | solution.py:19
  3.2 11.5 %collective-permute-start.2 = (f32[2,256,128]{2,1,0:T(8,128)S(1)}, f32[2,256,128]{2,1,0:T(8,128)S(1)}, u32[]{:S(2)}, u32[]{:S(2)}) collective-permute-start(f32[2,256,128]{2,1,0:T(8,128)S(1)} %get-tuple-element.23), channel_id=1, source_target_pairs={{1,0},{2,1},{3,2},{4,3},{5,4},{6,5},{7,6},{8,7},{9,8},{10,9},{11,1... | collective-permute-start | bytes 786440 | tf_op jit(solution)/shard_map/ppermute | solution.py:21
  7.8 7.0 %collective-permute-start = (f32[4,2,128]{2,1,0:T(2,128)S(1)}, f32[4,2,128]{2,1,0:T(2,128)S(1)}, u32[]{:S(2)}, u32[]{:S(2)}) collective-permute-start(f32[4,2,128]{2,1,0:T(2,128)S(1)} %get-tuple-element.30), channel_id=1, source_target_pairs={{16,0},{32,16},{48,32},{64,48},{80,64},{96,80},{112,96},{128,112},... | collective-permute-start | bytes 12296 | tf_op jit(solution)/shard_map/ppermute | solution.py:21
  12.4 3.1 %collective-permute-start.1 = (f32[4,2,128]{2,1,0:T(2,128)S(1)}, f32[4,2,128]{2,1,0:T(2,128)S(1)}, u32[]{:S(2)}, u32[]{:S(2)}) collective-permute-start(f32[4,2,128]{2,1,0:T(2,128)S(1)} %get-tuple-element.31), channel_id=1, source_target_pairs={{0,16},{16,32},{32,48},{48,64},{64,80},{80,96},{96,112},{112,128},... | collective-permute-start | bytes 12296 | tf_op jit(solution)/shard_map/ppermute | solution.py:19
  14.6 1.4 %copy-start.1 = (f32[3,4,256,128]{3,2,1,0:T(8,128)S(1)}, f32[3,4,256,128]{3,2,1,0:T(8,128)}, u32[]{:S(2)}) copy-start(f32[3,4,256,128]{3,2,1,0:T(8,128)} %param.4) | copy-start | bytes 4718596

commit v12 on v11

--- a/solution.py
+++ b/solution.py
@@ -108,7 +108,10 @@
     return tuple((value / main_diagonal for value in right_hand_sides))
 
 
-def thomas_kernel(rate_ref, right_ref, part_ref, first_ref, last_ref, ratio_ref, ahead_ref, lead_ref):
+def thomas_kernel(
+    chunks, devices, place_ref, rate_ref, right_ref,
+    part_ref, first_ref, last_ref, system_ref, ratio_ref, ahead_ref, lead_ref,
+):
     rows = ratio_ref.shape[0]
     sublanes = ratio_ref.shape[1]
 
@@ -157,23 +160,46 @@
         last_ref[at(i)] = last
         return part, first, last
 
-    lax.fori_loop(0, rows - 3, backward, (part, first, last), unroll=True)
+    part, first, last = lax.fori_loop(0, rows - 3, backward, (part, first, last), unroll=True)
     for ref in (part_ref, first_ref, last_ref):
         ref[at(0)] = zero
         ref[at(rows - 1)] = zero
-
-
-def local_solve(rate, right, chunks):
+    place = place_ref[0]
+    chunk_of = lax.broadcasted_iota(jnp.int32, zero.shape, 0) % chunks
+    low_open = (place > 0).astype(jnp.float32)
+    high_open = (place < devices - 1).astype(jnp.float32)
+    low_scale = jnp.where(chunk_of == 0, low_open, 1.0)
+    high_scale = jnp.where(chunk_of == chunks - 1, high_open, 1.0)
+    rate_first, rate_last = rate_ref[at(0)], rate_ref[at(rows - 1)]
+    part_end, first_end, last_end = (ref[at(rows - 2)] for ref in (part_ref, first_ref, last_ref))
+    equations = [
+        -rate_first * low_scale,
+        -rate_last * first_end,
+        (1.0 + 2.0 * rate_first) - rate_first * first,
+        (1.0 + 2.0 * rate_last) - rate_last * last_end,
+        -rate_first * last,
+        -rate_last * high_scale,
+        right_ref[at(0)] + rate_first * part,
+        right_ref[at(rows - 1)] + rate_last * part_end,
+    ]
+    for index, equation in enumerate(equations):
+        system_ref[pl.ds(index, sublanes, stride=len(equations))] = equation
+
+
+def local_solve(place, devices, rate, right, chunks):
     planes, length, lanes = rate.shape
     rows = length // chunks
     flat = jax.ShapeDtypeStruct((planes * length, lanes), jnp.float32)
     scratch = pltpu.VMEM((rows, planes * chunks, lanes), jnp.float32)
-    outs = pl.pallas_call(
-        thomas_kernel,
-        out_shape=(flat, flat, flat),
+    system = jax.ShapeDtypeStruct((planes * chunks * 8, lanes), jnp.float32)
+    return pl.pallas_call(
+        functools.partial(thomas_kernel, chunks, devices),
+        out_shape=(flat, flat, flat, system),
+        in_specs=[pl.BlockSpec(memory_space=pltpu.SMEM)]
+        + [pl.BlockSpec(memory_space=pltpu.VMEM)] * 2,
+        out_specs=tuple(pl.BlockSpec(memory_space=pltpu.VMEM) for _ in range(4)),
         scratch_shapes=[scratch, scratch, scratch],
-    )(rate.reshape(planes * length, lanes), right.reshape(planes * length, lanes))
-    return tuple(out.reshape(planes, chunks, rows, lanes) for out in outs)
+    )(place.reshape(1).astype(jnp.int32), rate.reshape(planes * length, lanes), right.reshape(planes * length, lanes))
 
 
 def finish_kernel(chunks, place_ref, system_ref, part_ref, first_ref, last_ref, out_ref, ratio_ref, value_ref):
@@ -234,33 +260,12 @@
     place = lax.axis_index("gx")
     device_count = lax.axis_size("gx")
     planes = field.shape[0]
-    part, first, last = local_solve(diffusion_number, rhs, chunks)
-    rows = part.shape[2]
-    rate = diffusion_number.reshape(planes, chunks, rows, -1)
-    right = rhs.reshape(planes, chunks, rows, -1)
-    low_open = (place > 0).astype(jnp.float32)
-    high_open = (place < device_count - 1).astype(jnp.float32)
-    chunk_of = lax.broadcasted_iota(jnp.int32, (1, chunks, 1), 1)
-    low_scale = jnp.where(chunk_of == 0, low_open, 1.0)
-    high_scale = jnp.where(chunk_of == chunks - 1, high_open, 1.0)
-    rate_first, rate_last = rate[:, :, 0], rate[:, :, rows - 1]
-    sub_first = -rate_first * low_scale
-    diag_first = (1.0 + 2.0 * rate_first) - rate_first * first[:, :, 1]
-    super_first = -rate_first * last[:, :, 1]
-    right_first = right[:, :, 0] + rate_first * part[:, :, 1]
-    sub_last = -rate_last * first[:, :, rows - 2]
-    diag_last = (1.0 + 2.0 * rate_last) - rate_last * last[:, :, rows - 2]
-    super_last = -rate_last * high_scale
-    right_last = right[:, :, rows - 1] + rate_last * part[:, :, rows - 2]
-    stacked = jnp.stack(
-        [sub_first, sub_last, diag_first, diag_last, super_first, super_last, right_first, right_last], 2
-    )
-    lanes = stacked.shape[-1]
-    stacked = stacked.reshape(planes, chunks * 8, lanes)
+    part, first, last, system = local_solve(place, device_count, diffusion_number, rhs, chunks)
+    lanes = field.shape[-1]
+    stacked = system.reshape(planes, chunks * 8, lanes)
     gathered = lax.all_gather(stacked, "gx", axis=1, tiled=True)
     length = field.shape[1]
-    flat = [value.reshape(planes * length, lanes) for value in (part, first, last)]
-    solved = finish(place, gathered, *flat, chunks)
+    solved = finish(place, gathered, part, first, last, chunks)
     return solved.reshape(planes, length, lanes)
 
 

time: 49.5 us -> 48.7 us (0.984)
  other arithmetic: 2.9 us -> 1.92 us
    add x1 -> x0, other arithmetic: 0.98 us -> none  [shards(): right_last = right[:, :, rows - 1] + rate_last * part[:, :, rows - 2]]
where the time goes in v12:
time: 48.7 us; the launch traced here: 48.4 us
  blocking collectives  22.7 us (47%)
  starting transfers between devices  12.4 us (25%)
  Pallas kernels  7.83 us (16%)
  local copies, waits for them, and re-layouts  2.72 us (6%)
  other arithmetic  1.92 us (4%)
  waiting for transfers between devices  0.7 us (1%)
    all_gather x1, blocking collectives, shards(): gathered = lax.all_gather(stacked, 'gx', axis=1, tiled=True)  22.7 us
    ppermute x2, starting transfers between devices, padded_2(): lax.ppermute(head, axis, [((i + 1) % count, i) for i in range(ends)])  8.41 us
    pallas_call x1, Pallas kernels, local_solve(): pl.pallas_call(functools.partial(thomas_kernel, chunks, devices), out_sha...  4.72 us
    ppermute x2, starting transfers between devices, padded_2(): lax.ppermute(tail, axis, [(i, (i + 1) % count) for i in range(ends)])  4.03 us
    pallas_call x1, Pallas kernels, finish(): pl.pallas_call(functools.partial(finish_kernel, chunks), out_shape=jax.Sh...  3.11 us
    add x1, other arithmetic, build_rhs(): field - transport + 0.05 * (curve_y + curve_z)  1.92 us
    slice x2, local copies, waits for them, and re-layouts, padded_2(): head = lax.slice_in_dim(cells, 0, width, axis=dim)  1.87 us
  transfers between devices with their start and end apart: 4, of which 1 were waited for; matrix products, arithmetic and copies ran while one was open for 2% of the time, Pallas kernels for 0%

profile of v12, /device:TPU:1, one launch (start us, length us, event | category | flops | bytes accessed | tf_op | source)
XLA Modules:
  0.0 48.4 jit_solution(1535733607602531689)
XLA Ops:
  0.0 0.0 copy-start
  0.0 1.1 %fusion.14 = (f32[2,256,128]{2,1,0:T(8,128)S(1)}, f32[2,256,128]{2,1,0:T(8,128)S(1)}) fusion(f32[4,256,128]{2,1,0:T(8,128)} %param.3), kind=kLoop, calls=%fused_computation.31 | loop fusion | bytes 1048576 | tf_op jit(solution)/shard_map/slice | solution.py:15
  1.1 2.1 %collective-permute-start.3 = (f32[2,256,128]{2,1,0:T(8,128)S(1)}, f32[2,256,128]{2,1,0:T(8,128)S(1)}, u32[]{:S(2)}, u32[]{:S(2)}) collective-permute-start(f32[2,256,128]{2,1,0:T(8,128)S(1)} %get-tuple-element.14), channel_id=1, source_target_pairs={{0,1},{1,2},{2,3},{3,4},{4,5},{5,6},{6,7},{7,8},{8,9},{9,10},{10,1... | collective-permute-start | bytes 786440 | tf_op jit(solution)/shard_map/ppermute | solution.py:19
  3.2 3.8 %collective-permute-start.2 = (f32[2,256,128]{2,1,0:T(8,128)S(1)}, f32[2,256,128]{2,1,0:T(8,128)S(1)}, u32[]{:S(2)}, u32[]{:S(2)}) collective-permute-start(f32[2,256,128]{2,1,0:T(8,128)S(1)} %get-tuple-element.13), channel_id=1, source_target_pairs={{1,0},{2,1},{3,2},{4,3},{5,4},{6,5},{7,6},{8,7},{9,8},{10,9},{11,1... | collective-permute-start | bytes 786440 | tf_op jit(solution)/shard_map/ppermute | solution.py:21
  7.0 0.7 %fusion.16 = (f32[4,2,128]{2,1,0:T(2,128)S(1)}, f32[4,2,128]{2,1,0:T(2,128)S(1)}) fusion(f32[4,256,128]{2,1,0:T(8,128)} %param.3), kind=kLoop, calls=%fused_computation.33 | loop fusion | bytes 16384 | tf_op jit(solution)/shard_map/slice | solution.py:15
  7.8 4.6 %collective-permute-start = (f32[4,2,128]{2,1,0:T(2,128)S(1)}, f32[4,2,128]{2,1,0:T(2,128)S(1)}, u32[]{:S(2)}, u32[]{:S(2)}) collective-permute-start(f32[4,2,128]{2,1,0:T(2,128)S(1)} %get-tuple-element.20), channel_id=1, source_target_pairs={{16,0},{32,16},{48,32},{64,48},{80,64},{96,80},{112,96},{128,112},... | collective-permute-start | bytes 12296 | tf_op jit(solution)/shard_map/ppermute | solution.py:21
  12.4 1.9 %collective-permute-start.1 = (f32[4,2,128]{2,1,0:T(2,128)S(1)}, f32[4,2,128]{2,1,0:T(2,128)S(1)}, u32[]{:S(2)}, u32[]{:S(2)}) collective-permute-start(f32[4,2,128]{2,1,0:T(2,128)S(1)} %get-tuple-element.21), channel_id=1, source_target_pairs={{0,16},{16,32},{32,48},{48,64},{64,80},{80,96},{96,112},{112,128},... | collective-permute-start | bytes 12296 | tf_op jit(solution)/shard_map/ppermute | solution.py:19
  14.3 0.0 copy-done
  14.3 0.2 fusion.15
  14.6 0.0 copy-start.1
  14.6 0.0 collective-permute-done.3
  14.6 0.1 constant_dynamic-update-slice_fusion.3
  14.7 0.0 collective-permute-done.2
  14.8 0.0 collective-permute-done
  14.8 0.7 %collective-permute-done.1 = f32[4,2,128]{2,1,0:T(2,128)S(1)} collective-permute-done((f32[4,2,128]{2,1,0:T(2,128)S(1)}, f32[4,2,128]{2,1,0:T(2,128)S(1)}, u32[]{:S(2)}, u32[]{:S(2)}) %collective-permute-start.1) | collective-permute-done | bytes 4128 | tf_op jit(solution)/shard_map/ppermute | solution.py:19
  15.5 0.5 %copy-done.1 = f32[3,4,256,128]{3,2,1,0:T(8,128)S(1)} copy-done((f32[3,4,256,128]{3,2,1,0:T(8,128)S(1)}, f32[3,4,256,128]{3,2,1,0:T(8,128)}, u32[]{:S(2)}) %copy-start.1) | copy-done | bytes 1572888
  16.0 1.9 %fusion.10 = f32[4,256,128]{2,1,0:T(8,128)} fusion(f32[4,256,128]{2,1,0:T(8,128)S(1)} %copy-done, f32[4,2,128]{2,1,0:T(2,128)S(1)} %collective-permute-done.1, f32[4,258,128]{2,1,0:T(8,128)S(1)} %constant_dynamic-update-slice_fusion, f32[4,256,2]{2,1,0:T(8,128)S(1)} %get-tuple-element.19, f32[4,256,2]{2,1,0:T(8,128)S(1)} %get-tuple-element.18, ...), kind=kLoop, calls=%fused_computation.16 | loop fusion | flops 6029312 | bytes 5787648 | tf_op jit(solution)/shard_map/add | solution.py:46
  17.9 4.7 %shard_map.37 = (f32[1024,128]{1,0:T(8,128)}, f32[1024,128]{1,0:T(8,128)}, f32[1024,128]{1,0:T(8,128)}, f32[64,128]{1,0:T(8,128)}) custom-call(s32[1]{0:T(128)} %bitcast.place_ref, f32[1024,128]{1,0:T(8,128)} %bitcast.18, f32[1024,128]{1,0:T(8,128)} %bitcast.16), custom_call_target="tpu_custom_call" | custom-call | tf_op jit(solution)/shard_map/pallas_call | solution.py:195
  22.6 22.7 %all_gather.3 = f32[4,256,128]{2,1,0:T(8,128)} all-gather(f32[4,16,128]{2,1,0:T(8,128)} %bitcast.19), channel_id=1, replica_groups=mesh['gx'=16,'gy'=16] {'gx'}, dimensions={1}, use_global_device_ids=true | all-gather | bytes 557056 | tf_op jit(solution)/shard_map/all_gather | solution.py:266
  45.3 3.1 %shard_map.38 = f32[1024,128]{1,0:T(8,128)} custom-call(s32[1]{0:T(128)} %bitcast.place_ref, f32[1024,128]{1,0:T(8,128)} %bitcast.17, f32[1024,128]{1,0:T(8,128)} %get-tuple-element.10.part_ref, f32[1024,128]{1,0:T(8,128)} %get-tuple-element.11.first_ref, f32[1024,128]{1,0:T(8,128)} %get-tuple-element.12.last_ref), custom_call_target="tpu_custom_call" | custom-call | tf_op jit(solution)/shard_map/pallas_call | solution.py:245
  (3 shorter events, 0.0 us)
Async XLA Ops:
  0.0 14.3 %copy-start = (f32[4,256,128]{2,1,0:T(8,128)S(1)}, f32[4,256,128]{2,1,0:T(8,128)}, u32[]{:S(2)}) copy-start(f32[4,256,128]{2,1,0:T(8,128)} %param.3) | copy-start | bytes 1572868
  1.1 13.4 %collective-permute-start.3 = (f32[2,256,128]{2,1,0:T(8,128)S(1)}, f32[2,256,128]{2,1,0:T(8,128)S(1)}, u32[]{:S(2)}, u32[]{:S(2)}) collective-permute-start(f32[2,256,128]{2,1,0:T(8,128)S(1)} %get-tuple-element.14), channel_id=1, source_target_pairs={{0,1},{1,2},{2,3},{3,4},{4,5},{5,6},{6,7},{7,8},{8,9},{9,10},{10,1... | collective-permute-start | bytes 786440 | tf_op jit(solution)/shard_map/ppermute | solution.py:19
  3.2 11.5 %collective-permute-start.2 = (f32[2,256,128]{2,1,0:T(8,128)S(1)}, f32[2,256,128]{2,1,0:T(8,128)S(1)}, u32[]{:S(2)}, u32[]{:S(2)}) collective-permute-start(f32[2,256,128]{2,1,0:T(8,128)S(1)} %get-tuple-element.13), channel_id=1, source_target_pairs={{1,0},{2,1},{3,2},{4,3},{5,4},{6,5},{7,6},{8,7},{9,8},{10,9},{11,1... | collective-permute-start | bytes 786440 | tf_op jit(solution)/shard_map/ppermute | solution.py:21
  7.8 7.0 %collective-permute-start = (f32[4,2,128]{2,1,0:T(2,128)S(1)}, f32[4,2,128]{2,1,0:T(2,128)S(1)}, u32[]{:S(2)}, u32[]{:S(2)}) collective-permute-start(f32[4,2,128]{2,1,0:T(2,128)S(1)} %get-tuple-element.20), channel_id=1, source_target_pairs={{16,0},{32,16},{48,32},{64,48},{80,64},{96,80},{112,96},{128,112},... | collective-permute-start | bytes 12296 | tf_op jit(solution)/shard_map/ppermute | solution.py:21
  12.4 3.1 %collective-permute-start.1 = (f32[4,2,128]{2,1,0:T(2,128)S(1)}, f32[4,2,128]{2,1,0:T(2,128)S(1)}, u32[]{:S(2)}, u32[]{:S(2)}) collective-permute-start(f32[4,2,128]{2,1,0:T(2,128)S(1)} %get-tuple-element.21), channel_id=1, source_target_pairs={{0,16},{16,32},{32,48},{48,64},{64,80},{80,96},{96,112},{112,128},... | collective-permute-start | bytes 12296 | tf_op jit(solution)/shard_map/ppermute | solution.py:19
  14.6 1.4 %copy-start.1 = (f32[3,4,256,128]{3,2,1,0:T(8,128)S(1)}, f32[3,4,256,128]{3,2,1,0:T(8,128)}, u32[]{:S(2)}) copy-start(f32[3,4,256,128]{3,2,1,0:T(8,128)} %param.4) | copy-start | bytes 4718596

commit v13 on v12

--- a/solution.py
+++ b/solution.py
@@ -144,9 +144,9 @@
         2, rows - 1, forward, (ratio, part, first, zero), unroll=True
     )
     last = rate_ref[at(rows - 2)] * inverse
-    part_ref[at(rows - 2)] = part
-    first_ref[at(rows - 2)] = first
-    last_ref[at(rows - 2)] = last
+    part_ref[rows - 2] = part
+    first_ref[rows - 2] = first
+    last_ref[rows - 2] = last
 
     def backward(j, carry):
         part, first, last = carry
@@ -155,15 +155,15 @@
         part = ahead_ref[i] - ratio * part
         first = lead_ref[i] - ratio * first
         last = -ratio * last
-        part_ref[at(i)] = part
-        first_ref[at(i)] = first
-        last_ref[at(i)] = last
+        part_ref[i] = part
+        first_ref[i] = first
+        last_ref[i] = last
         return part, first, last
 
     part, first, last = lax.fori_loop(0, rows - 3, backward, (part, first, last), unroll=True)
     for ref in (part_ref, first_ref, last_ref):
-        ref[at(0)] = zero
-        ref[at(rows - 1)] = zero
+        ref[0] = zero
+        ref[rows - 1] = zero
     place = place_ref[0]
     chunk_of = lax.broadcasted_iota(jnp.int32, zero.shape, 0) % chunks
     low_open = (place > 0).astype(jnp.float32)
@@ -171,7 +171,7 @@
     low_scale = jnp.where(chunk_of == 0, low_open, 1.0)
     high_scale = jnp.where(chunk_of == chunks - 1, high_open, 1.0)
     rate_first, rate_last = rate_ref[at(0)], rate_ref[at(rows - 1)]
-    part_end, first_end, last_end = (ref[at(rows - 2)] for ref in (part_ref, first_ref, last_ref))
+    part_end, first_end, last_end = (ref[rows - 2] for ref in (part_ref, first_ref, last_ref))
     equations = [
         -rate_first * low_scale,
         -rate_last * first_end,
@@ -189,12 +189,12 @@
 def local_solve(place, devices, rate, right, chunks):
     planes, length, lanes = rate.shape
     rows = length // chunks
-    flat = jax.ShapeDtypeStruct((planes * length, lanes), jnp.float32)
+    table = jax.ShapeDtypeStruct((rows, planes * chunks, lanes), jnp.float32)
     scratch = pltpu.VMEM((rows, planes * chunks, lanes), jnp.float32)
     system = jax.ShapeDtypeStruct((planes * chunks * 8, lanes), jnp.float32)
     return pl.pallas_call(
         functools.partial(thomas_kernel, chunks, devices),
-        out_shape=(flat, flat, flat, system),
+        out_shape=(table, table, table, system),
         in_specs=[pl.BlockSpec(memory_space=pltpu.SMEM)]
         + [pl.BlockSpec(memory_space=pltpu.VMEM)] * 2,
         out_specs=tuple(pl.BlockSpec(memory_space=pltpu.VMEM) for _ in range(4)),
@@ -205,8 +205,8 @@
 def finish_kernel(chunks, place_ref, system_ref, part_ref, first_ref, last_ref, out_ref, ratio_ref, value_ref):
     count, planes, lanes = ratio_ref.shape
     width = system_ref.shape[0] // planes
-    length = part_ref.shape[0] // planes
-    rows = length // chunks
+    rows = part_ref.shape[0] // (planes * chunks)
+    length = rows * chunks
 
     def coefficient(row, kind):
         return system_ref[pl.ds((row // 2) * 8 + kind * 2 + row % 2, planes, stride=width)]
@@ -233,7 +233,10 @@
             end_value = value_ref[own + 2 * chunk + 1, pl.ds(plane, 1), :]
             offset = plane * length + chunk * rows
             block = pl.ds(offset, rows)
-            out_ref[block] = part_ref[block] + first_ref[block] * start_value + last_ref[block] * end_value
+            table = pl.ds(plane * chunks + chunk, rows, stride=planes * chunks)
+            out_ref[block] = (
+                part_ref[table] + first_ref[table] * start_value + last_ref[table] * end_value
+            )
             out_ref[pl.ds(offset, 1)] = start_value
             out_ref[pl.ds(offset + rows - 1, 1)] = end_value
 
@@ -244,12 +247,16 @@
     table = pltpu.VMEM((count, planes, lanes), jnp.float32)
     return pl.pallas_call(
         functools.partial(finish_kernel, chunks),
-        out_shape=jax.ShapeDtypeStruct(part.shape, jnp.float32),
+        out_shape=jax.ShapeDtypeStruct((part.shape[0] * part.shape[1], lanes), jnp.float32),
         in_specs=[pl.BlockSpec(memory_space=pltpu.SMEM)]
         + [pl.BlockSpec(memory_space=pltpu.VMEM)] * 4,
         out_specs=pl.BlockSpec(memory_space=pltpu.VMEM),
         scratch_shapes=[table, table],
-    )(place.reshape(1).astype(jnp.int32), system.reshape(planes * width, lanes), part, first, last)
+    )(
+        place.reshape(1).astype(jnp.int32),
+        system.reshape(planes * width, lanes),
+        *(value.reshape(-1, lanes) for value in (part, first, last)),
+    )
 
 
 def shards(field, courant, diffusion_number):

time: 48.7 us -> 48.1 us (0.988)
  Pallas kernels: 7.83 us -> 7.23 us
    pallas_call x1, Pallas kernels: 4.72 us -> 3.8 us  [local_solve(): pl.pallas_call(functools.partial(thomas_kernel, chunks, devices), out_sha...]
where the time goes in v13:
time: 48.1 us; the launch traced here: 47.8 us
  blocking collectives  22.7 us (47%)
  starting transfers between devices  12.4 us (26%)
  Pallas kernels  7.23 us (15%)
  local copies, waits for them, and re-layouts  2.72 us (6%)
  other arithmetic  1.92 us (4%)
  waiting for transfers between devices  0.7 us (1%)
    all_gather x1, blocking collectives, shards(): gathered = lax.all_gather(stacked, 'gx', axis=1, tiled=True)  22.7 us
    ppermute x2, starting transfers between devices, padded_2(): lax.ppermute(head, axis, [((i + 1) % count, i) for i in range(ends)])  8.41 us
    ppermute x2, starting transfers between devices, padded_2(): lax.ppermute(tail, axis, [(i, (i + 1) % count) for i in range(ends)])  4.03 us
    pallas_call x1, Pallas kernels, local_solve(): pl.pallas_call(functools.partial(thomas_kernel, chunks, devices), out_sha...  3.8 us
    pallas_call x1, Pallas kernels, finish(): pl.pallas_call(functools.partial(finish_kernel, chunks), out_shape=jax.Sh...  3.43 us
    add x1, other arithmetic, build_rhs(): field - transport + 0.05 * (curve_y + curve_z)  1.92 us
    slice x2, local copies, waits for them, and re-layouts, padded_2(): head = lax.slice_in_dim(cells, 0, width, axis=dim)  1.87 us
  transfers between devices with their start and end apart: 4, of which 1 were waited for; matrix products, arithmetic and copies ran while one was open for 2% of the time, Pallas kernels for 0%

profile of v13, /device:TPU:1, one launch (start us, length us, event | category | flops | bytes accessed | tf_op | source)
XLA Modules:
  0.0 47.8 jit_solution(12577020154777181575)
XLA Ops:
  0.0 0.0 copy-start
  0.0 1.1 %fusion.14 = (f32[2,256,128]{2,1,0:T(8,128)S(1)}, f32[2,256,128]{2,1,0:T(8,128)S(1)}) fusion(f32[4,256,128]{2,1,0:T(8,128)} %param.3), kind=kLoop, calls=%fused_computation.31 | loop fusion | bytes 1048576 | tf_op jit(solution)/shard_map/slice | solution.py:15
  1.1 2.1 %collective-permute-start.3 = (f32[2,256,128]{2,1,0:T(8,128)S(1)}, f32[2,256,128]{2,1,0:T(8,128)S(1)}, u32[]{:S(2)}, u32[]{:S(2)}) collective-permute-start(f32[2,256,128]{2,1,0:T(8,128)S(1)} %get-tuple-element.14), channel_id=1, source_target_pairs={{0,1},{1,2},{2,3},{3,4},{4,5},{5,6},{6,7},{7,8},{8,9},{9,10},{10,1... | collective-permute-start | bytes 786440 | tf_op jit(solution)/shard_map/ppermute | solution.py:19
  3.2 3.8 %collective-permute-start.2 = (f32[2,256,128]{2,1,0:T(8,128)S(1)}, f32[2,256,128]{2,1,0:T(8,128)S(1)}, u32[]{:S(2)}, u32[]{:S(2)}) collective-permute-start(f32[2,256,128]{2,1,0:T(8,128)S(1)} %get-tuple-element.13), channel_id=1, source_target_pairs={{1,0},{2,1},{3,2},{4,3},{5,4},{6,5},{7,6},{8,7},{9,8},{10,9},{11,1... | collective-permute-start | bytes 786440 | tf_op jit(solution)/shard_map/ppermute | solution.py:21
  7.0 0.7 %fusion.16 = (f32[4,2,128]{2,1,0:T(2,128)S(1)}, f32[4,2,128]{2,1,0:T(2,128)S(1)}) fusion(f32[4,256,128]{2,1,0:T(8,128)} %param.3), kind=kLoop, calls=%fused_computation.33 | loop fusion | bytes 16384 | tf_op jit(solution)/shard_map/slice | solution.py:15
  7.8 4.6 %collective-permute-start = (f32[4,2,128]{2,1,0:T(2,128)S(1)}, f32[4,2,128]{2,1,0:T(2,128)S(1)}, u32[]{:S(2)}, u32[]{:S(2)}) collective-permute-start(f32[4,2,128]{2,1,0:T(2,128)S(1)} %get-tuple-element.20), channel_id=1, source_target_pairs={{16,0},{32,16},{48,32},{64,48},{80,64},{96,80},{112,96},{128,112},... | collective-permute-start | bytes 12296 | tf_op jit(solution)/shard_map/ppermute | solution.py:21
  12.4 1.9 %collective-permute-start.1 = (f32[4,2,128]{2,1,0:T(2,128)S(1)}, f32[4,2,128]{2,1,0:T(2,128)S(1)}, u32[]{:S(2)}, u32[]{:S(2)}) collective-permute-start(f32[4,2,128]{2,1,0:T(2,128)S(1)} %get-tuple-element.21), channel_id=1, source_target_pairs={{0,16},{16,32},{32,48},{48,64},{64,80},{80,96},{96,112},{112,128},... | collective-permute-start | bytes 12296 | tf_op jit(solution)/shard_map/ppermute | solution.py:19
  14.3 0.0 copy-done
  14.3 0.2 fusion.15
  14.6 0.0 copy-start.1
  14.6 0.0 collective-permute-done.3
  14.6 0.1 constant_dynamic-update-slice_fusion.3
  14.7 0.0 collective-permute-done.2
  14.8 0.0 collective-permute-done
  14.8 0.7 %collective-permute-done.1 = f32[4,2,128]{2,1,0:T(2,128)S(1)} collective-permute-done((f32[4,2,128]{2,1,0:T(2,128)S(1)}, f32[4,2,128]{2,1,0:T(2,128)S(1)}, u32[]{:S(2)}, u32[]{:S(2)}) %collective-permute-start.1) | collective-permute-done | bytes 4128 | tf_op jit(solution)/shard_map/ppermute | solution.py:19
  15.5 0.5 %copy-done.1 = f32[3,4,256,128]{3,2,1,0:T(8,128)S(1)} copy-done((f32[3,4,256,128]{3,2,1,0:T(8,128)S(1)}, f32[3,4,256,128]{3,2,1,0:T(8,128)}, u32[]{:S(2)}) %copy-start.1) | copy-done | bytes 1572888
  16.0 1.9 %fusion.10 = f32[4,256,128]{2,1,0:T(8,128)} fusion(f32[4,256,128]{2,1,0:T(8,128)S(1)} %copy-done, f32[4,2,128]{2,1,0:T(2,128)S(1)} %collective-permute-done.1, f32[4,258,128]{2,1,0:T(8,128)S(1)} %constant_dynamic-update-slice_fusion, f32[4,256,2]{2,1,0:T(8,128)S(1)} %get-tuple-element.19, f32[4,256,2]{2,1,0:T(8,128)S(1)} %get-tuple-element.18, ...), kind=kLoop, calls=%fused_computation.16 | loop fusion | flops 6029312 | bytes 5787648 | tf_op jit(solution)/shard_map/add | solution.py:46
  17.9 3.8 %shard_map.37 = (f32[128,8,128]{2,1,0:T(8,128)}, f32[128,8,128]{2,1,0:T(8,128)}, f32[128,8,128]{2,1,0:T(8,128)}, f32[64,128]{1,0:T(8,128)}) custom-call(s32[1]{0:T(128)} %bitcast.place_ref, f32[1024,128]{1,0:T(8,128)} %bitcast.21, f32[1024,128]{1,0:T(8,128)} %bitcast.19), custom_call_target="tpu_custom_call" | custom-call | tf_op jit(solution)/shard_map/pallas_call | solution.py:195
  21.7 22.7 %all_gather.3 = f32[4,256,128]{2,1,0:T(8,128)} all-gather(f32[4,16,128]{2,1,0:T(8,128)} %bitcast.25), channel_id=1, replica_groups=mesh['gx'=16,'gy'=16] {'gx'}, dimensions={1}, use_global_device_ids=true | all-gather | bytes 557056 | tf_op jit(solution)/shard_map/all_gather | solution.py:273
  44.3 3.4 %shard_map.38 = f32[1024,128]{1,0:T(8,128)} custom-call(s32[1]{0:T(128)} %bitcast.place_ref, f32[1024,128]{1,0:T(8,128)} %bitcast.20, f32[1024,128]{1,0:T(8,128)} %bitcast.22, f32[1024,128]{1,0:T(8,128)} %bitcast.23, f32[1024,128]{1,0:T(8,128)} %bitcast.24), custom_call_target="tpu_custom_call" | custom-call | tf_op jit(solution)/shard_map/pallas_call | solution.py:248
  (3 shorter events, 0.0 us)
Async XLA Ops:
  0.0 14.3 %copy-start = (f32[4,256,128]{2,1,0:T(8,128)S(1)}, f32[4,256,128]{2,1,0:T(8,128)}, u32[]{:S(2)}) copy-start(f32[4,256,128]{2,1,0:T(8,128)} %param.3) | copy-start | bytes 1572868
  1.1 13.4 %collective-permute-start.3 = (f32[2,256,128]{2,1,0:T(8,128)S(1)}, f32[2,256,128]{2,1,0:T(8,128)S(1)}, u32[]{:S(2)}, u32[]{:S(2)}) collective-permute-start(f32[2,256,128]{2,1,0:T(8,128)S(1)} %get-tuple-element.14), channel_id=1, source_target_pairs={{0,1},{1,2},{2,3},{3,4},{4,5},{5,6},{6,7},{7,8},{8,9},{9,10},{10,1... | collective-permute-start | bytes 786440 | tf_op jit(solution)/shard_map/ppermute | solution.py:19
  3.2 11.5 %collective-permute-start.2 = (f32[2,256,128]{2,1,0:T(8,128)S(1)}, f32[2,256,128]{2,1,0:T(8,128)S(1)}, u32[]{:S(2)}, u32[]{:S(2)}) collective-permute-start(f32[2,256,128]{2,1,0:T(8,128)S(1)} %get-tuple-element.13), channel_id=1, source_target_pairs={{1,0},{2,1},{3,2},{4,3},{5,4},{6,5},{7,6},{8,7},{9,8},{10,9},{11,1... | collective-permute-start | bytes 786440 | tf_op jit(solution)/shard_map/ppermute | solution.py:21
  7.8 7.0 %collective-permute-start = (f32[4,2,128]{2,1,0:T(2,128)S(1)}, f32[4,2,128]{2,1,0:T(2,128)S(1)}, u32[]{:S(2)}, u32[]{:S(2)}) collective-permute-start(f32[4,2,128]{2,1,0:T(2,128)S(1)} %get-tuple-element.20), channel_id=1, source_target_pairs={{16,0},{32,16},{48,32},{64,48},{80,64},{96,80},{112,96},{128,112},... | collective-permute-start | bytes 12296 | tf_op jit(solution)/shard_map/ppermute | solution.py:21
  12.4 3.1 %collective-permute-start.1 = (f32[4,2,128]{2,1,0:T(2,128)S(1)}, f32[4,2,128]{2,1,0:T(2,128)S(1)}, u32[]{:S(2)}, u32[]{:S(2)}) collective-permute-start(f32[4,2,128]{2,1,0:T(2,128)S(1)} %get-tuple-element.21), channel_id=1, source_target_pairs={{0,16},{16,32},{32,48},{48,64},{64,80},{80,96},{96,112},{112,128},... | collective-permute-start | bytes 12296 | tf_op jit(solution)/shard_map/ppermute | solution.py:19
  14.6 1.4 %copy-start.1 = (f32[3,4,256,128]{3,2,1,0:T(8,128)S(1)}, f32[3,4,256,128]{3,2,1,0:T(8,128)}, u32[]{:S(2)}) copy-start(f32[3,4,256,128]{3,2,1,0:T(8,128)} %param.4) | copy-start | bytes 4718596

commit v14 on v13

--- a/solution.py
+++ b/solution.py
@@ -202,7 +202,9 @@
     )(place.reshape(1).astype(jnp.int32), rate.reshape(planes * length, lanes), right.reshape(planes * length, lanes))
 
 
-def finish_kernel(chunks, place_ref, system_ref, part_ref, first_ref, last_ref, out_ref, ratio_ref, value_ref):
+def finish_kernel(
+    chunks, place_ref, system_ref, part_ref, first_ref, last_ref, out_ref, ratio_ref, value_ref, ends_ref
+):
     count, planes, lanes = ratio_ref.shape
     width = system_ref.shape[0] // planes
     rows = part_ref.shape[0] // (planes * chunks)
@@ -227,18 +229,25 @@
         value = value_ref[row] - ratio_ref[row] * value
         value_ref[row] = value
     own = place_ref[0] * (2 * chunks)
+    sublanes = planes * chunks
     for chunk in range(chunks):
         for plane in range(planes):
-            start_value = value_ref[own + 2 * chunk, pl.ds(plane, 1), :]
-            end_value = value_ref[own + 2 * chunk + 1, pl.ds(plane, 1), :]
-            offset = plane * length + chunk * rows
-            block = pl.ds(offset, rows)
-            table = pl.ds(plane * chunks + chunk, rows, stride=planes * chunks)
-            out_ref[block] = (
-                part_ref[table] + first_ref[table] * start_value + last_ref[table] * end_value
-            )
-            out_ref[pl.ds(offset, 1)] = start_value
-            out_ref[pl.ds(offset + rows - 1, 1)] = end_value
+            lane_row = pl.ds(plane * chunks + chunk, 1)
+            ends_ref[0, lane_row, :] = value_ref[own + 2 * chunk, pl.ds(plane, 1), :]
+            ends_ref[1, lane_row, :] = value_ref[own + 2 * chunk + 1, pl.ds(plane, 1), :]
+    start_value, end_value = ends_ref[0], ends_ref[1]
+
+    def at(i):
+        return pl.ds(i, sublanes, stride=rows)
+
+    def combine(i, carry):
+        row = pl.ds(i * sublanes, sublanes)
+        out_ref[at(i)] = part_ref[row] + first_ref[row] * start_value + last_ref[row] * end_value
+        return carry
+
+    lax.fori_loop(1, rows - 1, combine, 0, unroll=8)
+    out_ref[at(0)] = start_value
+    out_ref[at(rows - 1)] = end_value
 
 
 def finish(place, system, part, first, last, chunks):
@@ -251,7 +260,7 @@
         in_specs=[pl.BlockSpec(memory_space=pltpu.SMEM)]
         + [pl.BlockSpec(memory_space=pltpu.VMEM)] * 4,
         out_specs=pl.BlockSpec(memory_space=pltpu.VMEM),
-        scratch_shapes=[table, table],
+        scratch_shapes=[table, table, pltpu.VMEM((2, planes * chunks, lanes), jnp.float32)],
     )(
         place.reshape(1).astype(jnp.int32),
         system.reshape(planes * width, lanes),

time: 48.1 us -> 48.1 us (level)
  no operation moved by 1% of the time
where the time goes in v14:
time: 48.1 us; the launch traced here: 47.8 us
  blocking collectives  22.7 us (47%)
  starting transfers between devices  12.4 us (26%)
  Pallas kernels  7.27 us (15%)
  local copies, waits for them, and re-layouts  2.72 us (6%)
  other arithmetic  1.92 us (4%)
  waiting for transfers between devices  0.7 us (1%)
    all_gather x1, blocking collectives, shards(): gathered = lax.all_gather(stacked, 'gx', axis=1, tiled=True)  22.7 us
    ppermute x2, starting transfers between devices, padded_2(): lax.ppermute(head, axis, [((i + 1) % count, i) for i in range(ends)])  8.41 us
    ppermute x2, starting transfers between devices, padded_2(): lax.ppermute(tail, axis, [(i, (i + 1) % count) for i in range(ends)])  4.03 us
    pallas_call x1, Pallas kernels, local_solve(): pl.pallas_call(functools.partial(thomas_kernel, chunks, devices), out_sha...  3.8 us
    pallas_call x1, Pallas kernels, finish(): pl.pallas_call(functools.partial(finish_kernel, chunks), out_shape=jax.Sh...  3.47 us
    add x1, other arithmetic, build_rhs(): field - transport + 0.05 * (curve_y + curve_z)  1.92 us
    slice x2, local copies, waits for them, and re-layouts, padded_2(): head = lax.slice_in_dim(cells, 0, width, axis=dim)  1.87 us
  transfers between devices with their start and end apart: 4, of which 1 were waited for; matrix products, arithmetic and copies ran while one was open for 2% of the time, Pallas kernels for 0%

profile of v14, /device:TPU:1, one launch (start us, length us, event | category | flops | bytes accessed | tf_op | source)
XLA Modules:
  0.0 47.8 jit_solution(11484208803923368104)
XLA Ops:
  0.0 0.0 copy-start
  0.0 1.1 %fusion.14 = (f32[2,256,128]{2,1,0:T(8,128)S(1)}, f32[2,256,128]{2,1,0:T(8,128)S(1)}) fusion(f32[4,256,128]{2,1,0:T(8,128)} %param.3), kind=kLoop, calls=%fused_computation.31 | loop fusion | bytes 1048576 | tf_op jit(solution)/shard_map/slice | solution.py:15
  1.1 2.1 %collective-permute-start.3 = (f32[2,256,128]{2,1,0:T(8,128)S(1)}, f32[2,256,128]{2,1,0:T(8,128)S(1)}, u32[]{:S(2)}, u32[]{:S(2)}) collective-permute-start(f32[2,256,128]{2,1,0:T(8,128)S(1)} %get-tuple-element.14), channel_id=1, source_target_pairs={{0,1},{1,2},{2,3},{3,4},{4,5},{5,6},{6,7},{7,8},{8,9},{9,10},{10,1... | collective-permute-start | bytes 786440 | tf_op jit(solution)/shard_map/ppermute | solution.py:19
  3.2 3.8 %collective-permute-start.2 = (f32[2,256,128]{2,1,0:T(8,128)S(1)}, f32[2,256,128]{2,1,0:T(8,128)S(1)}, u32[]{:S(2)}, u32[]{:S(2)}) collective-permute-start(f32[2,256,128]{2,1,0:T(8,128)S(1)} %get-tuple-element.13), channel_id=1, source_target_pairs={{1,0},{2,1},{3,2},{4,3},{5,4},{6,5},{7,6},{8,7},{9,8},{10,9},{11,1... | collective-permute-start | bytes 786440 | tf_op jit(solution)/shard_map/ppermute | solution.py:21
  7.0 0.7 %fusion.16 = (f32[4,2,128]{2,1,0:T(2,128)S(1)}, f32[4,2,128]{2,1,0:T(2,128)S(1)}) fusion(f32[4,256,128]{2,1,0:T(8,128)} %param.3), kind=kLoop, calls=%fused_computation.33 | loop fusion | bytes 16384 | tf_op jit(solution)/shard_map/slice | solution.py:15
  7.8 4.6 %collective-permute-start = (f32[4,2,128]{2,1,0:T(2,128)S(1)}, f32[4,2,128]{2,1,0:T(2,128)S(1)}, u32[]{:S(2)}, u32[]{:S(2)}) collective-permute-start(f32[4,2,128]{2,1,0:T(2,128)S(1)} %get-tuple-element.20), channel_id=1, source_target_pairs={{16,0},{32,16},{48,32},{64,48},{80,64},{96,80},{112,96},{128,112},... | collective-permute-start | bytes 12296 | tf_op jit(solution)/shard_map/ppermute | solution.py:21
  12.4 1.9 %collective-permute-start.1 = (f32[4,2,128]{2,1,0:T(2,128)S(1)}, f32[4,2,128]{2,1,0:T(2,128)S(1)}, u32[]{:S(2)}, u32[]{:S(2)}) collective-permute-start(f32[4,2,128]{2,1,0:T(2,128)S(1)} %get-tuple-element.21), channel_id=1, source_target_pairs={{0,16},{16,32},{32,48},{48,64},{64,80},{80,96},{96,112},{112,128},... | collective-permute-start | bytes 12296 | tf_op jit(solution)/shard_map/ppermute | solution.py:19
  14.3 0.0 copy-done
  14.3 0.2 fusion.15
  14.6 0.0 copy-start.1
  14.6 0.0 collective-permute-done.3
  14.6 0.1 constant_dynamic-update-slice_fusion.3
  14.7 0.0 collective-permute-done.2
  14.8 0.0 collective-permute-done
  14.8 0.7 %collective-permute-done.1 = f32[4,2,128]{2,1,0:T(2,128)S(1)} collective-permute-done((f32[4,2,128]{2,1,0:T(2,128)S(1)}, f32[4,2,128]{2,1,0:T(2,128)S(1)}, u32[]{:S(2)}, u32[]{:S(2)}) %collective-permute-start.1) | collective-permute-done | bytes 4128 | tf_op jit(solution)/shard_map/ppermute | solution.py:19
  15.5 0.5 %copy-done.1 = f32[3,4,256,128]{3,2,1,0:T(8,128)S(1)} copy-done((f32[3,4,256,128]{3,2,1,0:T(8,128)S(1)}, f32[3,4,256,128]{3,2,1,0:T(8,128)}, u32[]{:S(2)}) %copy-start.1) | copy-done | bytes 1572888
  16.0 1.9 %fusion.10 = f32[4,256,128]{2,1,0:T(8,128)} fusion(f32[4,256,128]{2,1,0:T(8,128)S(1)} %copy-done, f32[4,2,128]{2,1,0:T(2,128)S(1)} %collective-permute-done.1, f32[4,258,128]{2,1,0:T(8,128)S(1)} %constant_dynamic-update-slice_fusion, f32[4,256,2]{2,1,0:T(8,128)S(1)} %get-tuple-element.19, f32[4,256,2]{2,1,0:T(8,128)S(1)} %get-tuple-element.18, ...), kind=kLoop, calls=%fused_computation.16 | loop fusion | flops 6029312 | bytes 5787648 | tf_op jit(solution)/shard_map/add | solution.py:46
  17.9 3.8 %shard_map.37 = (f32[128,8,128]{2,1,0:T(8,128)}, f32[128,8,128]{2,1,0:T(8,128)}, f32[128,8,128]{2,1,0:T(8,128)}, f32[64,128]{1,0:T(8,128)}) custom-call(s32[1]{0:T(128)} %bitcast.place_ref, f32[1024,128]{1,0:T(8,128)} %bitcast.21, f32[1024,128]{1,0:T(8,128)} %bitcast.19), custom_call_target="tpu_custom_call" | custom-call | tf_op jit(solution)/shard_map/pallas_call | solution.py:195
  21.7 22.7 %all_gather.3 = f32[4,256,128]{2,1,0:T(8,128)} all-gather(f32[4,16,128]{2,1,0:T(8,128)} %bitcast.25), channel_id=1, replica_groups=mesh['gx'=16,'gy'=16] {'gx'}, dimensions={1}, use_global_device_ids=true | all-gather | bytes 557056 | tf_op jit(solution)/shard_map/all_gather | solution.py:282
  44.3 3.5 %shard_map.38 = f32[1024,128]{1,0:T(8,128)} custom-call(s32[1]{0:T(128)} %bitcast.place_ref, f32[1024,128]{1,0:T(8,128)} %bitcast.20, f32[1024,128]{1,0:T(8,128)} %bitcast.22, f32[1024,128]{1,0:T(8,128)} %bitcast.23, f32[1024,128]{1,0:T(8,128)} %bitcast.24), custom_call_target="tpu_custom_call" | custom-call | tf_op jit(solution)/shard_map/pallas_call | solution.py:257
  (3 shorter events, 0.0 us)
Async XLA Ops:
  0.0 14.3 %copy-start = (f32[4,256,128]{2,1,0:T(8,128)S(1)}, f32[4,256,128]{2,1,0:T(8,128)}, u32[]{:S(2)}) copy-start(f32[4,256,128]{2,1,0:T(8,128)} %param.3) | copy-start | bytes 1572868
  1.1 13.4 %collective-permute-start.3 = (f32[2,256,128]{2,1,0:T(8,128)S(1)}, f32[2,256,128]{2,1,0:T(8,128)S(1)}, u32[]{:S(2)}, u32[]{:S(2)}) collective-permute-start(f32[2,256,128]{2,1,0:T(8,128)S(1)} %get-tuple-element.14), channel_id=1, source_target_pairs={{0,1},{1,2},{2,3},{3,4},{4,5},{5,6},{6,7},{7,8},{8,9},{9,10},{10,1... | collective-permute-start | bytes 786440 | tf_op jit(solution)/shard_map/ppermute | solution.py:19
  3.2 11.5 %collective-permute-start.2 = (f32[2,256,128]{2,1,0:T(8,128)S(1)}, f32[2,256,128]{2,1,0:T(8,128)S(1)}, u32[]{:S(2)}, u32[]{:S(2)}) collective-permute-start(f32[2,256,128]{2,1,0:T(8,128)S(1)} %get-tuple-element.13), channel_id=1, source_target_pairs={{1,0},{2,1},{3,2},{4,3},{5,4},{6,5},{7,6},{8,7},{9,8},{10,9},{11,1... | collective-permute-start | bytes 786440 | tf_op jit(solution)/shard_map/ppermute | solution.py:21
  7.8 7.0 %collective-permute-start = (f32[4,2,128]{2,1,0:T(2,128)S(1)}, f32[4,2,128]{2,1,0:T(2,128)S(1)}, u32[]{:S(2)}, u32[]{:S(2)}) collective-permute-start(f32[4,2,128]{2,1,0:T(2,128)S(1)} %get-tuple-element.20), channel_id=1, source_target_pairs={{16,0},{32,16},{48,32},{64,48},{80,64},{96,80},{112,96},{128,112},... | collective-permute-start | bytes 12296 | tf_op jit(solution)/shard_map/ppermute | solution.py:21
  12.4 3.1 %collective-permute-start.1 = (f32[4,2,128]{2,1,0:T(2,128)S(1)}, f32[4,2,128]{2,1,0:T(2,128)S(1)}, u32[]{:S(2)}, u32[]{:S(2)}) collective-permute-start(f32[4,2,128]{2,1,0:T(2,128)S(1)} %get-tuple-element.21), channel_id=1, source_target_pairs={{0,16},{16,32},{32,48},{48,64},{64,80},{80,96},{96,112},{112,128},... | collective-permute-start | bytes 12296 | tf_op jit(solution)/shard_map/ppermute | solution.py:19
  14.6 1.4 %copy-start.1 = (f32[3,4,256,128]{3,2,1,0:T(8,128)S(1)}, f32[3,4,256,128]{3,2,1,0:T(8,128)}, u32[]{:S(2)}) copy-start(f32[3,4,256,128]{3,2,1,0:T(8,128)} %param.4) | copy-start | bytes 4718596

commit v15 on v14

--- a/solution.py
+++ b/solution.py
@@ -213,10 +213,12 @@
     def coefficient(row, kind):
         return system_ref[pl.ds((row // 2) * 8 + kind * 2 + row % 2, planes, stride=width)]
 
-    ratio = value = None
-    for row in range(count):
+    middle = count // 2
+    ratio = value = back_ratio = back_value = None
+    for step in range(middle):
+        row, back = step, count - 1 - step
         sub, diag, upper, right = (coefficient(row, kind) for kind in range(4))
-        if row == 0:
+        if step == 0:
             inverse = 1.0 / diag
             value = right * inverse
         else:
@@ -225,9 +227,26 @@
         ratio = upper * inverse
         ratio_ref[row] = ratio
         value_ref[row] = value
-    for row in range(count - 2, -1, -1):
+        sub, diag, upper, right = (coefficient(back, kind) for kind in range(4))
+        if step == 0:
+            inverse = 1.0 / diag
+            back_value = right * inverse
+        else:
+            inverse = 1.0 / (diag - upper * back_ratio)
+            back_value = (right - upper * back_value) * inverse
+        back_ratio = sub * inverse
+        ratio_ref[back] = back_ratio
+        value_ref[back] = back_value
+    value = (value - ratio * back_value) / (1.0 - ratio * back_ratio)
+    back_value = back_value - back_ratio * value
+    value_ref[middle - 1] = value
+    value_ref[middle] = back_value
+    for step in range(1, middle):
+        row, back = middle - 1 - step, middle + step
         value = value_ref[row] - ratio_ref[row] * value
         value_ref[row] = value
+        back_value = value_ref[back] - ratio_ref[back] * back_value
+        value_ref[back] = back_value
     own = place_ref[0] * (2 * chunks)
     sublanes = planes * chunks
     for chunk in range(chunks):

time: 48.1 us -> 47.8 us (level)
  no operation moved by 1% of the time
where the time goes in v15:
time: 47.8 us; the launch traced here: 47.5 us
  blocking collectives  22.7 us (47%)
  starting transfers between devices  12.4 us (26%)
  Pallas kernels  6.95 us (15%)
  local copies, waits for them, and re-layouts  2.72 us (6%)
  other arithmetic  1.92 us (4%)
  waiting for transfers between devices  0.7 us (1%)
    all_gather x1, blocking collectives, shards(): gathered = lax.all_gather(stacked, 'gx', axis=1, tiled=True)  22.7 us
    ppermute x2, starting transfers between devices, padded_2(): lax.ppermute(head, axis, [((i + 1) % count, i) for i in range(ends)])  8.41 us
    ppermute x2, starting transfers between devices, padded_2(): lax.ppermute(tail, axis, [(i, (i + 1) % count) for i in range(ends)])  4.03 us
    pallas_call x1, Pallas kernels, local_solve(): pl.pallas_call(functools.partial(thomas_kernel, chunks, devices), out_sha...  3.8 us
    pallas_call x1, Pallas kernels, finish(): pl.pallas_call(functools.partial(finish_kernel, chunks), out_shape=jax.Sh...  3.14 us
    add x1, other arithmetic, build_rhs(): field - transport + 0.05 * (curve_y + curve_z)  1.92 us
    slice x2, local copies, waits for them, and re-layouts, padded_2(): head = lax.slice_in_dim(cells, 0, width, axis=dim)  1.87 us
  transfers between devices with their start and end apart: 4, of which 1 were waited for; matrix products, arithmetic and copies ran while one was open for 2% of the time, Pallas kernels for 0%

profile of v15, /device:TPU:1, one launch (start us, length us, event | category | flops | bytes accessed | tf_op | source)
XLA Modules:
  0.0 47.5 jit_solution(14893095433649641492)
XLA Ops:
  0.0 0.0 copy-start
  0.0 1.1 %fusion.14 = (f32[2,256,128]{2,1,0:T(8,128)S(1)}, f32[2,256,128]{2,1,0:T(8,128)S(1)}) fusion(f32[4,256,128]{2,1,0:T(8,128)} %param.3), kind=kLoop, calls=%fused_computation.31 | loop fusion | bytes 1048576 | tf_op jit(solution)/shard_map/slice | solution.py:15
  1.1 2.1 %collective-permute-start.3 = (f32[2,256,128]{2,1,0:T(8,128)S(1)}, f32[2,256,128]{2,1,0:T(8,128)S(1)}, u32[]{:S(2)}, u32[]{:S(2)}) collective-permute-start(f32[2,256,128]{2,1,0:T(8,128)S(1)} %get-tuple-element.14), channel_id=1, source_target_pairs={{0,1},{1,2},{2,3},{3,4},{4,5},{5,6},{6,7},{7,8},{8,9},{9,10},{10,1... | collective-permute-start | bytes 786440 | tf_op jit(solution)/shard_map/ppermute | solution.py:19
  3.2 3.8 %collective-permute-start.2 = (f32[2,256,128]{2,1,0:T(8,128)S(1)}, f32[2,256,128]{2,1,0:T(8,128)S(1)}, u32[]{:S(2)}, u32[]{:S(2)}) collective-permute-start(f32[2,256,128]{2,1,0:T(8,128)S(1)} %get-tuple-element.13), channel_id=1, source_target_pairs={{1,0},{2,1},{3,2},{4,3},{5,4},{6,5},{7,6},{8,7},{9,8},{10,9},{11,1... | collective-permute-start | bytes 786440 | tf_op jit(solution)/shard_map/ppermute | solution.py:21
  7.0 0.7 %fusion.16 = (f32[4,2,128]{2,1,0:T(2,128)S(1)}, f32[4,2,128]{2,1,0:T(2,128)S(1)}) fusion(f32[4,256,128]{2,1,0:T(8,128)} %param.3), kind=kLoop, calls=%fused_computation.33 | loop fusion | bytes 16384 | tf_op jit(solution)/shard_map/slice | solution.py:15
  7.8 4.6 %collective-permute-start = (f32[4,2,128]{2,1,0:T(2,128)S(1)}, f32[4,2,128]{2,1,0:T(2,128)S(1)}, u32[]{:S(2)}, u32[]{:S(2)}) collective-permute-start(f32[4,2,128]{2,1,0:T(2,128)S(1)} %get-tuple-element.20), channel_id=1, source_target_pairs={{16,0},{32,16},{48,32},{64,48},{80,64},{96,80},{112,96},{128,112},... | collective-permute-start | bytes 12296 | tf_op jit(solution)/shard_map/ppermute | solution.py:21
  12.4 1.9 %collective-permute-start.1 = (f32[4,2,128]{2,1,0:T(2,128)S(1)}, f32[4,2,128]{2,1,0:T(2,128)S(1)}, u32[]{:S(2)}, u32[]{:S(2)}) collective-permute-start(f32[4,2,128]{2,1,0:T(2,128)S(1)} %get-tuple-element.21), channel_id=1, source_target_pairs={{0,16},{16,32},{32,48},{48,64},{64,80},{80,96},{96,112},{112,128},... | collective-permute-start | bytes 12296 | tf_op jit(solution)/shard_map/ppermute | solution.py:19
  14.3 0.0 copy-done
  14.3 0.2 fusion.15
  14.6 0.0 copy-start.1
  14.6 0.0 collective-permute-done.3
  14.6 0.1 constant_dynamic-update-slice_fusion.3
  14.7 0.0 collective-permute-done.2
  14.8 0.0 collective-permute-done
  14.8 0.7 %collective-permute-done.1 = f32[4,2,128]{2,1,0:T(2,128)S(1)} collective-permute-done((f32[4,2,128]{2,1,0:T(2,128)S(1)}, f32[4,2,128]{2,1,0:T(2,128)S(1)}, u32[]{:S(2)}, u32[]{:S(2)}) %collective-permute-start.1) | collective-permute-done | bytes 4128 | tf_op jit(solution)/shard_map/ppermute | solution.py:19
  15.5 0.5 %copy-done.1 = f32[3,4,256,128]{3,2,1,0:T(8,128)S(1)} copy-done((f32[3,4,256,128]{3,2,1,0:T(8,128)S(1)}, f32[3,4,256,128]{3,2,1,0:T(8,128)}, u32[]{:S(2)}) %copy-start.1) | copy-done | bytes 1572888
  16.0 1.9 %fusion.10 = f32[4,256,128]{2,1,0:T(8,128)} fusion(f32[4,256,128]{2,1,0:T(8,128)S(1)} %copy-done, f32[4,2,128]{2,1,0:T(2,128)S(1)} %collective-permute-done.1, f32[4,258,128]{2,1,0:T(8,128)S(1)} %constant_dynamic-update-slice_fusion, f32[4,256,2]{2,1,0:T(8,128)S(1)} %get-tuple-element.19, f32[4,256,2]{2,1,0:T(8,128)S(1)} %get-tuple-element.18, ...), kind=kLoop, calls=%fused_computation.16 | loop fusion | flops 6029312 | bytes 5787648 | tf_op jit(solution)/shard_map/add | solution.py:46
  17.9 3.8 %shard_map.37 = (f32[128,8,128]{2,1,0:T(8,128)}, f32[128,8,128]{2,1,0:T(8,128)}, f32[128,8,128]{2,1,0:T(8,128)}, f32[64,128]{1,0:T(8,128)}) custom-call(s32[1]{0:T(128)} %bitcast.place_ref, f32[1024,128]{1,0:T(8,128)} %bitcast.21, f32[1024,128]{1,0:T(8,128)} %bitcast.19), custom_call_target="tpu_custom_call" | custom-call | tf_op jit(solution)/shard_map/pallas_call | solution.py:195
  21.7 22.7 %all_gather.3 = f32[4,256,128]{2,1,0:T(8,128)} all-gather(f32[4,16,128]{2,1,0:T(8,128)} %bitcast.25), channel_id=1, replica_groups=mesh['gx'=16,'gy'=16] {'gx'}, dimensions={1}, use_global_device_ids=true | all-gather | bytes 557056 | tf_op jit(solution)/shard_map/all_gather | solution.py:301
  44.3 3.1 %shard_map.38 = f32[1024,128]{1,0:T(8,128)} custom-call(s32[1]{0:T(128)} %bitcast.place_ref, f32[1024,128]{1,0:T(8,128)} %bitcast.20, f32[1024,128]{1,0:T(8,128)} %bitcast.22, f32[1024,128]{1,0:T(8,128)} %bitcast.23, f32[1024,128]{1,0:T(8,128)} %bitcast.24), custom_call_target="tpu_custom_call" | custom-call | tf_op jit(solution)/shard_map/pallas_call | solution.py:276
  (3 shorter events, 0.0 us)
Async XLA Ops:
  0.0 14.3 %copy-start = (f32[4,256,128]{2,1,0:T(8,128)S(1)}, f32[4,256,128]{2,1,0:T(8,128)}, u32[]{:S(2)}) copy-start(f32[4,256,128]{2,1,0:T(8,128)} %param.3) | copy-start | bytes 1572868
  1.1 13.4 %collective-permute-start.3 = (f32[2,256,128]{2,1,0:T(8,128)S(1)}, f32[2,256,128]{2,1,0:T(8,128)S(1)}, u32[]{:S(2)}, u32[]{:S(2)}) collective-permute-start(f32[2,256,128]{2,1,0:T(8,128)S(1)} %get-tuple-element.14), channel_id=1, source_target_pairs={{0,1},{1,2},{2,3},{3,4},{4,5},{5,6},{6,7},{7,8},{8,9},{9,10},{10,1... | collective-permute-start | bytes 786440 | tf_op jit(solution)/shard_map/ppermute | solution.py:19
  3.2 11.5 %collective-permute-start.2 = (f32[2,256,128]{2,1,0:T(8,128)S(1)}, f32[2,256,128]{2,1,0:T(8,128)S(1)}, u32[]{:S(2)}, u32[]{:S(2)}) collective-permute-start(f32[2,256,128]{2,1,0:T(8,128)S(1)} %get-tuple-element.13), channel_id=1, source_target_pairs={{1,0},{2,1},{3,2},{4,3},{5,4},{6,5},{7,6},{8,7},{9,8},{10,9},{11,1... | collective-permute-start | bytes 786440 | tf_op jit(solution)/shard_map/ppermute | solution.py:21
  7.8 7.0 %collective-permute-start = (f32[4,2,128]{2,1,0:T(2,128)S(1)}, f32[4,2,128]{2,1,0:T(2,128)S(1)}, u32[]{:S(2)}, u32[]{:S(2)}) collective-permute-start(f32[4,2,128]{2,1,0:T(2,128)S(1)} %get-tuple-element.20), channel_id=1, source_target_pairs={{16,0},{32,16},{48,32},{64,48},{80,64},{96,80},{112,96},{128,112},... | collective-permute-start | bytes 12296 | tf_op jit(solution)/shard_map/ppermute | solution.py:21
  12.4 3.1 %collective-permute-start.1 = (f32[4,2,128]{2,1,0:T(2,128)S(1)}, f32[4,2,128]{2,1,0:T(2,128)S(1)}, u32[]{:S(2)}, u32[]{:S(2)}) collective-permute-start(f32[4,2,128]{2,1,0:T(2,128)S(1)} %get-tuple-element.21), channel_id=1, source_target_pairs={{0,16},{16,32},{32,48},{48,64},{64,80},{80,96},{96,112},{112,128},... | collective-permute-start | bytes 12296 | tf_op jit(solution)/shard_map/ppermute | solution.py:19
  14.6 1.4 %copy-start.1 = (f32[3,4,256,128]{3,2,1,0:T(8,128)S(1)}, f32[3,4,256,128]{3,2,1,0:T(8,128)}, u32[]{:S(2)}) copy-start(f32[3,4,256,128]{3,2,1,0:T(8,128)} %param.4) | copy-start | bytes 4718596

commit v16 on v15

--- a/solution.py
+++ b/solution.py
@@ -119,17 +119,28 @@
         return pl.ds(i, sublanes, stride=rows)
 
     zero = jnp.zeros(ratio_ref.shape[1:], jnp.float32)
-    rate = rate_ref[at(1)]
+    top, bottom = 1, rows - 2
+    middle = (top + bottom + 1) // 2
+    rate = rate_ref[at(top)]
     inverse = 1.0 / (1.0 + 2.0 * rate)
     ratio = -rate * inverse
-    part = right_ref[at(1)] * inverse
+    part = right_ref[at(top)] * inverse
     first = rate * inverse
-    ratio_ref[1] = ratio
-    ahead_ref[1] = part
-    lead_ref[1] = first
-
-    def forward(i, carry):
-        ratio, part, first, _ = carry
+    ratio_ref[top] = ratio
+    ahead_ref[top] = part
+    lead_ref[top] = first
+    rate = rate_ref[at(bottom)]
+    inverse = 1.0 / (1.0 + 2.0 * rate)
+    back_ratio = -rate * inverse
+    back_part = right_ref[at(bottom)] * inverse
+    last = rate * inverse
+    ratio_ref[bottom] = back_ratio
+    ahead_ref[bottom] = back_part
+    lead_ref[bottom] = last
+
+    def forward(step, carry):
+        ratio, part, first, back_ratio, back_part, last = carry
+        i = top + step
         rate = rate_ref[at(i)]
         inverse = 1.0 / ((1.0 + 2.0 * rate) + rate * ratio)
         ratio = -rate * inverse
@@ -138,29 +149,49 @@
         ratio_ref[i] = ratio
         ahead_ref[i] = part
         lead_ref[i] = first
-        return ratio, part, first, inverse
-
-    _, part, first, inverse = lax.fori_loop(
-        2, rows - 1, forward, (ratio, part, first, zero), unroll=True
-    )
-    last = rate_ref[at(rows - 2)] * inverse
-    part_ref[rows - 2] = part
-    first_ref[rows - 2] = first
-    last_ref[rows - 2] = last
-
-    def backward(j, carry):
-        part, first, last = carry
-        i = rows - 3 - j
+        k = bottom - step
+        rate = rate_ref[at(k)]
+        inverse = 1.0 / ((1.0 + 2.0 * rate) + rate * back_ratio)
+        back_ratio = -rate * inverse
+        back_part = (right_ref[at(k)] + rate * back_part) * inverse
+        last = rate * last * inverse
+        ratio_ref[k] = back_ratio
+        ahead_ref[k] = back_part
+        lead_ref[k] = last
+        return ratio, part, first, back_ratio, back_part, last
+
+    ratio, part, first, back_ratio, back_part, last = lax.fori_loop(
+        1, middle - top, forward, (ratio, part, first, back_ratio, back_part, last), unroll=True
+    )
+    scale = 1.0 / (1.0 - ratio * back_ratio)
+    part = (part - ratio * back_part) * scale
+    first = first * scale
+    last_top = -ratio * last * scale
+    back_part = back_part - back_ratio * part
+    back_first = -back_ratio * first
+    last = last - back_ratio * last_top
+    part_ref[middle - 1], first_ref[middle - 1], last_ref[middle - 1] = part, first, last_top
+    part_ref[middle], first_ref[middle], last_ref[middle] = back_part, back_first, last
+
+    def backward(step, carry):
+        part, first, last_top, back_part, back_first, last = carry
+        i = middle - 1 - step
         ratio = ratio_ref[i]
         part = ahead_ref[i] - ratio * part
         first = lead_ref[i] - ratio * first
-        last = -ratio * last
-        part_ref[i] = part
-        first_ref[i] = first
-        last_ref[i] = last
-        return part, first, last
-
-    part, first, last = lax.fori_loop(0, rows - 3, backward, (part, first, last), unroll=True)
+        last_top = -ratio * last_top
+        part_ref[i], first_ref[i], last_ref[i] = part, first, last_top
+        k = middle + step
+        back_ratio = ratio_ref[k]
+        back_part = ahead_ref[k] - back_ratio * back_part
+        back_first = -back_ratio * back_first
+        last = lead_ref[k] - back_ratio * last
+        part_ref[k], first_ref[k], last_ref[k] = back_part, back_first, last
+        return part, first, last_top, back_part, back_first, last
+
+    part, first, last, _, _, _ = lax.fori_loop(
+        1, middle - top, backward, (part, first, last_top, back_part, back_first, last), unroll=True
+    )
     for ref in (part_ref, first_ref, last_ref):
         ref[0] = zero
         ref[rows - 1] = zero

time: 47.8 us -> 47.2 us (0.987)
  Pallas kernels: 6.95 us -> 6.33 us
    pallas_call x1, Pallas kernels: 3.8 us -> 3.18 us  [local_solve(): pl.pallas_call(functools.partial(thomas_kernel, chunks, devices), out_sha...]
where the time goes in v16:
time: 47.2 us; the launch traced here: 46.9 us
  blocking collectives  22.7 us (48%)
  starting transfers between devices  12.4 us (26%)
  Pallas kernels  6.33 us (13%)
  local copies, waits for them, and re-layouts  2.72 us (6%)
  other arithmetic  1.92 us (4%)
  waiting for transfers between devices  0.7 us (1%)
    all_gather x1, blocking collectives, shards(): gathered = lax.all_gather(stacked, 'gx', axis=1, tiled=True)  22.7 us
    ppermute x2, starting transfers between devices, padded_2(): lax.ppermute(head, axis, [((i + 1) % count, i) for i in range(ends)])  8.41 us
    ppermute x2, starting transfers between devices, padded_2(): lax.ppermute(tail, axis, [(i, (i + 1) % count) for i in range(ends)])  4.03 us
    pallas_call x1, Pallas kernels, local_solve(): pl.pallas_call(functools.partial(thomas_kernel, chunks, devices), out_sha...  3.18 us
    pallas_call x1, Pallas kernels, finish(): pl.pallas_call(functools.partial(finish_kernel, chunks), out_shape=jax.Sh...  3.14 us
    add x1, other arithmetic, build_rhs(): field - transport + 0.05 * (curve_y + curve_z)  1.92 us
    slice x2, local copies, waits for them, and re-layouts, padded_2(): head = lax.slice_in_dim(cells, 0, width, axis=dim)  1.87 us
  transfers between devices with their start and end apart: 4, of which 1 were waited for; matrix products, arithmetic and copies ran while one was open for 2% of the time, Pallas kernels for 0%

profile of v16, /device:TPU:1, one launch (start us, length us, event | category | flops | bytes accessed | tf_op | source)
XLA Modules:
  0.0 46.9 jit_solution(8751014747029197044)
XLA Ops:
  0.0 0.0 copy-start
  0.0 1.1 %fusion.14 = (f32[2,256,128]{2,1,0:T(8,128)S(1)}, f32[2,256,128]{2,1,0:T(8,128)S(1)}) fusion(f32[4,256,128]{2,1,0:T(8,128)} %param.3), kind=kLoop, calls=%fused_computation.31 | loop fusion | bytes 1048576 | tf_op jit(solution)/shard_map/slice | solution.py:15
  1.1 2.1 %collective-permute-start.3 = (f32[2,256,128]{2,1,0:T(8,128)S(1)}, f32[2,256,128]{2,1,0:T(8,128)S(1)}, u32[]{:S(2)}, u32[]{:S(2)}) collective-permute-start(f32[2,256,128]{2,1,0:T(8,128)S(1)} %get-tuple-element.14), channel_id=1, source_target_pairs={{0,1},{1,2},{2,3},{3,4},{4,5},{5,6},{6,7},{7,8},{8,9},{9,10},{10,1... | collective-permute-start | bytes 786440 | tf_op jit(solution)/shard_map/ppermute | solution.py:19
  3.2 3.8 %collective-permute-start.2 = (f32[2,256,128]{2,1,0:T(8,128)S(1)}, f32[2,256,128]{2,1,0:T(8,128)S(1)}, u32[]{:S(2)}, u32[]{:S(2)}) collective-permute-start(f32[2,256,128]{2,1,0:T(8,128)S(1)} %get-tuple-element.13), channel_id=1, source_target_pairs={{1,0},{2,1},{3,2},{4,3},{5,4},{6,5},{7,6},{8,7},{9,8},{10,9},{11,1... | collective-permute-start | bytes 786440 | tf_op jit(solution)/shard_map/ppermute | solution.py:21
  7.0 0.7 %fusion.16 = (f32[4,2,128]{2,1,0:T(2,128)S(1)}, f32[4,2,128]{2,1,0:T(2,128)S(1)}) fusion(f32[4,256,128]{2,1,0:T(8,128)} %param.3), kind=kLoop, calls=%fused_computation.33 | loop fusion | bytes 16384 | tf_op jit(solution)/shard_map/slice | solution.py:15
  7.8 4.6 %collective-permute-start = (f32[4,2,128]{2,1,0:T(2,128)S(1)}, f32[4,2,128]{2,1,0:T(2,128)S(1)}, u32[]{:S(2)}, u32[]{:S(2)}) collective-permute-start(f32[4,2,128]{2,1,0:T(2,128)S(1)} %get-tuple-element.20), channel_id=1, source_target_pairs={{16,0},{32,16},{48,32},{64,48},{80,64},{96,80},{112,96},{128,112},... | collective-permute-start | bytes 12296 | tf_op jit(solution)/shard_map/ppermute | solution.py:21
  12.4 1.9 %collective-permute-start.1 = (f32[4,2,128]{2,1,0:T(2,128)S(1)}, f32[4,2,128]{2,1,0:T(2,128)S(1)}, u32[]{:S(2)}, u32[]{:S(2)}) collective-permute-start(f32[4,2,128]{2,1,0:T(2,128)S(1)} %get-tuple-element.21), channel_id=1, source_target_pairs={{0,16},{16,32},{32,48},{48,64},{64,80},{80,96},{96,112},{112,128},... | collective-permute-start | bytes 12296 | tf_op jit(solution)/shard_map/ppermute | solution.py:19
  14.3 0.0 copy-done
  14.3 0.2 fusion.15
  14.6 0.0 copy-start.1
  14.6 0.0 collective-permute-done.3
  14.6 0.1 constant_dynamic-update-slice_fusion.3
  14.7 0.0 collective-permute-done.2
  14.8 0.0 collective-permute-done
  14.8 0.7 %collective-permute-done.1 = f32[4,2,128]{2,1,0:T(2,128)S(1)} collective-permute-done((f32[4,2,128]{2,1,0:T(2,128)S(1)}, f32[4,2,128]{2,1,0:T(2,128)S(1)}, u32[]{:S(2)}, u32[]{:S(2)}) %collective-permute-start.1) | collective-permute-done | bytes 4128 | tf_op jit(solution)/shard_map/ppermute | solution.py:19
  15.5 0.5 %copy-done.1 = f32[3,4,256,128]{3,2,1,0:T(8,128)S(1)} copy-done((f32[3,4,256,128]{3,2,1,0:T(8,128)S(1)}, f32[3,4,256,128]{3,2,1,0:T(8,128)}, u32[]{:S(2)}) %copy-start.1) | copy-done | bytes 1572888
  16.0 1.9 %fusion.10 = f32[4,256,128]{2,1,0:T(8,128)} fusion(f32[4,256,128]{2,1,0:T(8,128)S(1)} %copy-done, f32[4,2,128]{2,1,0:T(2,128)S(1)} %collective-permute-done.1, f32[4,258,128]{2,1,0:T(8,128)S(1)} %constant_dynamic-update-slice_fusion, f32[4,256,2]{2,1,0:T(8,128)S(1)} %get-tuple-element.19, f32[4,256,2]{2,1,0:T(8,128)S(1)} %get-tuple-element.18, ...), kind=kLoop, calls=%fused_computation.16 | loop fusion | flops 6029312 | bytes 5787648 | tf_op jit(solution)/shard_map/add | solution.py:46
  17.9 3.2 %shard_map.37 = (f32[128,8,128]{2,1,0:T(8,128)}, f32[128,8,128]{2,1,0:T(8,128)}, f32[128,8,128]{2,1,0:T(8,128)}, f32[64,128]{1,0:T(8,128)}) custom-call(s32[1]{0:T(128)} %bitcast.place_ref, f32[1024,128]{1,0:T(8,128)} %bitcast.21, f32[1024,128]{1,0:T(8,128)} %bitcast.19), custom_call_target="tpu_custom_call" | custom-call | tf_op jit(solution)/shard_map/pallas_call | solution.py:226
  21.1 22.7 %all_gather.3 = f32[4,256,128]{2,1,0:T(8,128)} all-gather(f32[4,16,128]{2,1,0:T(8,128)} %bitcast.25), channel_id=1, replica_groups=mesh['gx'=16,'gy'=16] {'gx'}, dimensions={1}, use_global_device_ids=true | all-gather | bytes 557056 | tf_op jit(solution)/shard_map/all_gather | solution.py:332
  43.7 3.1 %shard_map.38 = f32[1024,128]{1,0:T(8,128)} custom-call(s32[1]{0:T(128)} %bitcast.place_ref, f32[1024,128]{1,0:T(8,128)} %bitcast.20, f32[1024,128]{1,0:T(8,128)} %bitcast.22, f32[1024,128]{1,0:T(8,128)} %bitcast.23, f32[1024,128]{1,0:T(8,128)} %bitcast.24), custom_call_target="tpu_custom_call" | custom-call | tf_op jit(solution)/shard_map/pallas_call | solution.py:307
  (3 shorter events, 0.0 us)
Async XLA Ops:
  0.0 14.3 %copy-start = (f32[4,256,128]{2,1,0:T(8,128)S(1)}, f32[4,256,128]{2,1,0:T(8,128)}, u32[]{:S(2)}) copy-start(f32[4,256,128]{2,1,0:T(8,128)} %param.3) | copy-start | bytes 1572868
  1.1 13.4 %collective-permute-start.3 = (f32[2,256,128]{2,1,0:T(8,128)S(1)}, f32[2,256,128]{2,1,0:T(8,128)S(1)}, u32[]{:S(2)}, u32[]{:S(2)}) collective-permute-start(f32[2,256,128]{2,1,0:T(8,128)S(1)} %get-tuple-element.14), channel_id=1, source_target_pairs={{0,1},{1,2},{2,3},{3,4},{4,5},{5,6},{6,7},{7,8},{8,9},{9,10},{10,1... | collective-permute-start | bytes 786440 | tf_op jit(solution)/shard_map/ppermute | solution.py:19
  3.2 11.5 %collective-permute-start.2 = (f32[2,256,128]{2,1,0:T(8,128)S(1)}, f32[2,256,128]{2,1,0:T(8,128)S(1)}, u32[]{:S(2)}, u32[]{:S(2)}) collective-permute-start(f32[2,256,128]{2,1,0:T(8,128)S(1)} %get-tuple-element.13), channel_id=1, source_target_pairs={{1,0},{2,1},{3,2},{4,3},{5,4},{6,5},{7,6},{8,7},{9,8},{10,9},{11,1... | collective-permute-start | bytes 786440 | tf_op jit(solution)/shard_map/ppermute | solution.py:21
  7.8 7.0 %collective-permute-start = (f32[4,2,128]{2,1,0:T(2,128)S(1)}, f32[4,2,128]{2,1,0:T(2,128)S(1)}, u32[]{:S(2)}, u32[]{:S(2)}) collective-permute-start(f32[4,2,128]{2,1,0:T(2,128)S(1)} %get-tuple-element.20), channel_id=1, source_target_pairs={{16,0},{32,16},{48,32},{64,48},{80,64},{96,80},{112,96},{128,112},... | collective-permute-start | bytes 12296 | tf_op jit(solution)/shard_map/ppermute | solution.py:21
  12.4 3.1 %collective-permute-start.1 = (f32[4,2,128]{2,1,0:T(2,128)S(1)}, f32[4,2,128]{2,1,0:T(2,128)S(1)}, u32[]{:S(2)}, u32[]{:S(2)}) collective-permute-start(f32[4,2,128]{2,1,0:T(2,128)S(1)} %get-tuple-element.21), channel_id=1, source_target_pairs={{0,16},{16,32},{32,48},{48,64},{64,80},{80,96},{96,112},{112,128},... | collective-permute-start | bytes 12296 | tf_op jit(solution)/shard_map/ppermute | solution.py:19
  14.6 1.4 %copy-start.1 = (f32[3,4,256,128]{3,2,1,0:T(8,128)S(1)}, f32[3,4,256,128]{3,2,1,0:T(8,128)}, u32[]{:S(2)}) copy-start(f32[3,4,256,128]{3,2,1,0:T(8,128)} %param.4) | copy-start | bytes 4718596

commit v17 on v16

--- a/solution.py
+++ b/solution.py
@@ -12,7 +12,7 @@
     for axis, dim in sides:
         count = lax.axis_size(axis)
         ends = count if closed else count - 1
-        head = lax.slice_in_dim(cells, 0, width, axis=dim)
+        head = lax.slice_in_dim(lax.optimization_barrier(cells), 0, width, axis=dim)
         tail = lax.slice_in_dim(cells, cells.shape[dim] - width, cells.shape[dim], axis=dim)
         cells = jnp.concatenate(
             [

time: 47.2 us -> 48.8 us (1.034)
  local copies, waits for them, and re-layouts: 2.72 us -> 4.33 us
    slice x2 -> x4, local copies, waits for them, and re-layouts: 1.87 us -> 3.47 us  [the longest x2 1.79 us: padded_2(): lax.slice_in_dim(cells, cells.shape[dim] - width, cells.shape[dim], axis=...]
  transfers between devices with their start and end apart: 4 -> 4, of which waited for: 1 -> 1; matrix products, arithmetic and copies ran while one was open for 2% -> 6% of each run, Pallas kernels for 0% -> 0%
where the time goes in v17:
time: 48.8 us; the launch traced here: 48.4 us
  blocking collectives  22.6 us (46%)
  starting transfers between devices  12.5 us (26%)
  Pallas kernels  6.31 us (13%)
  local copies, waits for them, and re-layouts  4.33 us (9%)
  other arithmetic  1.92 us (4%)
  waiting for transfers between devices  0.7 us (1%)
    all_gather x1, blocking collectives, shards(): gathered = lax.all_gather(stacked, 'gx', axis=1, tiled=True)  22.6 us
    ppermute x2, starting transfers between devices, padded_2(): lax.ppermute(head, axis, [((i + 1) % count, i) for i in range(ends)])  8.49 us
    ppermute x2, starting transfers between devices, padded_2(): lax.ppermute(tail, axis, [(i, (i + 1) % count) for i in range(ends)])  4.01 us
    pallas_call x1, Pallas kernels, local_solve(): pl.pallas_call(functools.partial(thomas_kernel, chunks, devices), out_sha...  3.17 us
    pallas_call x1, Pallas kernels, finish(): pl.pallas_call(functools.partial(finish_kernel, chunks), out_shape=jax.Sh...  3.14 us
    add x1, other arithmetic, build_rhs(): field - transport + 0.05 * (curve_y + curve_z)  1.92 us
    slice x2, local copies, waits for them, and re-layouts, padded_2(): lax.slice_in_dim(cells, cells.shape[dim] - width, cells.shape[dim], axis=...  1.79 us
    slice x2, local copies, waits for them, and re-layouts, padded_2(): head = lax.slice_in_dim(lax.optimization_barrier(cells), 0, width, axis=dim)  1.69 us
  transfers between devices with their start and end apart: 4, of which 1 were waited for; matrix products, arithmetic and copies ran while one was open for 6% of the time, Pallas kernels for 0%

profile of v17, /device:TPU:1, one launch (start us, length us, event | category | flops | bytes accessed | tf_op | source)
XLA Modules:
  0.0 48.4 jit_solution(11965355419492073856)
XLA Ops:
  0.0 0.0 copy-start
  0.0 1.0 %slice.85 = f32[2,256,128]{2,1,0:T(8,128)S(1)} slice(f32[4,256,128]{2,1,0:T(8,128)} %param.3), slice={[2:4], [0:256], [0:128]} | slice | bytes 524288 | tf_op jit(solution)/shard_map/slice | solution.py:16
  1.0 2.1 %collective-permute-start.3 = (f32[2,256,128]{2,1,0:T(8,128)S(1)}, f32[2,256,128]{2,1,0:T(8,128)S(1)}, u32[]{:S(2)}, u32[]{:S(2)}) collective-permute-start(f32[2,256,128]{2,1,0:T(8,128)S(1)} %slice.85), channel_id=1, source_target_pairs={{0,1},{1,2},{2,3},{3,4},{4,5},{5,6},{6,7},{7,8},{8,9},{9,10},{10,1... | collective-permute-start | bytes 786440 | tf_op jit(solution)/shard_map/ppermute | solution.py:19
  3.2 1.0 %slice.101 = f32[2,256,128]{2,1,0:T(8,128)S(1)} slice(f32[4,256,128]{2,1,0:T(8,128)} %param.3), slice={[0:2], [0:256], [0:128]} | slice | bytes 524288 | tf_op jit(solution)/shard_map/slice | solution.py:15
  4.1 3.8 %collective-permute-start.2 = (f32[2,256,128]{2,1,0:T(8,128)S(1)}, f32[2,256,128]{2,1,0:T(8,128)S(1)}, u32[]{:S(2)}, u32[]{:S(2)}) collective-permute-start(f32[2,256,128]{2,1,0:T(8,128)S(1)} %slice.101), channel_id=1, source_target_pairs={{1,0},{2,1},{3,2},{4,3},{5,4},{6,5},{7,6},{8,7},{9,8},{10,9},{11,1... | collective-permute-start | bytes 786440 | tf_op jit(solution)/shard_map/ppermute | solution.py:21
  7.9 0.7 %slice.96 = f32[4,2,128]{2,1,0:T(2,128)S(1)} slice(f32[4,256,128]{2,1,0:T(8,128)} %param.3), slice={[0:4], [0:2], [0:128]} | slice | bytes 8192 | tf_op jit(solution)/shard_map/slice | solution.py:15
  8.7 4.7 %collective-permute-start = (f32[4,2,128]{2,1,0:T(2,128)S(1)}, f32[4,2,128]{2,1,0:T(2,128)S(1)}, u32[]{:S(2)}, u32[]{:S(2)}) collective-permute-start(f32[4,2,128]{2,1,0:T(2,128)S(1)} %slice.96), channel_id=1, source_target_pairs={{16,0},{32,16},{48,32},{64,48},{80,64},{96,80},{112,96},{128,112},... | collective-permute-start | bytes 12296 | tf_op jit(solution)/shard_map/ppermute | solution.py:21
  13.3 0.7 %slice.78 = f32[4,2,128]{2,1,0:T(2,128)S(1)} slice(f32[4,256,128]{2,1,0:T(8,128)} %param.3), slice={[0:4], [254:256], [0:128]} | slice | bytes 8192 | tf_op jit(solution)/shard_map/slice | solution.py:16
  14.1 1.9 %collective-permute-start.1 = (f32[4,2,128]{2,1,0:T(2,128)S(1)}, f32[4,2,128]{2,1,0:T(2,128)S(1)}, u32[]{:S(2)}, u32[]{:S(2)}) collective-permute-start(f32[4,2,128]{2,1,0:T(2,128)S(1)} %slice.78), channel_id=1, source_target_pairs={{0,16},{16,32},{32,48},{48,64},{64,80},{80,96},{96,112},{112,128},... | collective-permute-start | bytes 12296 | tf_op jit(solution)/shard_map/ppermute | solution.py:19
  16.0 0.0 copy-done
  16.0 0.2 fusion.14
  16.2 0.0 copy-start.1
  16.2 0.0 collective-permute-done.3
  16.3 0.1 constant_dynamic-update-slice_fusion.3
  16.4 0.0 collective-permute-done.2
  16.4 0.0 collective-permute-done
  16.4 0.7 %collective-permute-done.1 = f32[4,2,128]{2,1,0:T(2,128)S(1)} collective-permute-done((f32[4,2,128]{2,1,0:T(2,128)S(1)}, f32[4,2,128]{2,1,0:T(2,128)S(1)}, u32[]{:S(2)}, u32[]{:S(2)}) %collective-permute-start.1) | collective-permute-done | bytes 4128 | tf_op jit(solution)/shard_map/ppermute | solution.py:19
  17.1 0.5 %copy-done.1 = f32[3,4,256,128]{3,2,1,0:T(8,128)S(1)} copy-done((f32[3,4,256,128]{3,2,1,0:T(8,128)S(1)}, f32[3,4,256,128]{3,2,1,0:T(8,128)}, u32[]{:S(2)}) %copy-start.1) | copy-done | bytes 1572888
  17.6 1.9 %fusion.10 = f32[4,256,128]{2,1,0:T(8,128)} fusion(f32[4,256,128]{2,1,0:T(8,128)S(1)} %copy-done, f32[4,2,128]{2,1,0:T(2,128)S(1)} %collective-permute-done.1, f32[4,258,128]{2,1,0:T(8,128)S(1)} %constant_dynamic-update-slice_fusion, f32[4,256,2]{2,1,0:T(8,128)S(1)} %get-tuple-element.17, f32[4,256,2]{2,1,0:T(8,128)S(1)} %get-tuple-element.16, ...), kind=kLoop, calls=%fused_computation.16 | loop fusion | flops 6029312 | bytes 5787648 | tf_op jit(solution)/shard_map/add | solution.py:46
  19.6 3.2 %shard_map.37 = (f32[128,8,128]{2,1,0:T(8,128)}, f32[128,8,128]{2,1,0:T(8,128)}, f32[128,8,128]{2,1,0:T(8,128)}, f32[64,128]{1,0:T(8,128)}) custom-call(s32[1]{0:T(128)} %bitcast.place_ref, f32[1024,128]{1,0:T(8,128)} %bitcast.21, f32[1024,128]{1,0:T(8,128)} %bitcast.19), custom_call_target="tpu_custom_call" | custom-call | tf_op jit(solution)/shard_map/pallas_call | solution.py:226
  22.7 22.6 %all_gather.3 = f32[4,256,128]{2,1,0:T(8,128)} all-gather(f32[4,16,128]{2,1,0:T(8,128)} %bitcast.25), channel_id=1, replica_groups=mesh['gx'=16,'gy'=16] {'gx'}, dimensions={1}, use_global_device_ids=true | all-gather | bytes 557056 | tf_op jit(solution)/shard_map/all_gather | solution.py:332
  45.3 3.1 %shard_map.38 = f32[1024,128]{1,0:T(8,128)} custom-call(s32[1]{0:T(128)} %bitcast.place_ref, f32[1024,128]{1,0:T(8,128)} %bitcast.20, f32[1024,128]{1,0:T(8,128)} %bitcast.22, f32[1024,128]{1,0:T(8,128)} %bitcast.23, f32[1024,128]{1,0:T(8,128)} %bitcast.24), custom_call_target="tpu_custom_call" | custom-call | tf_op jit(solution)/shard_map/pallas_call | solution.py:307
  (3 shorter events, 0.0 us)
Async XLA Ops:
  0.0 16.0 %copy-start = (f32[4,256,128]{2,1,0:T(8,128)S(1)}, f32[4,256,128]{2,1,0:T(8,128)}, u32[]{:S(2)}) copy-start(f32[4,256,128]{2,1,0:T(8,128)} %param.3) | copy-start | bytes 1572868
  1.0 15.2 %collective-permute-start.3 = (f32[2,256,128]{2,1,0:T(8,128)S(1)}, f32[2,256,128]{2,1,0:T(8,128)S(1)}, u32[]{:S(2)}, u32[]{:S(2)}) collective-permute-start(f32[2,256,128]{2,1,0:T(8,128)S(1)} %slice.85), channel_id=1, source_target_pairs={{0,1},{1,2},{2,3},{3,4},{4,5},{5,6},{6,7},{7,8},{8,9},{9,10},{10,1... | collective-permute-start | bytes 786440 | tf_op jit(solution)/shard_map/ppermute | solution.py:19
  4.1 12.3 %collective-permute-start.2 = (f32[2,256,128]{2,1,0:T(8,128)S(1)}, f32[2,256,128]{2,1,0:T(8,128)S(1)}, u32[]{:S(2)}, u32[]{:S(2)}) collective-permute-start(f32[2,256,128]{2,1,0:T(8,128)S(1)} %slice.101), channel_id=1, source_target_pairs={{1,0},{2,1},{3,2},{4,3},{5,4},{6,5},{7,6},{8,7},{9,8},{10,9},{11,1... | collective-permute-start | bytes 786440 | tf_op jit(solution)/shard_map/ppermute | solution.py:21
  8.7 7.8 %collective-permute-start = (f32[4,2,128]{2,1,0:T(2,128)S(1)}, f32[4,2,128]{2,1,0:T(2,128)S(1)}, u32[]{:S(2)}, u32[]{:S(2)}) collective-permute-start(f32[4,2,128]{2,1,0:T(2,128)S(1)} %slice.96), channel_id=1, source_target_pairs={{16,0},{32,16},{48,32},{64,48},{80,64},{96,80},{112,96},{128,112},... | collective-permute-start | bytes 12296 | tf_op jit(solution)/shard_map/ppermute | solution.py:21
  14.1 3.0 %collective-permute-start.1 = (f32[4,2,128]{2,1,0:T(2,128)S(1)}, f32[4,2,128]{2,1,0:T(2,128)S(1)}, u32[]{:S(2)}, u32[]{:S(2)}) collective-permute-start(f32[4,2,128]{2,1,0:T(2,128)S(1)} %slice.78), channel_id=1, source_target_pairs={{0,16},{16,32},{32,48},{48,64},{64,80},{80,96},{96,112},{112,128},... | collective-permute-start | bytes 12296 | tf_op jit(solution)/shard_map/ppermute | solution.py:19
  16.2 1.4 %copy-start.1 = (f32[3,4,256,128]{3,2,1,0:T(8,128)S(1)}, f32[3,4,256,128]{3,2,1,0:T(8,128)}, u32[]{:S(2)}) copy-start(f32[3,4,256,128]{3,2,1,0:T(8,128)} %param.4) | copy-start | bytes 4718596
